TPU v7x, 512 devices: a whole 4x8x8 slice. The times are simulated.
512 devices in a mesh: tile: 16 (over x_hi, z), eval: 32 (over x_lo, y, core).
Axes of the slice: x: 4 (x_hi: 2, x_lo: 2; x = x_hi * 2 + x_lo), y: 8, z: 8, core: 2. Of those that a mesh axis runs over, the one named last changes fastest.
Arguments:
- target_geom: float32 [6, 128, 4096], P(None, 'tile', 'eval'), may hold values from -1 to 1
- eta: float32 [128, 4096], P('tile', 'eval'), may hold values from -3 to 3
- phi: float32 [128, 4096], P('tile', 'eval'), may hold values from -3 to 3
- sources: float32 [16, 4, 4, 1024], P('tile', None, None, 'eval')
- group_len: int32 [4, 32], replicated, may hold values from 1 to 32, 640 in all within a row
- owner: int32 [16], replicated, may hold values from 0 to 15, each once
Outputs:
- eta_next: float32 [128, 4096], P('tile', 'eval')
- phi_next: float32 [128, 4096], P('tile', 'eval')
- normal_velocity: float32 [128, 4096], P('tile', 'eval')
Inputs may be any that keep to these rules, and one draw needn't show every extreme that they name: owner holds distinct tile rows; round r's group is held by tile row owner[r]. `group_len`: each round has some column with all 32 slots live.
All inputs are finite; a program needn't handle non-finite values.
Results may differ from a plain program's by a relative error of at most 0.0001.
Values sent between devices are 32-bit elements; how exact they have to be, the bound alone decides.
No kernel may reach another device: no remote copies, remote signals or barrier semaphores. Data moves between devices by JAX's collectives and lax.ppermute only.
A program may use at most 64 MiB of HBM per device.

v0:
```python
import jax
import jax.numpy as jnp
from jax import lax
from jax.sharding import PartitionSpec as P

ROUNDS = 4


EPS2 = 0.05


def copy_for_each(x, axis):
    peers = lax.axis_size(axis)
    return lax.all_to_all(jnp.broadcast_to(x[None], (peers, *x.shape)), axis, 0, 0, tiled=True)


def joined_along(pieces, dim):
    lengths = list(pieces.shape[1:])
    lengths[dim] *= pieces.shape[0]
    return jnp.moveaxis(pieces, 0, dim).reshape(lengths)


def gathered_copies(x, axis, dim):
    pieces = copy_for_each(x, axis)
    return joined_along(pieces, dim)


def with_halo(x, sides, width):
    for axis, dim in sides:
        peers, length = (lax.axis_size(axis), x.shape[dim])
        up = [(i, (i + 1) % peers) for i in range(peers - 1)]
        down = [(j, i) for i, j in up]
        last = lax.slice_in_dim(x, length - width, length, axis=dim)
        first = lax.slice_in_dim(x, 0, width, axis=dim)
        before = lax.ppermute(last, axis, up)
        after = lax.ppermute(first, axis, down)
        x = jnp.concatenate([before, x, after], axis=dim)
    return x


def kernel_sum(targ, src):
    dx = targ[0][None] - src[0][:, None, None]
    dy = targ[1][None] - src[1][:, None, None]
    dz = targ[2][None] - src[2][:, None, None]
    dist2 = dx * dx + dy * dy + dz * dz + EPS2
    numer = targ[3][None] * dx + targ[4][None] * dy + targ[5][None] * dz
    return jnp.sum(src[3][:, None, None] * numer / (dist2 * jnp.sqrt(dist2)), axis=0)


def all_rounds(targ, stacked):
    total = kernel_sum(targ, stacked[0])
    for step in range(1, stacked.shape[0]):
        total = total + kernel_sum(targ, stacked[step])
    return total


def tendency(ext):
    centre = ext[:, 1:-1, 1:-1]
    grad_x = (ext[:, 2:, 1:-1] - ext[:, :-2, 1:-1]) * 0.5
    grad_y = (ext[:, 1:-1, 2:] - ext[:, 1:-1, :-2]) * 0.5
    slope = 1.0 + grad_x[0] * grad_x[0] + grad_y[0] * grad_y[0]
    velocity = centre[2]
    eta_rate = velocity * slope - (grad_x[1] * grad_x[0] + grad_y[1] * grad_y[0])
    phi_rate = (
        -centre[0]
        - 0.5 * (grad_x[1] * grad_x[1] + grad_y[1] * grad_y[1])
        + 0.5 * velocity * velocity * slope
    )
    return jnp.stack([eta_rate, phi_rate])


def smooth(rim):
    centre = rim[:, 1:-1, 1:-1]
    return (
        4.0 * centre + rim[:, 2:, 1:-1] + rim[:, :-2, 1:-1] + rim[:, 1:-1, 2:] + rim[:, 1:-1, :-2]
    ) / 8.0


def mask_strength(block, group_len, step, column):
    width = block.shape[1]
    length = lax.dynamic_index_in_dim(group_len[step], column, 0, keepdims=False)
    live = (jnp.arange(width, dtype=jnp.int32) < length).astype(jnp.float32)
    return jnp.concatenate([block[:3], block[3:] * live[None]], axis=0)


def body(target_geom, eta, phi, sources, group_len, owner):
    column = lax.axis_index("eval")
    blocks = []
    every_row = gathered_copies(sources, "tile", 0)
    for step in range(ROUNDS):
        chosen = lax.dynamic_index_in_dim(every_row[:, step], owner[step], 0, keepdims=False)
        blocks.append(mask_strength(chosen, group_len, step, column))
    stacked = jnp.stack(blocks)
    velocity = all_rounds(target_geom, gathered_copies(stacked, "eval", 2))
    fields = jnp.stack([eta, phi, velocity])
    rows_here, cols_here = eta.shape
    ext = with_halo(fields, (("tile", 1), ("eval", 2)), 2)
    rates = tendency(ext)
    row_ids = lax.axis_index("tile") * rows_here + jnp.arange(rows_here + 2, dtype=jnp.int32) - 1
    col_ids = column * cols_here + jnp.arange(cols_here + 2, dtype=jnp.int32) - 1
    row_ok = (row_ids >= 0) & (row_ids < rows_here * lax.axis_size("tile"))
    col_ok = (col_ids >= 0) & (col_ids < cols_here * lax.axis_size("eval"))
    inside = (row_ok[:, None] & col_ok[None, :]).astype(jnp.float32)
    smoothed = smooth(rates * inside[None])
    return (eta + 0.5 * smoothed[0], phi + 0.5 * smoothed[1], velocity)


def solution(mesh):
    return jax.shard_map(
        body,
        mesh=mesh,
        in_specs=(
            P(None, "tile", "eval"),
            P("tile", "eval"),
            P("tile", "eval"),
            P("tile", None, None, "eval"),
            P(),
            P(),
        ),
        out_specs=(P("tile", "eval"), P("tile", "eval"), P("tile", "eval")),
        check_vma=False,
    )
```

profile of v0, /device:TPU:61, one launch (start us, length us, event | category | flops | bytes accessed | tf_op | source)
XLA Modules:
  0.0 90.5 jit_solution(6693430371267795684)
XLA Ops:
  0.7 0.7 broadcast_in_dim.7
  1.4 0.7 reshape.329
  2.1 12.7 %all-to-all-start = ((f32[16,1,512]{2,1,0:T(1,128)}), f32[16,1,512]{2,1,0:T(1,128)S(1)}, u32[]{:S(2)}, u32[]{:S(2)}) async-start(f32[16,1,512]{2,1,0:T(1,128)} %reshape.329), calls=%async_computation | async-start | bytes 65536 | tf_op jit(solution)/shard_map/all_to_all | solution.py:14
  14.9 0.6 fusion.46
  23.2 0.7 constant_dynamic-slice_fusion.4
  23.9 0.6 constant_dynamic-slice_fusion
  24.5 0.5 broadcast.217
  25.0 0.7 reduce.64
  25.7 0.1 reshape.330
  25.9 0.6 compare_select_fusion.3
  26.6 0.6 compare_select_fusion.2
  27.2 0.7 compare_select_fusion.1
  27.9 0.7 compare_select_fusion
  28.7 0.8 reshape.331
  29.5 8.5 %all-to-all-start.1 = ((f32[32,1,512]{2,1,0:T(1,128)}), f32[32,1,512]{2,1,0:T(1,128)S(1)}, u32[]{:S(2)}, u32[]{:S(2)}) async-start(f32[32,1,512]{2,1,0:T(1,128)} %reshape.331), calls=%async_computation.1 | async-start | bytes 131072 | tf_op jit(solution)/shard_map/all_to_all | solution.py:14
  38.1 6.1 %all-to-all-done.1 = f32[32,1,512]{2,1,0:T(1,128)S(1)} async-done(((f32[32,1,512]{2,1,0:T(1,128)}), f32[32,1,512]{2,1,0:T(1,128)S(1)}, u32[]{:S(2)}, u32[]{:S(2)}) %all-to-all-start.1) | async-done | bytes 65568 | tf_op jit(solution)/shard_map/all_to_all | solution.py:14
  44.2 0.8 reduce.65
  45.0 0.2 reshape.332
  45.2 0.7 slice_reduce_fusion.11
  45.9 0.1 mul.280
  46.0 0.1 sub.191
  46.1 0.1 sub.196
  46.2 0.1 sub.201
  46.2 0.1 mul.296
  46.3 0.1 mul.306
  46.4 0.1 mul.316
  46.4 0.1 sub.204
  46.5 0.1 sub.207
  46.6 0.1 sub.210
  46.7 0.1 sub.213
  46.7 0.1 sub.216
  46.8 0.1 sub.219
  47.1 5.4 %fusion.7 = f32[8,128]{1,0:T(8,128)S(1)} fusion(f32[1024]{0:T(1024)S(1)} %sub.201, f32[8,128]{1,0:T(8,128)S(1)} %get-tuple-element.34, f32[8,128]{1,0:T(8,128)S(1)} %get-tuple-element.35, f32[1024]{0:T(1024)S(1)} %sub.196, f32[8,128]{1,0:T(8,128)S(1)} %get-tuple-element.31, f32[8,128]{1,0:T(8,128)S(1)} %get-tuple-element.32, f32[1024]{0:T(1024)S(1)} %sub.191, ...), kind=kLoop, calls=%fused_computation.35 | loop fusion | flops 18873344 | bytes 45056 | tf_op jit(solution)/shard_map/reduce_sum | solution.py:47
  52.5 13.7 %fusion.15 = (f32[8,128]{1,0:T(8,128)S(1)}, f32[8,128]{1,0:T(8,128)S(1)}, f32[8,128]{1,0:T(8,128)S(1)}) fusion(f32[1024]{0:T(1024)S(1)} %sub.210, f32[1024]{0:T(1024)S(1)} %sub.207, f32[1024]{0:T(1024)S(1)} %sub.204, f32[1024]{0:T(1024)S(1)} %mul.296, f32[8,128]{1,0:T(8,128)S(1)} %get-tuple-element.34, f32[8,128]{1,0:T(8,128)S(1)} %get-tuple-element.35, ...), kind=kLoop, calls=%fused_computation.43 | loop fusion | flops 56620032 | bytes 86016 | tf_op jit(solution)/shard_map/reduce_sum | solution.py:47
  66.3 3.1 %collective-permute-start = (f32[3,2,128]{2,1,0:T(2,128)S(1)}, f32[3,2,128]{2,1,0:T(2,128)S(1)}, u32[]{:S(2)}, u32[]{:S(2)}) collective-permute-start(f32[3,2,128]{2,1,0:T(2,128)S(1)} %get-tuple-element.36), channel_id=1, source_target_pairs={{0,32},{32,64},{64,96},{96,128},{128,160},{160,192},{192,224},{224... | collective-permute-start | bytes 9224 | tf_op jit(solution)/shard_map/ppermute | solution.py:35
  69.4 5.8 %collective-permute-start.1 = (f32[3,2,128]{2,1,0:T(2,128)S(1)}, f32[3,2,128]{2,1,0:T(2,128)S(1)}, u32[]{:S(2)}, u32[]{:S(2)}) collective-permute-start(f32[3,2,128]{2,1,0:T(2,128)S(1)} %get-tuple-element.37), channel_id=1, source_target_pairs={{32,0},{64,32},{96,64},{128,96},{160,128},{192,160},{224,192},{256... | collective-permute-start | bytes 9224 | tf_op jit(solution)/shard_map/ppermute | solution.py:36
  75.2 0.7 collective-permute-done.1
  75.9 0.1 fusion.44
  76.0 6.1 %collective-permute-start.2 = (f32[3,12,2]{2,1,0:T(8,128)S(1)}, f32[3,12,2]{2,1,0:T(8,128)S(1)}, u32[]{:S(2)}, u32[]{:S(2)}) collective-permute-start(f32[3,12,2]{2,1,0:T(8,128)S(1)} %get-tuple-element.28), channel_id=1, source_target_pairs={{0,1},{1,2},{2,3},{3,4},{4,5},{5,6},{6,7},{7,8},{8,9},{9,10},{10,1... | collective-permute-start | bytes 872 | tf_op jit(solution)/shard_map/ppermute | solution.py:35
  82.1 1.9 %collective-permute-start.3 = (f32[3,12,2]{2,1,0:T(8,128)S(1)}, f32[3,12,2]{2,1,0:T(8,128)S(1)}, u32[]{:S(2)}, u32[]{:S(2)}) collective-permute-start(f32[3,12,2]{2,1,0:T(8,128)S(1)} %get-tuple-element.29), channel_id=1, source_target_pairs={{1,0},{2,1},{3,2},{4,3},{5,4},{6,5},{7,6},{8,7},{9,8},{10,9},{11,1... | collective-permute-start | bytes 872 | tf_op jit(solution)/shard_map/ppermute | solution.py:36
  84.0 0.1 and_convert_fusion
  84.1 5.2 %collective-permute-done.3 = f32[3,12,2]{2,1,0:T(8,128)S(1)} collective-permute-done((f32[3,12,2]{2,1,0:T(8,128)S(1)}, f32[3,12,2]{2,1,0:T(8,128)S(1)}, u32[]{:S(2)}, u32[]{:S(2)}) %collective-permute-start.3) | collective-permute-done | bytes 320 | tf_op jit(solution)/shard_map/ppermute | solution.py:36
  89.3 0.1 pad_maximum_fusion.10
  89.4 0.1 fusion.34
  89.5 0.1 fusion.33
  89.7 0.1 add_subtract_fusion
  89.8 0.1 fusion.38
  89.8 0.6 fusion.40
  (39 shorter events, 0.5 us)
Async XLA Ops:
  0.6 14.2 %copy-start.5 = (s32[4,32]{1,0:T(4,128)S(1)}, s32[4,32]{1,0:T(4,128)}, u32[]{:S(2)}) copy-start(s32[4,32]{1,0:T(4,128)} %param.10) | copy-start | bytes 1540
  0.6 14.2 %copy-start.4 = (s32[16]{0:T(128)S(1)}, s32[16]{0:T(128)}, u32[]{:S(2)}) copy-start(s32[16]{0:T(128)} %param.11) | copy-start | bytes 196
  2.1 22.4 %all-to-all-start = ((f32[16,1,512]{2,1,0:T(1,128)}), f32[16,1,512]{2,1,0:T(1,128)S(1)}, u32[]{:S(2)}, u32[]{:S(2)}) async-start(f32[16,1,512]{2,1,0:T(1,128)} %reshape.329), calls=%async_computation | async-start | bytes 65536 | tf_op jit(solution)/shard_map/all_to_all | solution.py:14
  28.7 9.3 %copy-start.3 = (f32[6,8,128]{2,1,0:T(8,128)S(1)}, f32[6,8,128]{2,1,0:T(8,128)}, u32[]{:S(2)}) copy-start(f32[6,8,128]{2,1,0:T(8,128)} %param.6) | copy-start | bytes 73732
  29.5 14.7 %all-to-all-start.1 = ((f32[32,1,512]{2,1,0:T(1,128)}), f32[32,1,512]{2,1,0:T(1,128)S(1)}, u32[]{:S(2)}, u32[]{:S(2)}) async-start(f32[32,1,512]{2,1,0:T(1,128)} %reshape.331), calls=%async_computation.1 | async-start | bytes 131072 | tf_op jit(solution)/shard_map/all_to_all | solution.py:14
  52.5 13.7 %copy-start.1 = (f32[8,128]{1,0:T(8,128)S(1)}, f32[8,128]{1,0:T(8,128)}, u32[]{:S(2)}) copy-start(f32[8,128]{1,0:T(8,128)} %param.8) | copy-start | bytes 12292
  52.5 13.7 %copy-start.2 = (f32[8,128]{1,0:T(8,128)S(1)}, f32[8,128]{1,0:T(8,128)}, u32[]{:S(2)}) copy-start(f32[8,128]{1,0:T(8,128)} %param.7) | copy-start | bytes 12292
  66.2 23.4 %copy-start = (f32[8,128]{1,0:T(8,128)}, f32[8,128]{1,0:T(8,128)S(1)}, u32[]{:S(2)}) copy-start(f32[8,128]{1,0:T(8,128)S(1)} %add_add_fusion) | copy-start | bytes 12292
  66.3 8.9 %collective-permute-start = (f32[3,2,128]{2,1,0:T(2,128)S(1)}, f32[3,2,128]{2,1,0:T(2,128)S(1)}, u32[]{:S(2)}, u32[]{:S(2)}) collective-permute-start(f32[3,2,128]{2,1,0:T(2,128)S(1)} %get-tuple-element.36), channel_id=1, source_target_pairs={{0,32},{32,64},{64,96},{96,128},{128,160},{160,192},{192,224},{224... | collective-permute-start | bytes 9224 | tf_op jit(solution)/shard_map/ppermute | solution.py:35
  69.4 6.5 %collective-permute-start.1 = (f32[3,2,128]{2,1,0:T(2,128)S(1)}, f32[3,2,128]{2,1,0:T(2,128)S(1)}, u32[]{:S(2)}, u32[]{:S(2)}) collective-permute-start(f32[3,2,128]{2,1,0:T(2,128)S(1)} %get-tuple-element.37), channel_id=1, source_target_pairs={{32,0},{64,32},{96,64},{128,96},{160,128},{192,160},{224,192},{256... | collective-permute-start | bytes 9224 | tf_op jit(solution)/shard_map/ppermute | solution.py:36
  76.0 8.1 %collective-permute-start.2 = (f32[3,12,2]{2,1,0:T(8,128)S(1)}, f32[3,12,2]{2,1,0:T(8,128)S(1)}, u32[]{:S(2)}, u32[]{:S(2)}) collective-permute-start(f32[3,12,2]{2,1,0:T(8,128)S(1)} %get-tuple-element.28), channel_id=1, source_target_pairs={{0,1},{1,2},{2,3},{3,4},{4,5},{5,6},{6,7},{7,8},{8,9},{9,10},{10,1... | collective-permute-start | bytes 872 | tf_op jit(solution)/shard_map/ppermute | solution.py:35
  82.1 7.3 %collective-permute-start.3 = (f32[3,12,2]{2,1,0:T(8,128)S(1)}, f32[3,12,2]{2,1,0:T(8,128)S(1)}, u32[]{:S(2)}, u32[]{:S(2)}) collective-permute-start(f32[3,12,2]{2,1,0:T(8,128)S(1)} %get-tuple-element.29), channel_id=1, source_target_pairs={{1,0},{2,1},{3,2},{4,3},{5,4},{6,5},{7,6},{8,7},{9,8},{10,9},{11,1... | collective-permute-start | bytes 872 | tf_op jit(solution)/shard_map/ppermute | solution.py:36
where the time goes:
time: 91 us; the launch traced here: 90.5 us
  starting transfers between devices  38.2 us (42%)
  other arithmetic  24.4 us (27%)
  waiting for transfers between devices  12.1 us (13%)
  between operations  8.79 us (10%)
  local copies, waits for them, and re-layouts  7.03 us (8%)
    all_to_all x2, starting transfers between devices, copy_for_each(): lax.all_to_all(jnp.broadcast_to(x[None], (peers, *x.shape)), axis, 0, 0,...  21.2 us
    reduce_sum x2, other arithmetic, kernel_sum(): jnp.sum(src[3][:, None, None] * numer / (dist2 * jnp.sqrt(dist2)), axis=0)  19.1 us
    ppermute x2, starting transfers between devices, with_halo(): before = lax.ppermute(last, axis, up)  9.2 us
    ppermute x2, starting transfers between devices, with_halo(): after = lax.ppermute(first, axis, down)  7.73 us
    all_to_all x2, waiting for transfers between devices, copy_for_each(): lax.all_to_all(jnp.broadcast_to(x[None], (peers, *x.shape)), axis, 0, 0,...  6.14 us
    ppermute x2, waiting for transfers between devices, with_halo(): after = lax.ppermute(first, axis, down)  5.94 us
    mul x4, other arithmetic, mask_strength(): return jnp.concatenate([block[:3], block[3:] * live[None]], axis=0)  2.57 us
    unnamed x16, local copies, waits for them, and re-layouts  1.89 us
  transfers between devices with their start and end apart: 6, of which 3 were waited for; matrix products, arithmetic and copies ran while one was open for 2% of the time, Pallas kernels for 0%

commit v1 on v0

v1 whole, which is shorter than its diff:
```python
import jax
import jax.numpy as jnp
from jax import lax
from jax.sharding import PartitionSpec as P

ROUNDS = 4


EPS2 = 0.05


def shifted(x, axis, dim, width):
    peers, length = (lax.axis_size(axis), x.shape[dim])
    up = [(i, i + 1) for i in range(peers - 1)]
    down = [(j, i) for i, j in up]
    last = lax.slice_in_dim(x, length - width, length, axis=dim)
    first = lax.slice_in_dim(x, 0, width, axis=dim)
    return lax.ppermute(last, axis, up), lax.ppermute(first, axis, down)


def with_halo(x, sides, width):
    for axis, dim in sides:
        before, after = shifted(x, axis, dim, width)
        x = jnp.concatenate([before, x, after], axis=dim)
    return x


def kernel_sum(targ, src):
    dx = targ[0][None] - src[0][:, None, None]
    dy = targ[1][None] - src[1][:, None, None]
    dz = targ[2][None] - src[2][:, None, None]
    dist2 = dx * dx + dy * dy + dz * dz + EPS2
    numer = targ[3][None] * dx + targ[4][None] * dy + targ[5][None] * dz
    return jnp.sum(src[3][:, None, None] * numer / (dist2 * jnp.sqrt(dist2)), axis=0)


def gather_sources(sources, group_len, owner):
    row = lax.axis_index("tile")
    column = lax.axis_index("eval")
    width = sources.shape[-1]
    live = (jnp.arange(width, dtype=jnp.int32)[None, :] < group_len[:ROUNDS, column][:, None])
    mine = (owner[:ROUNDS] == row)
    local = sources[0]
    scale = jnp.concatenate(
        [jnp.broadcast_to(mine[:, None, None], (ROUNDS, 3, width)),
         (mine[:, None] & live)[:, None, :]], axis=1)
    picked = jnp.where(scale, local, 0.0)
    picked = lax.psum(picked, "tile")
    return lax.all_gather(picked, "eval", axis=2, tiled=True)


def tendency(ext, vel):
    centre = ext[:, 1:-1, 1:-1]
    grad_x = (ext[:, 2:, 1:-1] - ext[:, :-2, 1:-1]) * 0.5
    grad_y = (ext[:, 1:-1, 2:] - ext[:, 1:-1, :-2]) * 0.5
    slope = 1.0 + grad_x[0] * grad_x[0] + grad_y[0] * grad_y[0]
    eta_rate = vel * slope - (grad_x[1] * grad_x[0] + grad_y[1] * grad_y[0])
    phi_rate = (
        -centre[0]
        - 0.5 * (grad_x[1] * grad_x[1] + grad_y[1] * grad_y[1])
        + 0.5 * vel * vel * slope
    )
    return jnp.stack([eta_rate, phi_rate])


def smooth(rim):
    centre = rim[:, 1:-1, 1:-1]
    return (
        4.0 * centre + rim[:, 2:, 1:-1] + rim[:, :-2, 1:-1] + rim[:, 1:-1, 2:] + rim[:, 1:-1, :-2]
    ) / 8.0


def body(target_geom, eta, phi, sources, group_len, owner):
    rows_here, cols_here = eta.shape
    ext = with_halo(jnp.stack([eta, phi]), (("tile", 1), ("eval", 2)), 2)
    stacked = gather_sources(sources, group_len, owner)
    velocity = kernel_sum(target_geom, stacked[0])
    for step in range(1, ROUNDS):
        velocity = velocity + kernel_sum(target_geom, stacked[step])
    up, down = shifted(velocity, "tile", 0, 1)
    left, right = shifted(velocity, "eval", 1, 1)
    vel_rows = jnp.concatenate([up, velocity, down], axis=0)
    side = jnp.zeros((1, 1), jnp.float32)
    vel_left = jnp.concatenate([side, left, side], axis=0)
    vel_right = jnp.concatenate([side, right, side], axis=0)
    vel = jnp.concatenate([vel_left, vel_rows, vel_right], axis=1)
    rates = tendency(ext, vel)
    column = lax.axis_index("eval")
    row_ids = lax.axis_index("tile") * rows_here + jnp.arange(rows_here + 2, dtype=jnp.int32) - 1
    col_ids = column * cols_here + jnp.arange(cols_here + 2, dtype=jnp.int32) - 1
    row_ok = (row_ids >= 0) & (row_ids < rows_here * lax.axis_size("tile"))
    col_ok = (col_ids >= 0) & (col_ids < cols_here * lax.axis_size("eval"))
    inside = (row_ok[:, None] & col_ok[None, :]).astype(jnp.float32)
    smoothed = smooth(rates * inside[None])
    return (eta + 0.5 * smoothed[0], phi + 0.5 * smoothed[1], velocity)


def solution(mesh):
    return jax.shard_map(
        body,
        mesh=mesh,
        in_specs=(
            P(None, "tile", "eval"),
            P("tile", "eval"),
            P("tile", "eval"),
            P("tile", None, None, "eval"),
            P(),
            P(),
        ),
        out_specs=(P("tile", "eval"), P("tile", "eval"), P("tile", "eval")),
        check_vma=False,
    )
```

time: 91 us -> 245 us (2.69)
  blocking collectives: 0 us -> 117 us
  local copies, waits for them, and re-layouts: 7.03 us -> 64.4 us
  between operations: 8.79 us -> 0.9 us
  waiting for transfers between devices: 12.1 us -> 5.4 us
  other arithmetic: 24.4 us -> 21.1 us
  starting transfers between devices: 38.2 us -> 35.6 us
    psum x0 -> x1, blocking collectives: none -> 66.6 us  [gather_sources(): picked = lax.psum(picked, 'tile')]
    slice x1, local copies, waits for them, and re-layouts: 0.74 us -> 62 us  [kernel_sum(): src[3][:, None, None] * numer / (dist2 * jnp.sqrt(dist2))]
    all_gather x0 -> x1, blocking collectives: none -> 50.2 us  [gather_sources(): return lax.all_gather(picked, 'eval', axis=2, tiled=True)]
    all_to_all x2 -> x0, starting transfers between devices: 21.2 us -> none  [copy_for_each(): lax.all_to_all(jnp.broadcast_to(x[None], (peers, *x.shape)), axis, 0, 0,...]
    ppermute x4 -> x8, starting transfers between devices: 16.9 us -> 35.6 us  [shifted(): return (lax.ppermute(last, axis, up), lax.ppermute(first, axis, down))]
    all_to_all x2 -> x0, waiting for transfers between devices: 6.14 us -> none  [copy_for_each(): lax.all_to_all(jnp.broadcast_to(x[None], (peers, *x.shape)), axis, 0, 0,...]
    mul x5 -> x0, other arithmetic: 2.67 us -> none  [the longest x4 2.57 us: mask_strength(): return jnp.concatenate([block[:3], block[3:] * live[None]], axis=0)]
    ppermute x4 -> x8, waiting for transfers between devices: 5.95 us -> 5.4 us  [shifted(): return (lax.ppermute(last, axis, up), lax.ppermute(first, axis, down))]
  transfers between devices with their start and end apart: 6 -> 8, of which waited for: 3 -> 2; matrix products, arithmetic and copies ran while one was open for 2% -> 0% of each run, Pallas kernels for 0% -> 0%
where the time goes in v1:
time: 245 us; the launch traced here: 244 us
  blocking collectives  117 us (48%)
  local copies, waits for them, and re-layouts  64.4 us (26%)
  starting transfers between devices  35.6 us (15%)
  other arithmetic  21.1 us (9%)
  waiting for transfers between devices  5.4 us (2%)
    psum x1, blocking collectives, gather_sources(): picked = lax.psum(picked, 'tile')  66.6 us
    slice x1, local copies, waits for them, and re-layouts, kernel_sum(): src[3][:, None, None] * numer / (dist2 * jnp.sqrt(dist2))  62 us
    all_gather x1, blocking collectives, gather_sources(): return lax.all_gather(picked, 'eval', axis=2, tiled=True)  50.2 us
    ppermute x8, starting transfers between devices, shifted(): return (lax.ppermute(last, axis, up), lax.ppermute(first, axis, down))  35.6 us
    reduce_sum x2, other arithmetic, kernel_sum(): jnp.sum(src[3][:, None, None] * numer / (dist2 * jnp.sqrt(dist2)), axis=0)  19.1 us
    ppermute x8, waiting for transfers between devices, shifted(): return (lax.ppermute(last, axis, up), lax.ppermute(first, axis, down))  5.4 us
  transfers between devices with their start and end apart: 8, of which 2 were waited for; matrix products, arithmetic and copies ran while one was open for 0% of the time, Pallas kernels for 0%

profile of v1, /device:TPU:61, one launch (start us, length us, event | category | flops | bytes accessed | tf_op | source)
XLA Modules:
  0.0 244.2 jit_solution(5311817938171627228)
XLA Ops:
  0.6 0.0 copy-start
  0.7 0.7 copy-done
  1.3 0.2 dynamic-slice_reduce_fusion
  1.5 0.7 slice_compare_fusion
  2.2 0.1 compare_and_fusion
  2.2 0.1 broadcast_in_dim.5
  2.3 0.1 copy.28
  2.5 0.8 copy.27
  3.3 66.6 %psum.7 = f32[4,4,32]{1,0,2:T(4,128)S(1)} all-reduce(f32[4,4,32]{1,0,2:T(4,128)S(1)} %bitcast_select_fusion), channel_id=1, replica_groups=mesh['tile'=16,'eval'=32] {'tile'}, use_global_device_ids=true, to_apply=%region_0.1 | all-reduce | flops 512 | bytes 4096 | tf_op jit(solution)/shard_map/psum | solution.py:48
  69.9 50.2 %all_gather.3 = f32[4,4,1024]{1,0,2:T(4,128)S(1)} all-gather(f32[4,4,32]{1,0,2:T(4,128)S(1)} %psum.7), channel_id=1, replica_groups=mesh['tile'=16,'eval'=32] {'eval'}, dimensions={2}, use_global_device_ids=true | all-gather | bytes 67584 | tf_op jit(solution)/shard_map/all_gather | solution.py:49
  120.1 62.0 %slice_reduce_fusion.11 = (f32[1024]{0:T(1024)S(1)}, f32[1024]{0:T(1024)S(1)}, f32[1024]{0:T(1024)S(1)}, f32[1024]{0:T(1024)S(1)}, f32[1024]{0:T(1024)S(1)}, /*i...) fusion(f32[4,4,1024]{1,0,2:T(4,128)S(1)} %all_gather.3), kind=kLoop, calls=%fused_computation.71 | loop fusion | bytes 131072 | tf_op jit(solution)/shard_map/slice | solution.py:34
  182.1 0.0 copy-done.4
  182.2 5.4 %fusion.7 = f32[8,128]{1,0:T(8,128)S(1)} fusion(f32[1024]{0:T(1024)S(1)} %get-tuple-element.15, f32[8,128]{1,0:T(8,128)S(1)} %get-tuple-element.28, f32[8,128]{1,0:T(8,128)S(1)} %get-tuple-element.29, f32[1024]{0:T(1024)S(1)} %get-tuple-element.16, f32[8,128]{1,0:T(8,128)S(1)} %get-tuple-element.25, f32[8,128]{1,0:T(8,128)S(1)} %get-tuple-element.26, ...), kind=kLoop, calls=%fused_computation.35 | loop fusion | flops 18873344 | bytes 45056 | tf_op jit(solution)/shard_map/reduce_sum | solution.py:34
  187.6 0.0 copy-start.1
  187.6 0.0 copy-start.2
  187.6 13.7 %fusion.15 = (f32[8,128]{1,0:T(8,128)S(1)}, f32[8,128]{1,0:T(8,128)S(1)}, f32[8,128]{1,0:T(8,128)S(1)}) fusion(f32[1024]{0:T(1024)S(1)} %get-tuple-element.12, f32[1024]{0:T(1024)S(1)} %get-tuple-element.13, f32[1024]{0:T(1024)S(1)} %get-tuple-element.14, f32[1024]{0:T(1024)S(1)} %get-tuple-element.3, f32[8,128]{1,0:T(8,128)S(1)} %get-tuple-element.28, ...), kind=kLoop, calls=%fused_computation.43 | loop fusion | flops 56620032 | bytes 86016 | tf_op jit(solution)/shard_map/reduce_sum | solution.py:34
  201.3 0.0 copy-start.3
  201.3 1.9 collective-permute-start.1
  203.2 7.0 %collective-permute-start.2 = (f32[1,128]{1,0:T(1,128)S(1)}, f32[1,128]{1,0:T(1,128)S(1)}, u32[]{:S(2)}, u32[]{:S(2)}) collective-permute-start(f32[1,128]{1,0:T(1,128)S(1)} %get-tuple-element.39), channel_id=1, source_target_pairs={{32,0},{64,32},{96,64},{128,96},{160,128},{192,160},{224,192},{256... | collective-permute-start | bytes 1544 | tf_op jit(solution)/shard_map/ppermute | solution.py:18
  210.2 0.1 fusion.46
  210.3 7.1 %collective-permute-start = (f32[8,1]{1,0:T(8,128)S(1)}, f32[8,1]{1,0:T(8,128)S(1)}, u32[]{:S(2)}, u32[]{:S(2)}) collective-permute-start(f32[8,1]{1,0:T(8,128)S(1)} %get-tuple-element.36), channel_id=1, source_target_pairs={{0,1},{1,2},{2,3},{3,4},{4,5},{5,6},{6,7},{7,8},{8,9},{9,10},{10,1... | collective-permute-start | bytes 104 | tf_op jit(solution)/shard_map/ppermute | solution.py:18
  217.4 1.9 collective-permute-start.3
  219.3 0.0 copy-done.1
  219.4 1.9 collective-permute-start.4
  221.3 0.1 and_convert_fusion
  221.4 0.0 collective-permute-done
  221.4 7.0 %collective-permute-start.5 = (f32[2,2,128]{2,1,0:T(2,128)S(1)}, f32[2,2,128]{2,1,0:T(2,128)S(1)}, u32[]{:S(2)}, u32[]{:S(2)}) collective-permute-start(f32[2,2,128]{2,1,0:T(2,128)S(1)} %get-tuple-element.35), channel_id=1, source_target_pairs={{32,0},{64,32},{96,64},{128,96},{160,128},{192,160},{224,192},{256... | collective-permute-start | bytes 6152 | tf_op jit(solution)/shard_map/ppermute | solution.py:18
  228.4 0.1 copy.29
  228.5 0.1 fusion.43
  228.6 0.0 collective-permute-done.3
  228.6 0.1 copy.30
  228.6 0.1 fusion.44
  228.7 0.1 copy.31
  228.8 0.1 copy.32
  228.9 0.0 collective-permute-done.4
  228.9 0.2 collective-permute-done.5
  229.1 0.1 fusion.45
  229.2 6.9 %collective-permute-start.6 = (f32[2,12,2]{2,1,0:T(8,128)S(1)}, f32[2,12,2]{2,1,0:T(8,128)S(1)}, u32[]{:S(2)}, u32[]{:S(2)}) collective-permute-start(f32[2,12,2]{2,1,0:T(8,128)S(1)} %get-tuple-element.30), channel_id=1, source_target_pairs={{0,1},{1,2},{2,3},{3,4},{4,5},{5,6},{6,7},{7,8},{8,9},{9,10},{10,1... | collective-permute-start | bytes 584 | tf_op jit(solution)/shard_map/ppermute | solution.py:18
  236.1 1.9 collective-permute-start.7
  238.0 0.0 collective-permute-done.1
  238.0 0.0 collective-permute-done.2
  238.0 0.0 collective-permute-done.6
  238.1 5.2 %collective-permute-done.7 = f32[2,12,2]{2,1,0:T(8,128)S(1)} collective-permute-done((f32[2,12,2]{2,1,0:T(8,128)S(1)}, f32[2,12,2]{2,1,0:T(8,128)S(1)}, u32[]{:S(2)}, u32[]{:S(2)}) %collective-permute-start.7) | collective-permute-done | bytes 224 | tf_op jit(solution)/shard_map/ppermute | solution.py:18
  243.2 0.1 pad_maximum_fusion.8
  243.3 0.1 fusion.33
  243.4 0.1 add_subtract_fusion
  243.5 0.1 fusion.38
  243.6 0.6 fusion.40
  (14 shorter events, 0.1 us)
Async XLA Ops:
  0.6 0.7 copy-start
  120.1 62.0 %copy-start.4 = (f32[6,8,128]{2,1,0:T(8,128)S(1)}, f32[6,8,128]{2,1,0:T(8,128)}, u32[]{:S(2)}) copy-start(f32[6,8,128]{2,1,0:T(8,128)} %param.6) | copy-start | bytes 73732
  187.6 31.8 %copy-start.1 = (f32[8,128]{1,0:T(8,128)S(1)}, f32[8,128]{1,0:T(8,128)}, u32[]{:S(2)}) copy-start(f32[8,128]{1,0:T(8,128)} %param.8) | copy-start | bytes 12292
  187.6 31.8 %copy-start.2 = (f32[8,128]{1,0:T(8,128)S(1)}, f32[8,128]{1,0:T(8,128)}, u32[]{:S(2)}) copy-start(f32[8,128]{1,0:T(8,128)} %param.7) | copy-start | bytes 12292
  201.3 43.0 %copy-start.3 = (f32[8,128]{1,0:T(8,128)}, f32[8,128]{1,0:T(8,128)S(1)}, u32[]{:S(2)}) copy-start(f32[8,128]{1,0:T(8,128)S(1)} %add_add_fusion) | copy-start | bytes 12292
  201.3 36.7 %collective-permute-start.1 = (f32[1,128]{1,0:T(1,128)S(1)}, f32[1,128]{1,0:T(1,128)S(1)}, u32[]{:S(2)}, u32[]{:S(2)}) collective-permute-start(f32[1,128]{1,0:T(1,128)S(1)} %get-tuple-element.38), channel_id=1, source_target_pairs={{0,32},{32,64},{64,96},{96,128},{128,160},{160,192},{192,224},{224... | collective-permute-start | bytes 1544 | tf_op jit(solution)/shard_map/ppermute | solution.py:18
  203.2 34.8 %collective-permute-start.2 = (f32[1,128]{1,0:T(1,128)S(1)}, f32[1,128]{1,0:T(1,128)S(1)}, u32[]{:S(2)}, u32[]{:S(2)}) collective-permute-start(f32[1,128]{1,0:T(1,128)S(1)} %get-tuple-element.39), channel_id=1, source_target_pairs={{32,0},{64,32},{96,64},{128,96},{160,128},{192,160},{224,192},{256... | collective-permute-start | bytes 1544 | tf_op jit(solution)/shard_map/ppermute | solution.py:18
  210.3 11.1 %collective-permute-start = (f32[8,1]{1,0:T(8,128)S(1)}, f32[8,1]{1,0:T(8,128)S(1)}, u32[]{:S(2)}, u32[]{:S(2)}) collective-permute-start(f32[8,1]{1,0:T(8,128)S(1)} %get-tuple-element.36), channel_id=1, source_target_pairs={{0,1},{1,2},{2,3},{3,4},{4,5},{5,6},{6,7},{7,8},{8,9},{9,10},{10,1... | collective-permute-start | bytes 104 | tf_op jit(solution)/shard_map/ppermute | solution.py:18
  217.4 11.1 %collective-permute-start.3 = (f32[8,1]{1,0:T(8,128)S(1)}, f32[8,1]{1,0:T(8,128)S(1)}, u32[]{:S(2)}, u32[]{:S(2)}) collective-permute-start(f32[8,1]{1,0:T(8,128)S(1)} %get-tuple-element.37), channel_id=1, source_target_pairs={{1,0},{2,1},{3,2},{4,3},{5,4},{6,5},{7,6},{8,7},{9,8},{10,9},{11,1... | collective-permute-start | bytes 104 | tf_op jit(solution)/shard_map/ppermute | solution.py:18
  219.4 9.5 %collective-permute-start.4 = (f32[2,2,128]{2,1,0:T(2,128)S(1)}, f32[2,2,128]{2,1,0:T(2,128)S(1)}, u32[]{:S(2)}, u32[]{:S(2)}) collective-permute-start(f32[2,2,128]{2,1,0:T(2,128)S(1)} %get-tuple-element.34), channel_id=1, source_target_pairs={{0,32},{32,64},{64,96},{96,128},{128,160},{160,192},{192,224},{224... | collective-permute-start | bytes 6152 | tf_op jit(solution)/shard_map/ppermute | solution.py:18
  221.4 7.7 %collective-permute-start.5 = (f32[2,2,128]{2,1,0:T(2,128)S(1)}, f32[2,2,128]{2,1,0:T(2,128)S(1)}, u32[]{:S(2)}, u32[]{:S(2)}) collective-permute-start(f32[2,2,128]{2,1,0:T(2,128)S(1)} %get-tuple-element.35), channel_id=1, source_target_pairs={{32,0},{64,32},{96,64},{128,96},{160,128},{192,160},{224,192},{256... | collective-permute-start | bytes 6152 | tf_op jit(solution)/shard_map/ppermute | solution.py:18
  229.2 8.9 %collective-permute-start.6 = (f32[2,12,2]{2,1,0:T(8,128)S(1)}, f32[2,12,2]{2,1,0:T(8,128)S(1)}, u32[]{:S(2)}, u32[]{:S(2)}) collective-permute-start(f32[2,12,2]{2,1,0:T(8,128)S(1)} %get-tuple-element.30), channel_id=1, source_target_pairs={{0,1},{1,2},{2,3},{3,4},{4,5},{5,6},{6,7},{7,8},{8,9},{9,10},{10,1... | collective-permute-start | bytes 584 | tf_op jit(solution)/shard_map/ppermute | solution.py:18
  236.1 7.2 %collective-permute-start.7 = (f32[2,12,2]{2,1,0:T(8,128)S(1)}, f32[2,12,2]{2,1,0:T(8,128)S(1)}, u32[]{:S(2)}, u32[]{:S(2)}) collective-permute-start(f32[2,12,2]{2,1,0:T(8,128)S(1)} %get-tuple-element.31), channel_id=1, source_target_pairs={{1,0},{2,1},{3,2},{4,3},{5,4},{6,5},{7,6},{8,7},{9,8},{10,9},{11,1... | collective-permute-start | bytes 584 | tf_op jit(solution)/shard_map/ppermute | solution.py:18

commit v2 on v1

v2 whole, which is shorter than its diff:
```python
import functools

import jax
import jax.numpy as jnp
from jax import lax
from jax.experimental import pallas as pl
from jax.experimental.pallas import tpu as pltpu
from jax.sharding import PartitionSpec as P

ROUNDS = 4
SC = 32
CHUNK = 8

EPS2 = 0.05


def copy_for_each(x, axis):
    peers = lax.axis_size(axis)
    return lax.all_to_all(jnp.broadcast_to(x[None], (peers, *x.shape)), axis, 0, 0, tiled=True)


def from_peer(received, me, offset, peers):
    peer = me + offset
    ok = (peer >= 0) & (peer < peers)
    chunk = lax.dynamic_index_in_dim(received, jnp.clip(peer, 0, peers - 1), 0, keepdims=False)
    return jnp.where(ok, chunk, jnp.zeros_like(chunk))


def velocity_kernel(len_ref, src_ref, targ_ref, out_ref):
    tx, ty, tz = targ_ref[0], targ_ref[1], targ_ref[2]
    nx, ny, nz = targ_ref[3], targ_ref[4], targ_ref[5]

    def term(row, slot, acc):
        sx = src_ref[row, slot]
        sy = src_ref[row + 1, slot]
        sz = src_ref[row + 2, slot]
        q = src_ref[row + 3, slot]
        dx = tx - sx
        dy = ty - sy
        dz = tz - sz
        dist2 = dx * dx + dy * dy + dz * dz + EPS2
        numer = nx * dx + ny * dy + nz * dz
        r = lax.rsqrt(dist2)
        return acc + (q * numer) * (r * r * r)

    acc = jnp.zeros(out_ref.shape, jnp.float32)
    for step in range(ROUNDS):
        row = step * 4

        def column(c, acc, step=step, row=row):
            chunks = (len_ref[step, c] + (CHUNK - 1)) // CHUNK

            def chunk(j, acc):
                base = c * SC + j * CHUNK
                for u in range(CHUNK):
                    acc = term(row, base + u, acc)
                return acc

            return lax.fori_loop(0, chunks, chunk, acc)

        acc = lax.fori_loop(0, len_ref.shape[1], column, acc)
    out_ref[...] = acc


def velocity(group_len, src, targ):
    return pl.pallas_call(
        velocity_kernel,
        out_shape=jax.ShapeDtypeStruct(targ.shape[1:], jnp.float32),
        in_specs=[
            pl.BlockSpec(memory_space=pltpu.SMEM),
            pl.BlockSpec(memory_space=pltpu.SMEM),
            pl.BlockSpec(memory_space=pltpu.VMEM),
        ],
        out_specs=pl.BlockSpec(memory_space=pltpu.VMEM),
    )(group_len, src, targ)


def tendency(ext, vel):
    centre = ext[:, 1:-1, 1:-1]
    grad_x = (ext[:, 2:, 1:-1] - ext[:, :-2, 1:-1]) * 0.5
    grad_y = (ext[:, 1:-1, 2:] - ext[:, 1:-1, :-2]) * 0.5
    slope = 1.0 + grad_x[0] * grad_x[0] + grad_y[0] * grad_y[0]
    eta_rate = vel * slope - (grad_x[1] * grad_x[0] + grad_y[1] * grad_y[0])
    phi_rate = (
        -centre[0]
        - 0.5 * (grad_x[1] * grad_x[1] + grad_y[1] * grad_y[1])
        + 0.5 * vel * vel * slope
    )
    return jnp.stack([eta_rate, phi_rate])


def smooth(rim):
    centre = rim[:, 1:-1, 1:-1]
    return (
        4.0 * centre + rim[:, 2:, 1:-1] + rim[:, :-2, 1:-1] + rim[:, 1:-1, 2:] + rim[:, 1:-1, :-2]
    ) / 8.0


def body(target_geom, eta, phi, sources, group_len, owner):
    rows_here, cols_here = eta.shape
    n_tile, n_eval = lax.axis_size("tile"), lax.axis_size("eval")
    row = lax.axis_index("tile")
    column = lax.axis_index("eval")
    width = sources.shape[-1]
    group_len = group_len[:ROUNDS]
    owner = owner[:ROUNDS]

    live = jnp.arange(width, dtype=jnp.int32)[None, :] < group_len[:, column][:, None]
    mine = owner == row
    keep = jnp.concatenate(
        [jnp.broadcast_to(mine[:, None, None], (ROUNDS, 3, width)), (mine[:, None] & live)[:, None, :]],
        axis=1)
    picked = jnp.where(keep, sources[0], 0.0)

    fields = jnp.stack([eta, phi])
    n_src = ROUNDS * 4 * width
    payload = jnp.concatenate([
        picked.reshape(-1),
        fields[:, :2].reshape(-1), fields[:, -2:].reshape(-1),
        target_geom[:, :1].reshape(-1), target_geom[:, -1:].reshape(-1),
    ])
    got = copy_for_each(payload, "tile")
    src_rows = got[:, :n_src].reshape(n_tile, ROUNDS, 4, width)
    stacked = src_rows[owner, jnp.arange(ROUNDS)]
    rim = 2 * cols_here * 2
    above = from_peer(got[:, n_src:], row, -1, n_tile)
    below = from_peer(got[:, n_src:], row, 1, n_tile)
    f_above = above[rim:2 * rim].reshape(2, 2, cols_here)
    f_below = below[:rim].reshape(2, 2, cols_here)
    t_above = above[2 * rim + 6 * cols_here:].reshape(6, cols_here)
    t_below = below[2 * rim:2 * rim + 6 * cols_here].reshape(6, cols_here)
    ext_rows = jnp.concatenate([f_above, fields, f_below], axis=1)

    payload = jnp.concatenate([
        stacked.reshape(-1),
        ext_rows[:, :, :2].reshape(-1), ext_rows[:, :, -2:].reshape(-1),
        target_geom[:, :, 0].reshape(-1), target_geom[:, :, -1].reshape(-1),
    ])
    got = copy_for_each(payload, "eval")
    all_src = got[:, :n_src].reshape(n_eval, ROUNDS * 4, width)
    all_src = jnp.moveaxis(all_src, 0, 1).reshape(ROUNDS * 4, n_eval * width)
    rim = 2 * (rows_here + 4) * 2
    left = from_peer(got[:, n_src:], column, -1, n_eval)
    right = from_peer(got[:, n_src:], column, 1, n_eval)
    f_left = left[rim:2 * rim].reshape(2, rows_here + 4, 2)
    f_right = right[:rim].reshape(2, rows_here + 4, 2)
    t_left = left[2 * rim + 6 * rows_here:].reshape(6, rows_here)
    t_right = right[2 * rim:2 * rim + 6 * rows_here].reshape(6, rows_here)
    ext = jnp.concatenate([f_left, ext_rows, f_right], axis=2)

    sides = jnp.concatenate([t_left, t_right], axis=1)
    sides = jnp.pad(sides, ((0, 0), (0, cols_here - 2 * rows_here)))
    halo = jnp.stack([t_above, t_below, sides], axis=1)
    halo = jnp.pad(halo, ((0, 0), (0, rows_here - 3), (0, 0)))
    vel_all = velocity(group_len, all_src, jnp.concatenate([target_geom, halo], axis=1))
    vel_main = vel_all[:rows_here]
    vel_up = vel_all[rows_here:rows_here + 1]
    vel_down = vel_all[rows_here + 1:rows_here + 2]
    vel_left = vel_all[rows_here + 2, :rows_here][:, None]
    vel_right = vel_all[rows_here + 2, rows_here:2 * rows_here][:, None]

    vel_rows = jnp.concatenate([vel_up, vel_main, vel_down], axis=0)
    corner = jnp.zeros((1, 1), jnp.float32)
    vel_l = jnp.concatenate([corner, vel_left, corner], axis=0)
    vel_r = jnp.concatenate([corner, vel_right, corner], axis=0)
    vel = jnp.concatenate([vel_l, vel_rows, vel_r], axis=1)
    rates = tendency(ext, vel)
    row_ids = row * rows_here + jnp.arange(rows_here + 2, dtype=jnp.int32) - 1
    col_ids = column * cols_here + jnp.arange(cols_here + 2, dtype=jnp.int32) - 1
    row_ok = (row_ids >= 0) & (row_ids < rows_here * n_tile)
    col_ok = (col_ids >= 0) & (col_ids < cols_here * n_eval)
    inside = (row_ok[:, None] & col_ok[None, :]).astype(jnp.float32)
    smoothed = smooth(rates * inside[None])
    return (eta + 0.5 * smoothed[0], phi + 0.5 * smoothed[1], vel_main)


def solution(mesh):
    return jax.shard_map(
        body,
        mesh=mesh,
        in_specs=(
            P(None, "tile", "eval"),
            P("tile", "eval"),
            P("tile", "eval"),
            P("tile", None, None, "eval"),
            P(),
            P(),
        ),
        out_specs=(P("tile", "eval"), P("tile", "eval"), P("tile", "eval")),
        check_vma=False,
    )
```

time: 245 us -> 79.5 us (0.32)
  the two profiles are of different devices: /device:TPU:61 before, /device:TPU:1 now
where the time goes in v2:
time: 79.5 us; the launch traced here: 79 us
  Pallas kernels  26.3 us (33%)
  starting transfers between devices  23.3 us (29%)
  waiting for transfers between devices  16.9 us (21%)
  local copies, waits for them, and re-layouts  8.63 us (11%)
  other arithmetic  2.87 us (4%)
  between operations  0.96 us (1%)
    pallas_call x1, Pallas kernels, velocity(): pl.pallas_call(velocity_kernel, out_shape=jax.ShapeDtypeStruct(targ.shape...  26.3 us
    all_to_all x2, starting transfers between devices, copy_for_each(): lax.all_to_all(jnp.broadcast_to(x[None], (peers, *x.shape)), axis, 0, 0,...  23.3 us
    all_to_all x2, waiting for transfers between devices, copy_for_each(): lax.all_to_all(jnp.broadcast_to(x[None], (peers, *x.shape)), axis, 0, 0,...  16.9 us
  transfers between devices with their start and end apart: 2, of which 2 were waited for; matrix products, arithmetic and copies ran while one was open for 1% of the time, Pallas kernels for 0%

profile of v2, /device:TPU:1, one launch (start us, length us, event | category | flops | bytes accessed | tf_op | source)
XLA Modules:
  0.0 79.0 jit_solution(672547068721199875)
XLA Ops:
  0.7 0.9 %dynamic-slice_reduce_fusion = s32[4]{0:T(128)S(1)} fusion(s32[4,32]{1,0:T(4,128)} %len_ref.1, s32[]{:T(128)S(6)} %select_n.74), kind=kLoop, calls=%fused_computation.65 | loop fusion | bytes 36 | tf_op jit(solution)/shard_map/dynamic_slice | solution.py:108
  1.5 0.7 slice_compare_fusion
  2.2 0.1 compare_and_fusion
  2.3 0.1 broadcast_in_dim.12
  2.4 0.1 concatenate.65
  2.5 0.1 squeeze.8
  2.6 0.7 copy-done.1
  3.3 0.8 broadcast_in_dim.14
  4.1 13.5 %all-to-all-start = ((f32[16,1,3072]{2,1,0:T(1,128)}), f32[16,1,3072]{2,1,0:T(1,128)S(1)}, u32[]{:S(2)}, u32[]{:S(2)}) async-start(f32[16,1,3072]{2,1,0:T(1,128)} %broadcast_in_dim.14), calls=%async_computation | async-start | bytes 393216 | tf_op jit(solution)/shard_map/all_to_all | solution.py:19
  17.7 0.1 slice_reduce_fusion
  17.9 0.1 reshape_squeeze.6
  17.9 0.1 reshape_squeeze.7
  18.0 0.1 and_convert_fusion
  18.1 8.6 %all-to-all-done = f32[16,1,3072]{2,1,0:T(1,128)S(1)} async-done(((f32[16,1,3072]{2,1,0:T(1,128)}), f32[16,1,3072]{2,1,0:T(1,128)S(1)}, u32[]{:S(2)}, u32[]{:S(2)}) %all-to-all-start) | async-done | bytes 196640 | tf_op jit(solution)/shard_map/all_to_all | solution.py:19
  26.8 0.1 fusion.19
  26.9 0.1 reshape.316
  27.0 0.1 reshape.317
  27.1 0.1 reshape.314
  27.2 0.6 gather_fusion
  27.8 0.1 reshape.315
  27.9 0.1 concatenate.69
  28.0 0.7 broadcast_in_dim.16
  28.7 9.7 %all-to-all-start.1 = ((f32[32,1,704]{2,1,0:T(1,128)}), f32[32,1,704]{2,1,0:T(1,128)S(1)}, u32[]{:S(2)}, u32[]{:S(2)}) async-start(f32[32,1,704]{2,1,0:T(1,128)} %broadcast_in_dim.16), calls=%async_computation.1 | async-start | bytes 196608 | tf_op jit(solution)/shard_map/all_to_all | solution.py:19
  38.4 8.3 %all-to-all-done.1 = f32[32,1,704]{2,1,0:T(1,128)S(1)} async-done(((f32[32,1,704]{2,1,0:T(1,128)}), f32[32,1,704]{2,1,0:T(1,128)S(1)}, u32[]{:S(2)}, u32[]{:S(2)}) %all-to-all-start.1) | async-done | bytes 90144 | tf_op jit(solution)/shard_map/all_to_all | solution.py:19
  46.8 0.1 slice_reduce_fusion.4
  46.9 0.1 slice.194
  47.0 0.1 slice.196
  47.1 0.1 select_maximum_fusion.2
  47.2 0.6 pad_maximum_fusion.targ_ref
  47.8 0.1 reshape.318
  47.9 0.1 copy.35
  48.0 0.8 reshape.319.src_ref
  48.7 26.3 %shard_map.85 = f32[16,128]{1,0:T(8,128)} custom-call(s32[4,32]{1,0:T(4,128)} %len_ref.1, f32[16,1024]{1,0:T(8,128)} %reshape.319.src_ref, f32[6,16,128]{2,1,0:T(8,128)} %pad_maximum_fusion.targ_ref), custom_call_target="tpu_custom_call" | custom-call | tf_op jit(solution)/shard_map/pallas_call | solution.py:66
  75.1 0.7 slice.238
  75.7 0.8 fusion.20
  76.5 0.8 %slice_bitcast_fusion.3 = (f32[8,1]{0,1:T(1,128)S(1)}, f32[8,1]{0,1:T(1,128)S(1)}) fusion(f32[16,128]{1,0:T(8,128)} %shard_map.85), kind=kLoop, calls=%fused_computation.85 | loop fusion | bytes 128 | tf_op jit(solution)/shard_map/broadcast_in_dim;squeeze | solution.py:159
  77.3 0.1 slice.203
  77.4 0.1 slice.205
  77.5 0.1 pad_maximum_fusion.9
  77.6 0.1 fusion.1
  77.7 0.1 fusion.11
  77.8 0.1 copy.20
  77.9 0.1 fusion.12
  78.0 0.1 copy.21
  78.1 0.1 fusion.2
  78.2 0.1 add_subtract_fusion
  78.3 0.1 fusion.6
  78.4 0.6 fusion.8
  (39 shorter events, 0.3 us)
Async XLA Ops:
  0.6 1.9 %copy-start = (f32[6,8,128]{2,1,0:T(8,128)S(1)}, f32[6,8,128]{2,1,0:T(8,128)}, u32[]{:S(2)}) copy-start(f32[6,8,128]{2,1,0:T(8,128)} %param.6) | copy-start | bytes 73732
  1.5 0.9 %copy-start.4 = (f32[1,4,4,32]{3,2,1,0:T(4,128)S(1)}, f32[1,4,4,32]{3,2,1,0:T(4,128)}, u32[]{:S(2)}) copy-start(f32[1,4,4,32]{3,2,1,0:T(4,128)} %param.9) | copy-start | bytes 6148
  2.6 0.7 copy-start.1
  2.6 0.7 copy-start.2
  4.1 13.6 %copy-start.5 = (s32[16]{0:T(128)S(1)}, s32[16]{0:T(128)}, u32[]{:S(2)}) copy-start(s32[16]{0:T(128)} %param.11) | copy-start | bytes 196
  4.1 22.6 %all-to-all-start = ((f32[16,1,3072]{2,1,0:T(1,128)}), f32[16,1,3072]{2,1,0:T(1,128)S(1)}, u32[]{:S(2)}, u32[]{:S(2)}) async-start(f32[16,1,3072]{2,1,0:T(1,128)} %broadcast_in_dim.14), calls=%async_computation | async-start | bytes 393216 | tf_op jit(solution)/shard_map/all_to_all | solution.py:19
  28.7 18.1 %all-to-all-start.1 = ((f32[32,1,704]{2,1,0:T(1,128)}), f32[32,1,704]{2,1,0:T(1,128)S(1)}, u32[]{:S(2)}, u32[]{:S(2)}) async-start(f32[32,1,704]{2,1,0:T(1,128)} %broadcast_in_dim.16), calls=%async_computation.1 | async-start | bytes 196608 | tf_op jit(solution)/shard_map/all_to_all | solution.py:19
  75.7 2.4 %copy-start.3 = (f32[8,128]{1,0:T(8,128)}, f32[8,128]{1,0:T(8,128)S(1)}, u32[]{:S(2)}) copy-start(f32[8,128]{1,0:T(8,128)S(1)} %slice.238) | copy-start | bytes 12292

commit v3 on v2

--- a/solution.py
+++ b/solution.py
@@ -29,12 +29,13 @@
 def velocity_kernel(len_ref, src_ref, targ_ref, out_ref):
     tx, ty, tz = targ_ref[0], targ_ref[1], targ_ref[2]
     nx, ny, nz = targ_ref[3], targ_ref[4], targ_ref[5]
+    per_column = ROUNDS * SC * 4
 
-    def term(row, slot, acc):
-        sx = src_ref[row, slot]
-        sy = src_ref[row + 1, slot]
-        sz = src_ref[row + 2, slot]
-        q = src_ref[row + 3, slot]
+    def term(at, acc):
+        sx = src_ref[at]
+        sy = src_ref[at + 1]
+        sz = src_ref[at + 2]
+        q = src_ref[at + 3]
         dx = tx - sx
         dy = ty - sy
         dz = tz - sz
@@ -45,15 +46,15 @@
 
     acc = jnp.zeros(out_ref.shape, jnp.float32)
     for step in range(ROUNDS):
-        row = step * 4
 
-        def column(c, acc, step=step, row=row):
+        def column(c, acc, step=step):
             chunks = (len_ref[step, c] + (CHUNK - 1)) // CHUNK
+            start = c * per_column + step * SC * 4
 
             def chunk(j, acc):
-                base = c * SC + j * CHUNK
+                base = start + j * (CHUNK * 4)
                 for u in range(CHUNK):
-                    acc = term(row, base + u, acc)
+                    acc = term(base + 4 * u, acc)
                 return acc
 
             return lax.fori_loop(0, chunks, chunk, acc)
@@ -105,22 +106,15 @@
     group_len = group_len[:ROUNDS]
     owner = owner[:ROUNDS]
 
-    live = jnp.arange(width, dtype=jnp.int32)[None, :] < group_len[:, column][:, None]
-    mine = owner == row
-    keep = jnp.concatenate(
-        [jnp.broadcast_to(mine[:, None, None], (ROUNDS, 3, width)), (mine[:, None] & live)[:, None, :]],
-        axis=1)
-    picked = jnp.where(keep, sources[0], 0.0)
-
     fields = jnp.stack([eta, phi])
     n_src = ROUNDS * 4 * width
     payload = jnp.concatenate([
-        picked.reshape(-1),
+        jnp.swapaxes(sources[0], 1, 2).reshape(-1),
         fields[:, :2].reshape(-1), fields[:, -2:].reshape(-1),
         target_geom[:, :1].reshape(-1), target_geom[:, -1:].reshape(-1),
     ])
     got = copy_for_each(payload, "tile")
-    src_rows = got[:, :n_src].reshape(n_tile, ROUNDS, 4, width)
+    src_rows = got[:, :n_src].reshape(n_tile, ROUNDS, width * 4)
     stacked = src_rows[owner, jnp.arange(ROUNDS)]
     rim = 2 * cols_here * 2
     above = from_peer(got[:, n_src:], row, -1, n_tile)
@@ -137,8 +131,10 @@
         target_geom[:, :, 0].reshape(-1), target_geom[:, :, -1].reshape(-1),
     ])
     got = copy_for_each(payload, "eval")
-    all_src = got[:, :n_src].reshape(n_eval, ROUNDS * 4, width)
-    all_src = jnp.moveaxis(all_src, 0, 1).reshape(ROUNDS * 4, n_eval * width)
+    all_src = got[:, :n_src].reshape(n_eval, ROUNDS, width * 4)
+    lane = jnp.arange(width * 4, dtype=jnp.int32)
+    keep = ((lane % 4) != 3)[None, None, :] | ((lane // 4)[None, None, :] < group_len.T[:, :, None])
+    all_src = jnp.where(keep, all_src, 0.0).reshape(-1)
     rim = 2 * (rows_here + 4) * 2
     left = from_peer(got[:, n_src:], column, -1, n_eval)
     right = from_peer(got[:, n_src:], column, 1, n_eval)

time: 79.5 us -> 77.3 us (0.972)
  waiting for transfers between devices: 16.9 us -> 15.4 us
  Pallas kernels: 26.3 us -> 25 us
    unnamed x17 -> x20, local copies, waits for them, and re-layouts: 0.77 us -> 2.78 us
    all_to_all x2, waiting for transfers between devices: 16.9 us -> 15.4 us  [copy_for_each(): lax.all_to_all(jnp.broadcast_to(x[None], (peers, *x.shape)), axis, 0, 0,...]
    pallas_call x1, Pallas kernels: 26.3 us -> 25 us  [velocity(): pl.pallas_call(velocity_kernel, out_shape=jax.ShapeDtypeStruct(targ.shape...]
    reshape x5 -> x2, local copies, waits for them, and re-layouts: 1.15 us -> 0.12 us  [the longest x1 0.1 us: body(): jnp.swapaxes(sources[0], 1, 2).reshape(-1)]
    transpose x0 -> x2, local copies, waits for them, and re-layouts: none -> 0.88 us  [the longest x1 0.8 us: body(): jnp.swapaxes(sources[0], 1, 2).reshape(-1)]
    dynamic_slice x1 -> x0, local copies, waits for them, and re-layouts: 0.87 us -> none  [body(): group_len[:, column][:, None]]
where the time goes in v3:
time: 77.3 us; the launch traced here: 76.7 us
  Pallas kernels  25 us (32%)
  starting transfers between devices  23.1 us (30%)
  waiting for transfers between devices  15.4 us (20%)
  local copies, waits for them, and re-layouts  9.37 us (12%)
  other arithmetic  2.82 us (4%)
  between operations  0.9 us (1%)
    pallas_call x1, Pallas kernels, velocity(): pl.pallas_call(velocity_kernel, out_shape=jax.ShapeDtypeStruct(targ.shape...  25 us
    all_to_all x2, starting transfers between devices, copy_for_each(): lax.all_to_all(jnp.broadcast_to(x[None], (peers, *x.shape)), axis, 0, 0,...  23.1 us
    all_to_all x2, waiting for transfers between devices, copy_for_each(): lax.all_to_all(jnp.broadcast_to(x[None], (peers, *x.shape)), axis, 0, 0,...  15.4 us
    unnamed x20, local copies, waits for them, and re-layouts  2.78 us
  transfers between devices with their start and end apart: 2, of which 2 were waited for; matrix products, arithmetic and copies ran while one was open for 1% of the time, Pallas kernels for 0%

profile of v3, /device:TPU:1, one launch (start us, length us, event | category | flops | bytes accessed | tf_op | source)
XLA Modules:
  0.0 76.7 jit_solution(386227378822765074)
XLA Ops:
  0.6 0.8 %copy.19 = f32[4,32,4]{2,1,0:T(8,128)S(1)} copy(f32[4,32,4]{1,2,0:T(4,128)} %bitcast.80) | data formatting | bytes 4096 | tf_op jit(solution)/shard_map/transpose | solution.py:112
  1.4 0.1 reshape.283
  1.5 0.6 copy-done
  2.2 0.7 copy-done.1
  2.9 0.0 copy-done.2
  2.9 0.8 %broadcast_in_dim.9 = f32[16,1,3072]{2,1,0:T(1,128)} broadcast(f32[3072]{0:T(1024)S(1)} %constant_dynamic-update-slice_fusion), dimensions={2} | broadcast | bytes 208896 | tf_op jit(solution)/shard_map/broadcast_in_dim | solution.py:19
  3.7 13.4 %all-to-all-start = ((f32[16,1,3072]{2,1,0:T(1,128)}), f32[16,1,3072]{2,1,0:T(1,128)S(1)}, u32[]{:S(2)}, u32[]{:S(2)}) async-start(f32[16,1,3072]{2,1,0:T(1,128)} %broadcast_in_dim.9), calls=%async_computation | async-start | bytes 393216 | tf_op jit(solution)/shard_map/all_to_all | solution.py:19
  17.1 0.1 slice_reduce_fusion
  17.3 0.0 copy-start.5
  17.3 0.7 copy-done.5
  18.0 0.1 and_convert_fusion
  18.1 0.1 reshape_squeeze.6
  18.2 0.1 reshape_squeeze.7
  18.2 0.7 copy-done.4
  18.9 0.1 copy.18
  19.0 0.1 compare_or_fusion
  19.1 7.1 %all-to-all-done = f32[16,1,3072]{2,1,0:T(1,128)S(1)} async-done(((f32[16,1,3072]{2,1,0:T(1,128)}), f32[16,1,3072]{2,1,0:T(1,128)S(1)}, u32[]{:S(2)}, u32[]{:S(2)}) %all-to-all-start) | async-done | bytes 196640 | tf_op jit(solution)/shard_map/all_to_all | solution.py:19
  26.3 0.1 fusion.20
  26.4 0.1 reshape.290
  26.5 0.1 reshape.291
  26.6 0.6 gather_fusion
  27.2 0.1 concatenate.62
  27.3 0.7 broadcast_in_dim.11
  28.0 9.7 %all-to-all-start.1 = ((f32[32,1,704]{2,1,0:T(1,128)}), f32[32,1,704]{2,1,0:T(1,128)S(1)}, u32[]{:S(2)}, u32[]{:S(2)}) async-start(f32[32,1,704]{2,1,0:T(1,128)} %broadcast_in_dim.11), calls=%async_computation.1 | async-start | bytes 196608 | tf_op jit(solution)/shard_map/all_to_all | solution.py:19
  37.7 8.3 %all-to-all-done.1 = f32[32,1,704]{2,1,0:T(1,128)S(1)} async-done(((f32[32,1,704]{2,1,0:T(1,128)}), f32[32,1,704]{2,1,0:T(1,128)S(1)}, u32[]{:S(2)}, u32[]{:S(2)}) %all-to-all-start.1) | async-done | bytes 90144 | tf_op jit(solution)/shard_map/all_to_all | solution.py:19
  46.1 0.1 slice_reduce_fusion.4
  46.2 0.1 slice.194
  46.3 0.1 slice.196
  46.4 0.1 select_maximum_fusion.2
  46.5 0.6 pad_maximum_fusion.targ_ref
  47.1 0.6 broadcast_select_fusion.src_ref
  47.7 25.0 %shard_map.85 = f32[16,128]{1,0:T(8,128)} custom-call(s32[4,32]{1,0:T(4,128)} %len_ref.1, f32[16384]{0:T(1024)} %broadcast_select_fusion.src_ref, f32[6,16,128]{2,1,0:T(8,128)} %pad_maximum_fusion.targ_ref), custom_call_target="tpu_custom_call" | custom-call | tf_op jit(solution)/shard_map/pallas_call | solution.py:67
  72.8 0.7 slice.238
  73.4 0.8 fusion.21
  74.2 0.8 %slice_bitcast_fusion.4 = (f32[8,1]{0,1:T(1,128)S(1)}, f32[8,1]{0,1:T(1,128)S(1)}) fusion(f32[16,128]{1,0:T(8,128)} %shard_map.85), kind=kLoop, calls=%fused_computation.87 | loop fusion | bytes 128 | tf_op jit(solution)/shard_map/broadcast_in_dim;squeeze | solution.py:155
  75.0 0.1 slice.203
  75.1 0.1 slice.205
  75.2 0.1 pad_maximum_fusion.9
  75.3 0.1 fusion.1
  75.4 0.1 fusion.11
  75.5 0.1 copy.22
  75.6 0.1 fusion.12
  75.7 0.1 copy.23
  75.8 0.1 fusion.2
  75.8 0.0 copy-done.3
  75.9 0.1 add_subtract_fusion
  76.0 0.1 fusion.6
  76.0 0.6 fusion.8
  (36 shorter events, 0.3 us)
Async XLA Ops:
  1.4 0.7 copy-start
  2.2 0.7 copy-start.1
  2.2 0.7 copy-start.2
  3.7 22.5 %all-to-all-start = ((f32[16,1,3072]{2,1,0:T(1,128)}), f32[16,1,3072]{2,1,0:T(1,128)S(1)}, u32[]{:S(2)}, u32[]{:S(2)}) async-start(f32[16,1,3072]{2,1,0:T(1,128)} %broadcast_in_dim.9), calls=%async_computation | async-start | bytes 393216 | tf_op jit(solution)/shard_map/all_to_all | solution.py:19
  17.3 0.7 copy-start.5
  18.2 0.7 copy-start.4
  28.0 18.1 %all-to-all-start.1 = ((f32[32,1,704]{2,1,0:T(1,128)}), f32[32,1,704]{2,1,0:T(1,128)S(1)}, u32[]{:S(2)}, u32[]{:S(2)}) async-start(f32[32,1,704]{2,1,0:T(1,128)} %broadcast_in_dim.11), calls=%async_computation.1 | async-start | bytes 196608 | tf_op jit(solution)/shard_map/all_to_all | solution.py:19
  73.4 2.4 %copy-start.3 = (f32[8,128]{1,0:T(8,128)}, f32[8,128]{1,0:T(8,128)S(1)}, u32[]{:S(2)}) copy-start(f32[8,128]{1,0:T(8,128)S(1)} %slice.238) | copy-start | bytes 12292

commit v4 on v3

--- a/solution.py
+++ b/solution.py
@@ -74,6 +74,36 @@
         ],
         out_specs=pl.BlockSpec(memory_space=pltpu.VMEM),
     )(group_len, src, targ)
+
+
+def halo_kernel(src_ref, targ_ref, out_ref):
+    def group(g, carry):
+        tx, ty, tz = targ_ref[g, 0], targ_ref[g, 1], targ_ref[g, 2]
+        nx, ny, nz = targ_ref[g, 3], targ_ref[g, 4], targ_ref[g, 5]
+
+        def chunk(j, acc):
+            dx = tx - src_ref[0, j]
+            dy = ty - src_ref[1, j]
+            dz = tz - src_ref[2, j]
+            dist2 = dx * dx + dy * dy + dz * dz + EPS2
+            numer = nx * dx + ny * dy + nz * dz
+            r = lax.rsqrt(dist2)
+            return acc + (src_ref[3, j] * numer) * (r * r * r)
+
+        out_ref[g] = lax.fori_loop(0, src_ref.shape[1], chunk, jnp.zeros(out_ref.shape[1:], jnp.float32),
+                                   unroll=8)
+        return carry
+
+    lax.fori_loop(0, targ_ref.shape[0], group, 0)
+
+
+def halo_velocity(src, targ):
+    return pl.pallas_call(
+        halo_kernel,
+        out_shape=jax.ShapeDtypeStruct((targ.shape[0], 8, 128), jnp.float32),
+        in_specs=[pl.BlockSpec(memory_space=pltpu.VMEM), pl.BlockSpec(memory_space=pltpu.VMEM)],
+        out_specs=pl.BlockSpec(memory_space=pltpu.VMEM),
+    )(src, targ)
 
 
 def tendency(ext, vel):
@@ -144,16 +174,19 @@
     t_right = right[2 * rim:2 * rim + 6 * rows_here].reshape(6, rows_here)
     ext = jnp.concatenate([f_left, ext_rows, f_right], axis=2)
 
-    sides = jnp.concatenate([t_left, t_right], axis=1)
-    sides = jnp.pad(sides, ((0, 0), (0, cols_here - 2 * rows_here)))
-    halo = jnp.stack([t_above, t_below, sides], axis=1)
-    halo = jnp.pad(halo, ((0, 0), (0, rows_here - 3), (0, 0)))
-    vel_all = velocity(group_len, all_src, jnp.concatenate([target_geom, halo], axis=1))
-    vel_main = vel_all[:rows_here]
-    vel_up = vel_all[rows_here:rows_here + 1]
-    vel_down = vel_all[rows_here + 1:rows_here + 2]
-    vel_left = vel_all[rows_here + 2, :rows_here][:, None]
-    vel_right = vel_all[rows_here + 2, rows_here:2 * rows_here][:, None]
+    vel_main = velocity(group_len, all_src, target_geom)
+
+    halo = jnp.concatenate([t_above, t_below, t_left, t_right], axis=1)
+    n_halo = halo.shape[1]
+    groups = n_halo // 8
+    halo_t = jnp.broadcast_to(jnp.swapaxes(halo.reshape(6, groups, 8), 0, 1)[..., None], (groups, 6, 8, 128))
+    src_t = all_src.reshape(-1, 4).T.reshape(4, -1, 1, 128)
+    src_t = jnp.broadcast_to(src_t, (4, src_t.shape[1], 8, 128))
+    vel_halo = halo_velocity(src_t, halo_t).sum(axis=-1).reshape(-1)
+    vel_up = vel_halo[None, :cols_here]
+    vel_down = vel_halo[None, cols_here:2 * cols_here]
+    vel_left = vel_halo[2 * cols_here:2 * cols_here + rows_here][:, None]
+    vel_right = vel_halo[2 * cols_here + rows_here:][:, None]
 
     vel_rows = jnp.concatenate([vel_up, vel_main, vel_down], axis=0)
     corner = jnp.zeros((1, 1), jnp.float32)

time: 77.3 us -> 84.9 us (1.098)
  local copies, waits for them, and re-layouts: 9.37 us -> 15.7 us
  other arithmetic: 2.82 us -> 7.58 us
  waiting for transfers between devices: 15.4 us -> 12.3 us
    pallas_call x1, Pallas kernels: 25 us -> 18 us  [velocity(): pl.pallas_call(velocity_kernel, out_shape=jax.ShapeDtypeStruct(targ.shape...]
    pallas_call x0 -> x1, Pallas kernels: none -> 6.41 us  [halo_velocity(): pl.pallas_call(halo_kernel, out_shape=jax.ShapeDtypeStruct((targ.shape[0]...]
    broadcast_in_dim x0 -> x6, local copies, waits for them, and re-layouts: none -> 4.41 us  [the longest x2 3.05 us: body(): src_t = jnp.broadcast_to(src_t, (4, src_t.shape[1], 8, 128))]
    all_to_all x2, waiting for transfers between devices: 15.4 us -> 12.3 us  [copy_for_each(): lax.all_to_all(jnp.broadcast_to(x[None], (peers, *x.shape)), axis, 0, 0,...]
    unnamed x20 -> x12, local copies, waits for them, and re-layouts: 2.78 us -> 0.11 us
    or x0 -> x1, local copies, waits for them, and re-layouts: none -> 2.27 us  [body(): (lane % 4 != 3)[None, None, :]]
    reshape x0 -> x2, local copies, waits for them, and re-layouts: none -> 2.26 us  [the longest x1 2.15 us: body(): all_src = got[:, :n_src].reshape(n_eval, ROUNDS, width * 4)]
    select_n x1 -> x2, other arithmetic: 0.63 us -> 2.19 us  [body(): all_src = jnp.where(keep, all_src, 0.0).reshape(-1)]
  transfers between devices with their start and end apart: 2 -> 2, of which waited for: 2 -> 2; matrix products, arithmetic and copies ran while one was open for 1% -> 6% of each run, Pallas kernels for 0% -> 0%
where the time goes in v4:
time: 84.9 us; the launch traced here: 84.1 us
  Pallas kernels  24.4 us (29%)
  starting transfers between devices  23.1 us (27%)
  local copies, waits for them, and re-layouts  15.7 us (18%)
  waiting for transfers between devices  12.3 us (14%)
  other arithmetic  7.58 us (9%)
  between operations  0.98 us (1%)
    all_to_all x2, starting transfers between devices, copy_for_each(): lax.all_to_all(jnp.broadcast_to(x[None], (peers, *x.shape)), axis, 0, 0,...  23.1 us
    pallas_call x1, Pallas kernels, velocity(): pl.pallas_call(velocity_kernel, out_shape=jax.ShapeDtypeStruct(targ.shape...  18 us
    all_to_all x2, waiting for transfers between devices, copy_for_each(): lax.all_to_all(jnp.broadcast_to(x[None], (peers, *x.shape)), axis, 0, 0,...  12.3 us
    pallas_call x1, Pallas kernels, halo_velocity(): pl.pallas_call(halo_kernel, out_shape=jax.ShapeDtypeStruct((targ.shape[0]...  6.41 us
    broadcast_in_dim x2, local copies, waits for them, and re-layouts, body(): src_t = jnp.broadcast_to(src_t, (4, src_t.shape[1], 8, 128))  3.05 us
    or x1, local copies, waits for them, and re-layouts, body(): (lane % 4 != 3)[None, None, :]  2.27 us
    select_n x2, other arithmetic, body(): all_src = jnp.where(keep, all_src, 0.0).reshape(-1)  2.19 us
    reshape x1, local copies, waits for them, and re-layouts, body(): all_src = got[:, :n_src].reshape(n_eval, ROUNDS, width * 4)  2.15 us
  transfers between devices with their start and end apart: 2, of which 2 were waited for; matrix products, arithmetic and copies ran while one was open for 6% of the time, Pallas kernels for 0%

profile of v4, /device:TPU:1, one launch (start us, length us, event | category | flops | bytes accessed | tf_op | source)
XLA Modules:
  0.0 84.1 jit_solution(13604036692077382680)
XLA Ops:
  0.6 0.8 copy.22
  1.4 0.1 reshape.290
  1.5 0.8 fusion.19
  2.4 0.8 pad_maximum_fusion.12
  3.2 0.8 broadcast_in_dim.26
  4.0 13.4 %all-to-all-start = ((f32[16,1,3072]{2,1,0:T(1,128)}), f32[16,1,3072]{2,1,0:T(1,128)S(1)}, u32[]{:S(2)}, u32[]{:S(2)}) async-start(f32[16,1,3072]{2,1,0:T(1,128)} %broadcast_in_dim.26), calls=%async_computation | async-start | bytes 393216 | tf_op jit(solution)/shard_map/all_to_all | solution.py:19
  17.4 0.9 %slice_reduce_fusion = (f32[6,8]{1,0:T(8,128)S(1)}, f32[6,8]{1,0:T(8,128)S(1)}) fusion(f32[6,8,128]{2,1,0:T(8,128)} %targ_ref.1), kind=kLoop, calls=%fused_computation.21 | loop fusion | bytes 768 | tf_op jit(solution)/shard_map/slice | solution.py:161
  18.4 0.7 fusion.18
  19.1 0.1 reshape_squeeze.6
  19.2 0.1 reshape_squeeze.7
  19.2 0.8 copy.21
  20.0 0.1 compare_or_fusion
  20.1 6.3 %all-to-all-done = f32[16,1,3072]{2,1,0:T(1,128)S(1)} async-done(((f32[16,1,3072]{2,1,0:T(1,128)}), f32[16,1,3072]{2,1,0:T(1,128)S(1)}, u32[]{:S(2)}, u32[]{:S(2)}) %all-to-all-start) | async-done | bytes 196640 | tf_op jit(solution)/shard_map/all_to_all | solution.py:19
  26.6 0.7 pad_maximum_fusion.9
  27.3 0.1 reshape.297
  27.4 0.1 reshape.298
  27.6 0.6 gather_fusion
  28.1 0.1 concatenate.59
  28.2 0.7 broadcast_in_dim.28
  28.9 9.7 %all-to-all-start.1 = ((f32[32,1,704]{2,1,0:T(1,128)}), f32[32,1,704]{2,1,0:T(1,128)S(1)}, u32[]{:S(2)}, u32[]{:S(2)}) async-start(f32[32,1,704]{2,1,0:T(1,128)} %broadcast_in_dim.28), calls=%async_computation.1 | async-start | bytes 196608 | tf_op jit(solution)/shard_map/all_to_all | solution.py:19
  38.7 2.3 %or.18 = pred[4096,4]{1,0:T(8,128)(4,1)S(1)} reshape(pred[32,4,128]{2,1,0:T(4,128)(4,1)S(1)} %compare_or_fusion) | data formatting | bytes 32768 | tf_op jit(solution)/shard_map/or | solution.py:166
  41.0 6.0 %all-to-all-done.1 = f32[32,1,704]{2,1,0:T(1,128)S(1)} async-done(((f32[32,1,704]{2,1,0:T(1,128)}), f32[32,1,704]{2,1,0:T(1,128)S(1)}, u32[]{:S(2)}, u32[]{:S(2)}) %all-to-all-start.1) | async-done | bytes 90144 | tf_op jit(solution)/shard_map/all_to_all | solution.py:19
  47.0 2.1 %reshape.299 = f32[4096,4]{1,0:T(8,128)S(1)} reshape(f32[32,512]{1,0:T(8,128)S(1)} %get-tuple-element.12) | data formatting | bytes 131072 | tf_op jit(solution)/shard_map/reshape | solution.py:164
  49.2 1.6 %broadcast_select_fusion = f32[4096,4]{1,0:T(8,128)} fusion(pred[4096,4]{1,0:T(8,128)(4,1)S(1)} %or.18, f32[4096,4]{1,0:T(8,128)S(1)} %reshape.299), kind=kLoop, calls=%fused_computation.1 | loop fusion | flops 16384 | bytes 147456 | tf_op jit(solution)/shard_map/jit(_where)/select_n | solution.py:167
  50.8 2.2 %copy.25 = f32[4,32,128]{2,1,0:T(8,128)S(1)} copy(f32[4,32,128]{0,2,1:T(8,128)} %bitcast.61) | data formatting | bytes 131072 | tf_op jit(solution)/shard_map/broadcast_in_dim | solution.py:184
  53.0 0.1 slice_reduce_fusion.6
  53.1 0.1 slice.195
  53.2 0.1 pad_maximum_fusion.11
  53.3 0.1 reshape.300
  53.5 0.8 broadcast_in_dim.58.src_ref
  54.3 1.2 %broadcast_in_dim.59.targ_ref = f32[34,6,8,128]{3,2,1,0:T(8,128)} broadcast(f32[34,6,8]{2,1,0:T(8,128)S(1)} %copy.26), dimensions={0,1,2} | broadcast | bytes 842112 | tf_op jit(solution)/shard_map/broadcast_in_dim | solution.py:182
  55.5 6.4 %shard_map.85 = f32[34,8,128]{2,1,0:T(8,128)} custom-call(f32[4,32,8,128]{3,2,1,0:T(8,128)} %broadcast_in_dim.58.src_ref, f32[34,6,8,128]{3,2,1,0:T(8,128)} %broadcast_in_dim.59.targ_ref), custom_call_target="tpu_custom_call" | custom-call | tf_op jit(solution)/shard_map/pallas_call | solution.py:101
  61.9 1.0 %reduce_sum.9 = f32[34,8]{1,0:T(8,128)S(1)} reduce(f32[34,8,128]{2,1,0:T(8,128)} %shard_map.85, f32[]{:T(128)} %constant.91.clone.1), dimensions={2}, to_apply=%region_0.1 | reduce | flops 34544 | bytes 140356 | tf_op jit(solution)/shard_map/reduce_sum | solution.py:185
  63.0 0.1 slice.203
  63.0 0.1 slice.205
  63.2 0.1 pad_maximum_fusion.8
  63.3 0.1 fusion.1
  63.4 0.1 broadcast_in_dim.61
  63.4 0.1 broadcast_in_dim.63
  63.6 0.6 broadcast_select_fusion.1.src_ref
  64.2 18.0 %shard_map.86 = f32[8,128]{1,0:T(8,128)} custom-call(s32[4,32]{1,0:T(4,128)} %len_ref.1, f32[16384]{0:T(1024)} %broadcast_select_fusion.1.src_ref, f32[6,8,128]{2,1,0:T(8,128)} %targ_ref.1), custom_call_target="tpu_custom_call" | custom-call | tf_op jit(solution)/shard_map/pallas_call | solution.py:67
  82.3 0.1 copy.27
  82.5 0.1 copy.28
  82.6 0.1 fusion.2
  82.7 0.7 maximum_bitcast_fusion
  83.4 0.1 add_subtract_fusion
  83.5 0.1 fusion.6
  83.5 0.6 fusion.8
  (36 shorter events, 0.7 us)
Async XLA Ops:
  4.0 22.5 %all-to-all-start = ((f32[16,1,3072]{2,1,0:T(1,128)}), f32[16,1,3072]{2,1,0:T(1,128)S(1)}, u32[]{:S(2)}, u32[]{:S(2)}) async-start(f32[16,1,3072]{2,1,0:T(1,128)} %broadcast_in_dim.26), calls=%async_computation | async-start | bytes 393216 | tf_op jit(solution)/shard_map/all_to_all | solution.py:19
  28.9 18.1 %all-to-all-start.1 = ((f32[32,1,704]{2,1,0:T(1,128)}), f32[32,1,704]{2,1,0:T(1,128)S(1)}, u32[]{:S(2)}, u32[]{:S(2)}) async-start(f32[32,1,704]{2,1,0:T(1,128)} %broadcast_in_dim.28), calls=%async_computation.1 | async-start | bytes 196608 | tf_op jit(solution)/shard_map/all_to_all | solution.py:19
  53.0 10.2 %copy-start = (f32[8,128]{1,0:T(8,128)S(1)}, f32[8,128]{1,0:T(8,128)}, u32[]{:S(2)}) copy-start(f32[8,128]{1,0:T(8,128)} %param.8) | copy-start | bytes 12292
  53.0 10.2 %copy-start.1 = (f32[8,128]{1,0:T(8,128)S(1)}, f32[8,128]{1,0:T(8,128)}, u32[]{:S(2)}) copy-start(f32[8,128]{1,0:T(8,128)} %param.7) | copy-start | bytes 12292

commit v5 on v3

--- a/solution.py
+++ b/solution.py
@@ -44,20 +44,26 @@
         r = lax.rsqrt(dist2)
         return acc + (q * numer) * (r * r * r)
 
+    def run(start, size):
+        def block(j, acc):
+            base = start + j * (size * 4)
+            for u in range(size):
+                acc = term(base + 4 * u, acc)
+            return acc
+        return block
+
     acc = jnp.zeros(out_ref.shape, jnp.float32)
     for step in range(ROUNDS):
 
         def column(c, acc, step=step):
-            chunks = (len_ref[step, c] + (CHUNK - 1)) // CHUNK
+            n = len_ref[step, c]
+            eights = n // CHUNK
+            pairs = eights // 2
+            fours = (n - eights * CHUNK + 3) // 4
             start = c * per_column + step * SC * 4
-
-            def chunk(j, acc):
-                base = start + j * (CHUNK * 4)
-                for u in range(CHUNK):
-                    acc = term(base + 4 * u, acc)
-                return acc
-
-            return lax.fori_loop(0, chunks, chunk, acc)
+            acc = lax.fori_loop(0, pairs, run(start, 2 * CHUNK), acc)
+            acc = lax.fori_loop(pairs * 2, eights, run(start, CHUNK), acc)
+            return lax.fori_loop(0, fours, run(start + eights * CHUNK * 4, 4), acc)
 
         acc = lax.fori_loop(0, len_ref.shape[1], column, acc)
     out_ref[...] = acc

time: 77.3 us -> 77.9 us (level)
  no operation moved by 1% of the time
where the time goes in v5:
time: 77.9 us; the launch traced here: 77.3 us
  Pallas kernels  25.7 us (33%)
  starting transfers between devices  23.1 us (30%)
  waiting for transfers between devices  15.4 us (20%)
  local copies, waits for them, and re-layouts  9.37 us (12%)
  other arithmetic  2.82 us (4%)
  between operations  0.9 us (1%)
    pallas_call x1, Pallas kernels, velocity(): pl.pallas_call(velocity_kernel, out_shape=jax.ShapeDtypeStruct(targ.shape...  25.7 us
    all_to_all x2, starting transfers between devices, copy_for_each(): lax.all_to_all(jnp.broadcast_to(x[None], (peers, *x.shape)), axis, 0, 0,...  23.1 us
    all_to_all x2, waiting for transfers between devices, copy_for_each(): lax.all_to_all(jnp.broadcast_to(x[None], (peers, *x.shape)), axis, 0, 0,...  15.4 us
    unnamed x20, local copies, waits for them, and re-layouts  2.78 us
  transfers between devices with their start and end apart: 2, of which 2 were waited for; matrix products, arithmetic and copies ran while one was open for 1% of the time, Pallas kernels for 0%

profile of v5, /device:TPU:1, one launch (start us, length us, event | category | flops | bytes accessed | tf_op | source)
XLA Modules:
  0.0 77.3 jit_solution(11109242104774592660)
XLA Ops:
  0.6 0.8 %copy.19 = f32[4,32,4]{2,1,0:T(8,128)S(1)} copy(f32[4,32,4]{1,2,0:T(4,128)} %bitcast.80) | data formatting | bytes 4096 | tf_op jit(solution)/shard_map/transpose | solution.py:118
  1.4 0.1 reshape.283
  1.5 0.6 copy-done
  2.2 0.7 copy-done.1
  2.9 0.0 copy-done.2
  2.9 0.8 %broadcast_in_dim.9 = f32[16,1,3072]{2,1,0:T(1,128)} broadcast(f32[3072]{0:T(1024)S(1)} %constant_dynamic-update-slice_fusion), dimensions={2} | broadcast | bytes 208896 | tf_op jit(solution)/shard_map/broadcast_in_dim | solution.py:19
  3.7 13.4 %all-to-all-start = ((f32[16,1,3072]{2,1,0:T(1,128)}), f32[16,1,3072]{2,1,0:T(1,128)S(1)}, u32[]{:S(2)}, u32[]{:S(2)}) async-start(f32[16,1,3072]{2,1,0:T(1,128)} %broadcast_in_dim.9), calls=%async_computation | async-start | bytes 393216 | tf_op jit(solution)/shard_map/all_to_all | solution.py:19
  17.1 0.1 slice_reduce_fusion
  17.3 0.0 copy-start.5
  17.3 0.7 copy-done.5
  18.0 0.1 and_convert_fusion
  18.1 0.1 reshape_squeeze.6
  18.2 0.1 reshape_squeeze.7
  18.2 0.7 copy-done.4
  18.9 0.1 copy.18
  19.0 0.1 compare_or_fusion
  19.1 7.1 %all-to-all-done = f32[16,1,3072]{2,1,0:T(1,128)S(1)} async-done(((f32[16,1,3072]{2,1,0:T(1,128)}), f32[16,1,3072]{2,1,0:T(1,128)S(1)}, u32[]{:S(2)}, u32[]{:S(2)}) %all-to-all-start) | async-done | bytes 196640 | tf_op jit(solution)/shard_map/all_to_all | solution.py:19
  26.3 0.1 fusion.20
  26.4 0.1 reshape.290
  26.5 0.1 reshape.291
  26.6 0.6 gather_fusion
  27.2 0.1 concatenate.62
  27.3 0.7 broadcast_in_dim.11
  28.0 9.7 %all-to-all-start.1 = ((f32[32,1,704]{2,1,0:T(1,128)}), f32[32,1,704]{2,1,0:T(1,128)S(1)}, u32[]{:S(2)}, u32[]{:S(2)}) async-start(f32[32,1,704]{2,1,0:T(1,128)} %broadcast_in_dim.11), calls=%async_computation.1 | async-start | bytes 196608 | tf_op jit(solution)/shard_map/all_to_all | solution.py:19
  37.7 8.3 %all-to-all-done.1 = f32[32,1,704]{2,1,0:T(1,128)S(1)} async-done(((f32[32,1,704]{2,1,0:T(1,128)}), f32[32,1,704]{2,1,0:T(1,128)S(1)}, u32[]{:S(2)}, u32[]{:S(2)}) %all-to-all-start.1) | async-done | bytes 90144 | tf_op jit(solution)/shard_map/all_to_all | solution.py:19
  46.1 0.1 slice_reduce_fusion.4
  46.2 0.1 slice.194
  46.3 0.1 slice.196
  46.4 0.1 select_maximum_fusion.2
  46.5 0.6 pad_maximum_fusion.targ_ref
  47.1 0.6 broadcast_select_fusion.src_ref
  47.7 25.7 %shard_map.85 = f32[16,128]{1,0:T(8,128)} custom-call(s32[4,32]{1,0:T(4,128)} %len_ref.1, f32[16384]{0:T(1024)} %broadcast_select_fusion.src_ref, f32[6,16,128]{2,1,0:T(8,128)} %pad_maximum_fusion.targ_ref), custom_call_target="tpu_custom_call" | custom-call | tf_op jit(solution)/shard_map/pallas_call | solution.py:73
  73.4 0.7 slice.238
  74.1 0.8 fusion.21
  74.8 0.8 %slice_bitcast_fusion.4 = (f32[8,1]{0,1:T(1,128)S(1)}, f32[8,1]{0,1:T(1,128)S(1)}) fusion(f32[16,128]{1,0:T(8,128)} %shard_map.85), kind=kLoop, calls=%fused_computation.87 | loop fusion | bytes 128 | tf_op jit(solution)/shard_map/broadcast_in_dim;squeeze | solution.py:161
  75.7 0.1 slice.203
  75.8 0.1 slice.205
  75.9 0.1 pad_maximum_fusion.9
  76.0 0.1 fusion.1
  76.1 0.1 fusion.11
  76.1 0.1 copy.22
  76.2 0.1 fusion.12
  76.3 0.1 copy.23
  76.4 0.1 fusion.2
  76.5 0.0 copy-done.3
  76.5 0.1 add_subtract_fusion
  76.6 0.1 fusion.6
  76.7 0.6 fusion.8
  (36 shorter events, 0.3 us)
Async XLA Ops:
  1.4 0.7 copy-start
  2.2 0.7 copy-start.1
  2.2 0.7 copy-start.2
  3.7 22.5 %all-to-all-start = ((f32[16,1,3072]{2,1,0:T(1,128)}), f32[16,1,3072]{2,1,0:T(1,128)S(1)}, u32[]{:S(2)}, u32[]{:S(2)}) async-start(f32[16,1,3072]{2,1,0:T(1,128)} %broadcast_in_dim.9), calls=%async_computation | async-start | bytes 393216 | tf_op jit(solution)/shard_map/all_to_all | solution.py:19
  17.3 0.7 copy-start.5
  18.2 0.7 copy-start.4
  28.0 18.1 %all-to-all-start.1 = ((f32[32,1,704]{2,1,0:T(1,128)}), f32[32,1,704]{2,1,0:T(1,128)S(1)}, u32[]{:S(2)}, u32[]{:S(2)}) async-start(f32[32,1,704]{2,1,0:T(1,128)} %broadcast_in_dim.11), calls=%async_computation.1 | async-start | bytes 196608 | tf_op jit(solution)/shard_map/all_to_all | solution.py:19
  74.1 2.4 %copy-start.3 = (f32[8,128]{1,0:T(8,128)}, f32[8,128]{1,0:T(8,128)S(1)}, u32[]{:S(2)}) copy-start(f32[8,128]{1,0:T(8,128)S(1)} %slice.238) | copy-start | bytes 12292

commit v6 on v3

--- a/solution.py
+++ b/solution.py
@@ -9,7 +9,7 @@
 
 ROUNDS = 4
 SC = 32
-CHUNK = 8
+BLOCK = 16
 
 EPS2 = 0.05
 
@@ -26,10 +26,10 @@
     return jnp.where(ok, chunk, jnp.zeros_like(chunk))
 
 
-def velocity_kernel(len_ref, src_ref, targ_ref, out_ref):
+def velocity_kernel(idx_ref, src_ref, targ_ref, out_ref):
     tx, ty, tz = targ_ref[0], targ_ref[1], targ_ref[2]
     nx, ny, nz = targ_ref[3], targ_ref[4], targ_ref[5]
-    per_column = ROUNDS * SC * 4
+    total = idx_ref[idx_ref.shape[0] - 1]
 
     def term(at, acc):
         sx = src_ref[at]
@@ -44,26 +44,29 @@
         r = lax.rsqrt(dist2)
         return acc + (q * numer) * (r * r * r)
 
-    acc = jnp.zeros(out_ref.shape, jnp.float32)
-    for step in range(ROUNDS):
+    def block(b, acc):
+        first = b * BLOCK
+        for u in range(BLOCK):
+            acc = term(idx_ref[first + u] * 4, acc)
+        return acc
 
-        def column(c, acc, step=step):
-            chunks = (len_ref[step, c] + (CHUNK - 1)) // CHUNK
-            start = c * per_column + step * SC * 4
-
-            def chunk(j, acc):
-                base = start + j * (CHUNK * 4)
-                for u in range(CHUNK):
-                    acc = term(base + 4 * u, acc)
-                return acc
-
-            return lax.fori_loop(0, chunks, chunk, acc)
-
-        acc = lax.fori_loop(0, len_ref.shape[1], column, acc)
-    out_ref[...] = acc
+    blocks = (total + (BLOCK - 1)) // BLOCK
+    out_ref[...] = lax.fori_loop(0, blocks, block, jnp.zeros(out_ref.shape, jnp.float32))
 
 
-def velocity(group_len, src, targ):
+def live_slots(group_len, slots):
+    lengths = group_len.T.reshape(-1)
+    ends = jnp.cumsum(lengths)
+    at = jnp.arange(slots, dtype=jnp.int32)
+    passed = ends[None, :] <= at[:, None]
+    segment = jnp.sum(passed.astype(jnp.int32), axis=1)
+    before = jnp.sum(jnp.where(passed, lengths[None, :], 0), axis=1)
+    total = ends[-1]
+    idx = jnp.where(at < total, segment * SC + (at - before), slots)
+    return jnp.concatenate([idx, total[None]])
+
+
+def velocity(idx, src, targ):
     return pl.pallas_call(
         velocity_kernel,
         out_shape=jax.ShapeDtypeStruct(targ.shape[1:], jnp.float32),
@@ -73,7 +76,7 @@
             pl.BlockSpec(memory_space=pltpu.VMEM),
         ],
         out_specs=pl.BlockSpec(memory_space=pltpu.VMEM),
-    )(group_len, src, targ)
+    )(idx, src, targ)
 
 
 def tendency(ext, vel):
@@ -131,10 +134,8 @@
         target_geom[:, :, 0].reshape(-1), target_geom[:, :, -1].reshape(-1),
     ])
     got = copy_for_each(payload, "eval")
-    all_src = got[:, :n_src].reshape(n_eval, ROUNDS, width * 4)
-    lane = jnp.arange(width * 4, dtype=jnp.int32)
-    keep = ((lane % 4) != 3)[None, None, :] | ((lane // 4)[None, None, :] < group_len.T[:, :, None])
-    all_src = jnp.where(keep, all_src, 0.0).reshape(-1)
+    all_src = jnp.concatenate([got[:, :n_src].reshape(-1), jnp.zeros((4,), jnp.float32)])
+    idx = live_slots(group_len, n_eval * ROUNDS * width)
     rim = 2 * (rows_here + 4) * 2
     left = from_peer(got[:, n_src:], column, -1, n_eval)
     right = from_peer(got[:, n_src:], column, 1, n_eval)
@@ -148,7 +149,7 @@
     sides = jnp.pad(sides, ((0, 0), (0, cols_here - 2 * rows_here)))
     halo = jnp.stack([t_above, t_below, sides], axis=1)
     halo = jnp.pad(halo, ((0, 0), (0, rows_here - 3), (0, 0)))
-    vel_all = velocity(group_len, all_src, jnp.concatenate([target_geom, halo], axis=1))
+    vel_all = velocity(idx, all_src, jnp.concatenate([target_geom, halo], axis=1))
     vel_main = vel_all[:rows_here]
     vel_up = vel_all[rows_here:rows_here + 1]
     vel_down = vel_all[rows_here + 1:rows_here + 2]

time: 77.3 us -> 73 us (0.944)
  Pallas kernels: 25 us -> 19.6 us
  other arithmetic: 2.82 us -> 6.18 us
  waiting for transfers between devices: 15.4 us -> 12.7 us
    pallas_call x1, Pallas kernels: 25 us -> 19.6 us  [velocity(): pl.pallas_call(velocity_kernel, out_shape=jax.ShapeDtypeStruct(targ.shape...]
    all_to_all x2, waiting for transfers between devices: 15.4 us -> 12.7 us  [copy_for_each(): lax.all_to_all(jnp.broadcast_to(x[None], (peers, *x.shape)), axis, 0, 0,...]
    unnamed x20, local copies, waits for them, and re-layouts: 2.78 us -> 0.72 us
    concatenate x0 -> x1, other arithmetic: none -> 1.25 us  [live_slots(): return jnp.concatenate([idx, total[None]])]
    reduce_sum x0 -> x1, other arithmetic: none -> 1.15 us  [live_slots(): segment = jnp.sum(passed.astype(jnp.int32), axis=1)]
    slice x1, local copies, waits for them, and re-layouts: 0.01 us -> 0.82 us  [body(): target_geom[:, -1:].reshape(-1)]
  transfers between devices with their start and end apart: 2 -> 2, of which waited for: 2 -> 2; matrix products, arithmetic and copies ran while one was open for 1% -> 6% of each run, Pallas kernels for 0% -> 0%
where the time goes in v6:
time: 73 us; the launch traced here: 72.3 us
  starting transfers between devices  23.3 us (32%)
  Pallas kernels  19.6 us (27%)
  waiting for transfers between devices  12.7 us (17%)
  local copies, waits for them, and re-layouts  9.46 us (13%)
  other arithmetic  6.18 us (8%)
  between operations  0.97 us (1%)
    all_to_all x2, starting transfers between devices, copy_for_each(): lax.all_to_all(jnp.broadcast_to(x[None], (peers, *x.shape)), axis, 0, 0,...  23.3 us
    pallas_call x1, Pallas kernels, velocity(): pl.pallas_call(velocity_kernel, out_shape=jax.ShapeDtypeStruct(targ.shape...  19.6 us
    all_to_all x2, waiting for transfers between devices, copy_for_each(): lax.all_to_all(jnp.broadcast_to(x[None], (peers, *x.shape)), axis, 0, 0,...  12.7 us
  transfers between devices with their start and end apart: 2, of which 2 were waited for; matrix products, arithmetic and copies ran while one was open for 6% of the time, Pallas kernels for 0%

profile of v6, /device:TPU:1, one launch (start us, length us, event | category | flops | bytes accessed | tf_op | source)
XLA Modules:
  0.0 72.3 jit_solution(10369897528969433112)
XLA Ops:
  0.6 0.8 %copy.33 = f32[4,32,4]{2,1,0:T(8,128)S(1)} copy(f32[4,32,4]{1,2,0:T(4,128)} %bitcast.79) | data formatting | bytes 4096 | tf_op jit(solution)/shard_map/transpose | solution.py:115
  1.4 0.1 reshape.264
  1.5 0.8 %fusion.18 = (f32[6,1,128]{2,1,0:T(1,128)S(1)}, f32[6,1,128]{2,1,0:T(1,128)S(1)}) fusion(f32[6,8,128]{2,1,0:T(8,128)} %param.6), kind=kLoop, calls=%fused_computation.90 | loop fusion | bytes 12288 | tf_op jit(solution)/shard_map/slice | solution.py:117
  2.4 0.8 %pad_maximum_fusion.12 = (f32[2,2,128]{2,1,0:T(2,128)S(1)}, f32[2,2,128]{2,1,0:T(2,128)S(1)}) fusion(f32[1,8,128]{2,1,0:T(8,128)} %bitcast.65, f32[1,8,128]{2,1,0:T(8,128)} %bitcast.69), kind=kLoop, calls=%fused_computation.67 | loop fusion | flops 1024 | bytes 12288 | tf_op jit(solution)/shard_map/stack | solution.py:112
  3.2 0.8 %broadcast_in_dim.43 = f32[16,1,3072]{2,1,0:T(1,128)} broadcast(f32[3072]{0:T(1024)S(1)} %constant_dynamic-update-slice_fusion), dimensions={2} | broadcast | bytes 208896 | tf_op jit(solution)/shard_map/broadcast_in_dim | solution.py:19
  4.0 13.5 %all-to-all-start = ((f32[16,1,3072]{2,1,0:T(1,128)}), f32[16,1,3072]{2,1,0:T(1,128)S(1)}, u32[]{:S(2)}, u32[]{:S(2)}) async-start(f32[16,1,3072]{2,1,0:T(1,128)} %broadcast_in_dim.43), calls=%async_computation | async-start | bytes 393216 | tf_op jit(solution)/shard_map/all_to_all | solution.py:19
  17.6 0.1 slice_reduce_fusion
  17.7 0.1 copy.30
  17.8 0.1 reshape.285
  17.9 0.1 broadcast_in_dim.24
  18.0 0.2 reduce-window.4
  18.2 0.1 reduce
  18.3 0.5 slice.232
  18.8 1.2 %convert_reduce_fusion = (s32[4096]{0:T(1024)S(1)}, s32[4096]{0:T(1024)S(1)}) fusion(s32[128]{0:T(128)S(1)} %reduce, s32[128]{0:T(128)S(1)} %broadcast_in_dim.24), kind=kLoop, calls=%fused_computation.2 | loop fusion | flops 2613248 | bytes 33792 | tf_op jit(solution)/shard_map/reduce_sum | solution.py:62
  20.0 0.7 add_select_fusion
  20.7 0.1 reshape_squeeze.6
  20.8 0.1 reshape_squeeze.7
  20.8 1.3 %pad_add_fusion.idx_ref = s32[4097]{0:T(1024)} fusion(s32[1]{0:T(128)} %bitcast.2, s32[4096]{0:T(1024)S(1)} %add_select_fusion), kind=kLoop, calls=%fused_computation.28 | loop fusion | flops 4097 | bytes 32776 | tf_op jit(solution)/shard_map/concatenate | solution.py:66
  22.2 4.4 %all-to-all-done = f32[16,1,3072]{2,1,0:T(1,128)S(1)} async-done(((f32[16,1,3072]{2,1,0:T(1,128)}), f32[16,1,3072]{2,1,0:T(1,128)S(1)}, u32[]{:S(2)}, u32[]{:S(2)}) %all-to-all-start) | async-done | bytes 196640 | tf_op jit(solution)/shard_map/all_to_all | solution.py:19
  26.7 0.6 copy-done.1
  27.4 0.1 reshape.271
  27.5 0.1 reshape.272
  27.6 0.6 gather_fusion
  28.2 0.1 concatenate.69
  28.3 0.7 broadcast_in_dim.45
  28.9 9.7 %all-to-all-start.1 = ((f32[32,1,704]{2,1,0:T(1,128)}), f32[32,1,704]{2,1,0:T(1,128)S(1)}, u32[]{:S(2)}, u32[]{:S(2)}) async-start(f32[32,1,704]{2,1,0:T(1,128)} %broadcast_in_dim.45), calls=%async_computation.1 | async-start | bytes 196608 | tf_op jit(solution)/shard_map/all_to_all | solution.py:19
  38.7 8.3 %all-to-all-done.1 = f32[32,1,704]{2,1,0:T(1,128)S(1)} async-done(((f32[32,1,704]{2,1,0:T(1,128)}), f32[32,1,704]{2,1,0:T(1,128)S(1)}, u32[]{:S(2)}, u32[]{:S(2)}) %all-to-all-start.1) | async-done | bytes 90144 | tf_op jit(solution)/shard_map/all_to_all | solution.py:19
  47.1 0.1 slice_reduce_fusion.4
  47.2 0.1 slice.202
  47.3 0.1 slice.204
  47.3 0.1 select_maximum_fusion.2
  47.5 0.6 pad_maximum_fusion.targ_ref
  48.1 0.6 concatenate.70.src_ref
  48.7 19.6 %shard_map.85 = f32[16,128]{1,0:T(8,128)} custom-call(s32[4097]{0:T(1024)} %pad_add_fusion.idx_ref, f32[16388]{0:T(1024)} %concatenate.70.src_ref, f32[6,16,128]{2,1,0:T(8,128)} %pad_maximum_fusion.targ_ref), custom_call_target="tpu_custom_call" | custom-call | tf_op jit(solution)/shard_map/pallas_call | solution.py:70
  68.4 0.7 slice.247
  69.0 0.8 %fusion.20 = (f32[1,128]{1,0:T(1,128)S(1)}, f32[1,128]{1,0:T(1,128)S(1)}) fusion(f32[16,128]{1,0:T(8,128)} %shard_map.85), kind=kLoop, calls=%fused_computation.92 | loop fusion | bytes 2048 | tf_op jit(solution)/shard_map/slice | solution.py:154
  69.8 0.8 %slice_bitcast_fusion.4 = (f32[8,1]{0,1:T(1,128)S(1)}, f32[8,1]{0,1:T(1,128)S(1)}) fusion(f32[16,128]{1,0:T(8,128)} %shard_map.85), kind=kLoop, calls=%fused_computation.86 | loop fusion | bytes 128 | tf_op jit(solution)/shard_map/broadcast_in_dim;squeeze | solution.py:156
  70.6 0.1 slice.211
  70.7 0.1 slice.213
  70.8 0.1 pad_maximum_fusion.9
  70.9 0.1 fusion.1
  71.0 0.1 fusion.11
  71.1 0.1 copy.36
  71.3 0.1 copy.37
  71.4 0.1 fusion.2
  71.5 0.1 add_subtract_fusion
  71.6 0.1 fusion.6
  71.6 0.6 fusion.8
  (41 shorter events, 0.5 us)
Async XLA Ops:
  4.0 13.6 %copy-start = (f32[6,8,128]{2,1,0:T(8,128)S(1)}, f32[6,8,128]{2,1,0:T(8,128)}, u32[]{:S(2)}) copy-start(f32[6,8,128]{2,1,0:T(8,128)} %param.6) | copy-start | bytes 73732
  4.0 13.7 %copy-start.4 = (s32[4,32]{1,0:T(4,128)S(1)}, s32[4,32]{1,0:T(4,128)}, u32[]{:S(2)}) copy-start(s32[4,32]{1,0:T(4,128)} %param.10) | copy-start | bytes 1540
  4.0 22.6 %all-to-all-start = ((f32[16,1,3072]{2,1,0:T(1,128)}), f32[16,1,3072]{2,1,0:T(1,128)S(1)}, u32[]{:S(2)}, u32[]{:S(2)}) async-start(f32[16,1,3072]{2,1,0:T(1,128)} %broadcast_in_dim.43), calls=%async_computation | async-start | bytes 393216 | tf_op jit(solution)/shard_map/all_to_all | solution.py:19
  17.5 1.3 %copy-start.5 = (s32[16]{0:T(128)S(1)}, s32[16]{0:T(128)}, u32[]{:S(2)}) copy-start(s32[16]{0:T(128)} %param.11) | copy-start | bytes 196
  26.6 0.7 copy-start.1
  26.6 0.7 copy-start.2
  28.9 18.1 %all-to-all-start.1 = ((f32[32,1,704]{2,1,0:T(1,128)}), f32[32,1,704]{2,1,0:T(1,128)S(1)}, u32[]{:S(2)}, u32[]{:S(2)}) async-start(f32[32,1,704]{2,1,0:T(1,128)} %broadcast_in_dim.45), calls=%async_computation.1 | async-start | bytes 196608 | tf_op jit(solution)/shard_map/all_to_all | solution.py:19
  69.0 2.5 %copy-start.3 = (f32[8,128]{1,0:T(8,128)}, f32[8,128]{1,0:T(8,128)S(1)}, u32[]{:S(2)}) copy-start(f32[8,128]{1,0:T(8,128)S(1)} %slice.247) | copy-start | bytes 12292

commit v7 on v6

--- a/solution.py
+++ b/solution.py
@@ -26,16 +26,21 @@
     return jnp.where(ok, chunk, jnp.zeros_like(chunk))
 
 
-def velocity_kernel(idx_ref, src_ref, targ_ref, out_ref):
-    tx, ty, tz = targ_ref[0], targ_ref[1], targ_ref[2]
-    nx, ny, nz = targ_ref[3], targ_ref[4], targ_ref[5]
+def velocity_kernel(idx_ref, src_ref, main_ref, halo_ref, out_main_ref, out_halo_ref):
+    tx = jnp.concatenate([main_ref[0], halo_ref[0]])
+    ty = jnp.concatenate([main_ref[1], halo_ref[1]])
+    tz = jnp.concatenate([main_ref[2], halo_ref[2]])
+    nx = jnp.concatenate([main_ref[3], halo_ref[3]])
+    ny = jnp.concatenate([main_ref[4], halo_ref[4]])
+    nz = jnp.concatenate([main_ref[5], halo_ref[5]])
     total = idx_ref[idx_ref.shape[0] - 1]
+    rows = main_ref.shape[1]
 
     def term(at, acc):
         sx = src_ref[at]
-        sy = src_ref[at + 1]
-        sz = src_ref[at + 2]
-        q = src_ref[at + 3]
+        sy = src_ref[at + SC]
+        sz = src_ref[at + 2 * SC]
+        q = src_ref[at + 3 * SC]
         dx = tx - sx
         dy = ty - sy
         dz = tz - sz
@@ -47,11 +52,13 @@
     def block(b, acc):
         first = b * BLOCK
         for u in range(BLOCK):
-            acc = term(idx_ref[first + u] * 4, acc)
+            acc = term(idx_ref[first + u], acc)
         return acc
 
     blocks = (total + (BLOCK - 1)) // BLOCK
-    out_ref[...] = lax.fori_loop(0, blocks, block, jnp.zeros(out_ref.shape, jnp.float32))
+    acc = lax.fori_loop(0, blocks, block, jnp.zeros((2 * rows, main_ref.shape[2]), jnp.float32))
+    out_main_ref[...] = acc[:rows]
+    out_halo_ref[...] = acc[rows:]
 
 
 def live_slots(group_len, slots):
@@ -62,21 +69,23 @@
     segment = jnp.sum(passed.astype(jnp.int32), axis=1)
     before = jnp.sum(jnp.where(passed, lengths[None, :], 0), axis=1)
     total = ends[-1]
-    idx = jnp.where(at < total, segment * SC + (at - before), slots)
+    idx = jnp.where(at < total, segment * (4 * SC) + (at - before), slots * 4)
     return jnp.concatenate([idx, total[None]])
 
 
-def velocity(idx, src, targ):
+def velocity(idx, src, main, halo):
+    block = jax.ShapeDtypeStruct(main.shape[1:], jnp.float32)
     return pl.pallas_call(
         velocity_kernel,
-        out_shape=jax.ShapeDtypeStruct(targ.shape[1:], jnp.float32),
+        out_shape=(block, block),
         in_specs=[
             pl.BlockSpec(memory_space=pltpu.SMEM),
             pl.BlockSpec(memory_space=pltpu.SMEM),
             pl.BlockSpec(memory_space=pltpu.VMEM),
+            pl.BlockSpec(memory_space=pltpu.VMEM),
         ],
-        out_specs=pl.BlockSpec(memory_space=pltpu.VMEM),
-    )(idx, src, targ)
+        out_specs=(pl.BlockSpec(memory_space=pltpu.VMEM), pl.BlockSpec(memory_space=pltpu.VMEM)),
+    )(idx, src, main, halo)
 
 
 def tendency(ext, vel):
@@ -112,7 +121,7 @@
     fields = jnp.stack([eta, phi])
     n_src = ROUNDS * 4 * width
     payload = jnp.concatenate([
-        jnp.swapaxes(sources[0], 1, 2).reshape(-1),
+        sources[0].reshape(-1),
         fields[:, :2].reshape(-1), fields[:, -2:].reshape(-1),
         target_geom[:, :1].reshape(-1), target_geom[:, -1:].reshape(-1),
     ])
@@ -134,7 +143,7 @@
         target_geom[:, :, 0].reshape(-1), target_geom[:, :, -1].reshape(-1),
     ])
     got = copy_for_each(payload, "eval")
-    all_src = jnp.concatenate([got[:, :n_src].reshape(-1), jnp.zeros((4,), jnp.float32)])
+    all_src = jnp.concatenate([got[:, :n_src].reshape(-1), jnp.zeros((4 * SC,), jnp.float32)])
     idx = live_slots(group_len, n_eval * ROUNDS * width)
     rim = 2 * (rows_here + 4) * 2
     left = from_peer(got[:, n_src:], column, -1, n_eval)
@@ -149,12 +158,11 @@
     sides = jnp.pad(sides, ((0, 0), (0, cols_here - 2 * rows_here)))
     halo = jnp.stack([t_above, t_below, sides], axis=1)
     halo = jnp.pad(halo, ((0, 0), (0, rows_here - 3), (0, 0)))
-    vel_all = velocity(idx, all_src, jnp.concatenate([target_geom, halo], axis=1))
-    vel_main = vel_all[:rows_here]
-    vel_up = vel_all[rows_here:rows_here + 1]
-    vel_down = vel_all[rows_here + 1:rows_here + 2]
-    vel_left = vel_all[rows_here + 2, :rows_here][:, None]
-    vel_right = vel_all[rows_here + 2, rows_here:2 * rows_here][:, None]
+    vel_main, vel_halo = velocity(idx, all_src, target_geom, halo)
+    vel_up = vel_halo[0:1]
+    vel_down = vel_halo[1:2]
+    vel_left = vel_halo[2, :rows_here][:, None]
+    vel_right = vel_halo[2, rows_here:2 * rows_here][:, None]
 
     vel_rows = jnp.concatenate([vel_up, vel_main, vel_down], axis=0)
     corner = jnp.zeros((1, 1), jnp.float32)

time: 73 us -> 72 us (0.986)
  local copies, waits for them, and re-layouts: 9.46 us -> 8.68 us
    transpose x1 -> x0, local copies, waits for them, and re-layouts: 0.8 us -> none  [body(): jnp.swapaxes(sources[0], 1, 2).reshape(-1)]
    another operation x1 -> x2, local copies, waits for them, and re-layouts: 0.83 us -> 1.61 us  [the longest x1 0.83 us: body(): vel_left = vel_halo[2, :rows_here][:, None]]
where the time goes in v7:
time: 72 us; the launch traced here: 71.4 us
  starting transfers between devices  23.3 us (32%)
  Pallas kernels  19.6 us (27%)
  waiting for transfers between devices  12.7 us (18%)
  local copies, waits for them, and re-layouts  8.68 us (12%)
  other arithmetic  6.17 us (9%)
  between operations  0.96 us (1%)
    all_to_all x2, starting transfers between devices, copy_for_each(): lax.all_to_all(jnp.broadcast_to(x[None], (peers, *x.shape)), axis, 0, 0,...  23.3 us
    pallas_call x1, Pallas kernels, velocity(): pl.pallas_call(velocity_kernel, out_shape=(block, block), in_specs=[pl.Bl...  19.6 us
    all_to_all x2, waiting for transfers between devices, copy_for_each(): lax.all_to_all(jnp.broadcast_to(x[None], (peers, *x.shape)), axis, 0, 0,...  12.7 us
    broadcast_in_dim x2, local copies, waits for them, and re-layouts, copy_for_each(): jnp.broadcast_to(x[None], (peers, *x.shape))  1.45 us
  transfers between devices with their start and end apart: 2, of which 2 were waited for; matrix products, arithmetic and copies ran while one was open for 6% of the time, Pallas kernels for 0%

profile of v7, /device:TPU:1, one launch (start us, length us, event | category | flops | bytes accessed | tf_op | source)
XLA Modules:
  0.0 71.4 jit_solution(11333447612613698300)
XLA Ops:
  0.6 0.8 %reshape_squeeze.9 = f32[512]{0:T(512)S(1)} reshape(f32[1,4,4,32]{3,2,1,0:T(4,128)} %param.9) | data formatting | bytes 4096 | tf_op jit(solution)/shard_map/reshape;squeeze | solution.py:124
  1.4 0.8 %fusion.18 = (f32[6,1,128]{2,1,0:T(1,128)S(1)}, f32[6,1,128]{2,1,0:T(1,128)S(1)}) fusion(f32[6,8,128]{2,1,0:T(8,128)} %main_ref.1), kind=kLoop, calls=%fused_computation.89 | loop fusion | bytes 12288 | tf_op jit(solution)/shard_map/slice | solution.py:126
  2.2 0.8 %pad_maximum_fusion.11 = (f32[2,2,128]{2,1,0:T(2,128)S(1)}, f32[2,2,128]{2,1,0:T(2,128)S(1)}) fusion(f32[1,8,128]{2,1,0:T(8,128)} %bitcast.62, f32[1,8,128]{2,1,0:T(8,128)} %bitcast.66), kind=kLoop, calls=%fused_computation.66 | loop fusion | flops 1024 | bytes 12288 | tf_op jit(solution)/shard_map/stack | solution.py:121
  3.1 0.8 %broadcast_in_dim.44 = f32[16,1,3072]{2,1,0:T(1,128)} broadcast(f32[3072]{0:T(1024)S(1)} %constant_dynamic-update-slice_fusion), dimensions={2} | broadcast | bytes 208896 | tf_op jit(solution)/shard_map/broadcast_in_dim | solution.py:19
  3.8 13.5 %all-to-all-start = ((f32[16,1,3072]{2,1,0:T(1,128)}), f32[16,1,3072]{2,1,0:T(1,128)S(1)}, u32[]{:S(2)}, u32[]{:S(2)}) async-start(f32[16,1,3072]{2,1,0:T(1,128)} %broadcast_in_dim.44), calls=%async_computation | async-start | bytes 393216 | tf_op jit(solution)/shard_map/all_to_all | solution.py:19
  17.4 0.1 slice_reduce_fusion
  17.6 0.1 copy.28
  17.7 0.1 reshape.281
  17.8 0.1 broadcast_in_dim.24
  17.9 0.2 reduce-window.4
  18.0 0.1 reduce
  18.1 0.5 slice.228
  18.7 1.2 %convert_reduce_fusion = (s32[4096]{0:T(1024)S(1)}, s32[4096]{0:T(1024)S(1)}) fusion(s32[128]{0:T(128)S(1)} %reduce, s32[128]{0:T(128)S(1)} %broadcast_in_dim.24), kind=kLoop, calls=%fused_computation.2 | loop fusion | flops 2613248 | bytes 33792 | tf_op jit(solution)/shard_map/reduce_sum | solution.py:69
  19.9 0.7 add_select_fusion
  20.6 0.1 reshape_squeeze.10
  20.6 0.1 reshape_squeeze.11
  20.7 1.3 %pad_add_fusion.idx_ref = s32[4097]{0:T(1024)} fusion(s32[1]{0:T(128)} %bitcast.2, s32[4096]{0:T(1024)S(1)} %add_select_fusion), kind=kLoop, calls=%fused_computation.27 | loop fusion | flops 4097 | bytes 32776 | tf_op jit(solution)/shard_map/concatenate | solution.py:73
  22.0 4.4 %all-to-all-done = f32[16,1,3072]{2,1,0:T(1,128)S(1)} async-done(((f32[16,1,3072]{2,1,0:T(1,128)}), f32[16,1,3072]{2,1,0:T(1,128)S(1)}, u32[]{:S(2)}, u32[]{:S(2)}) %all-to-all-start) | async-done | bytes 196640 | tf_op jit(solution)/shard_map/all_to_all | solution.py:19
  26.6 0.6 copy-done.1
  27.2 0.1 fusion.19
  27.3 0.1 reshape.267
  27.4 0.1 reshape.268
  27.5 0.6 gather_fusion
  28.1 0.1 concatenate.66
  28.1 0.7 broadcast_in_dim.46
  28.8 9.7 %all-to-all-start.1 = ((f32[32,1,704]{2,1,0:T(1,128)}), f32[32,1,704]{2,1,0:T(1,128)S(1)}, u32[]{:S(2)}, u32[]{:S(2)}) async-start(f32[32,1,704]{2,1,0:T(1,128)} %broadcast_in_dim.46), calls=%async_computation.1 | async-start | bytes 196608 | tf_op jit(solution)/shard_map/all_to_all | solution.py:19
  38.6 8.3 %all-to-all-done.1 = f32[32,1,704]{2,1,0:T(1,128)S(1)} async-done(((f32[32,1,704]{2,1,0:T(1,128)}), f32[32,1,704]{2,1,0:T(1,128)S(1)}, u32[]{:S(2)}, u32[]{:S(2)}) %all-to-all-start.1) | async-done | bytes 90144 | tf_op jit(solution)/shard_map/all_to_all | solution.py:19
  47.0 0.1 slice_reduce_fusion.4
  47.1 0.1 slice.199
  47.1 0.1 slice.201
  47.2 0.1 select_maximum_fusion.2
  47.3 0.6 concatenate.67.src_ref
  48.0 0.6 select_maximum_fusion.halo_ref
  48.6 19.6 %shard_map.85 = (f32[8,128]{1,0:T(8,128)}, f32[8,128]{1,0:T(8,128)}) custom-call(s32[4097]{0:T(1024)} %pad_add_fusion.idx_ref, f32[16512]{0:T(1024)} %concatenate.67.src_ref, f32[6,8,128]{2,1,0:T(8,128)} %main_ref.1, f32[6,8,128]{2,1,0:T(8,128)} %select_maximum_fusion.halo_ref), custom_call_target="tpu_custom_call" | custom-call | tf_op jit(solution)/shard_map/pallas_call | solution.py:78
  68.1 0.8 %fusion.20 = (f32[1,128]{1,0:T(1,128)S(1)}, f32[1,128]{1,0:T(1,128)S(1)}) fusion(f32[8,128]{1,0:T(8,128)} %get-tuple-element.5), kind=kLoop, calls=%fused_computation.91 | loop fusion | bytes 2048 | tf_op jit(solution)/shard_map/slice | solution.py:162
  68.9 0.8 %slice_bitcast_fusion.4 = (f32[8,1]{0,1:T(1,128)S(1)}, f32[8,1]{0,1:T(1,128)S(1)}) fusion(f32[8,128]{1,0:T(8,128)} %get-tuple-element.5), kind=kLoop, calls=%fused_computation.87 | loop fusion | bytes 128 | tf_op jit(solution)/shard_map/broadcast_in_dim;squeeze | solution.py:164
  69.7 0.1 slice.207
  69.8 0.1 slice.209
  69.9 0.1 pad_maximum_fusion.8
  70.0 0.1 fusion.1
  70.1 0.1 fusion.11
  70.2 0.1 copy.33
  70.3 0.1 fusion.12
  70.4 0.1 copy.34
  70.5 0.1 fusion.2
  70.6 0.1 add_subtract_fusion
  70.7 0.1 fusion.6
  70.8 0.6 fusion.8
  (38 shorter events, 0.4 us)
Async XLA Ops:
  3.8 13.6 %copy-start = (f32[6,8,128]{2,1,0:T(8,128)S(1)}, f32[6,8,128]{2,1,0:T(8,128)}, u32[]{:S(2)}) copy-start(f32[6,8,128]{2,1,0:T(8,128)} %main_ref.1) | copy-start | bytes 73732
  3.8 13.7 %copy-start.4 = (s32[4,32]{1,0:T(4,128)S(1)}, s32[4,32]{1,0:T(4,128)}, u32[]{:S(2)}) copy-start(s32[4,32]{1,0:T(4,128)} %param.10) | copy-start | bytes 1540
  3.8 22.6 %all-to-all-start = ((f32[16,1,3072]{2,1,0:T(1,128)}), f32[16,1,3072]{2,1,0:T(1,128)S(1)}, u32[]{:S(2)}, u32[]{:S(2)}) async-start(f32[16,1,3072]{2,1,0:T(1,128)} %broadcast_in_dim.44), calls=%async_computation | async-start | bytes 393216 | tf_op jit(solution)/shard_map/all_to_all | solution.py:19
  17.4 1.3 %copy-start.5 = (s32[16]{0:T(128)S(1)}, s32[16]{0:T(128)}, u32[]{:S(2)}) copy-start(s32[16]{0:T(128)} %param.11) | copy-start | bytes 196
  26.5 0.7 copy-start.1
  26.5 0.7 copy-start.2
  28.8 18.1 %all-to-all-start.1 = ((f32[32,1,704]{2,1,0:T(1,128)}), f32[32,1,704]{2,1,0:T(1,128)S(1)}, u32[]{:S(2)}, u32[]{:S(2)}) async-start(f32[32,1,704]{2,1,0:T(1,128)} %broadcast_in_dim.46), calls=%async_computation.1 | async-start | bytes 196608 | tf_op jit(solution)/shard_map/all_to_all | solution.py:19
  68.1 2.4 %copy-start.3 = (f32[8,128]{1,0:T(8,128)S(1)}, f32[8,128]{1,0:T(8,128)}, u32[]{:S(2)}) copy-start(f32[8,128]{1,0:T(8,128)} %get-tuple-element.4) | copy-start | bytes 12292

commit v8 on v7

--- a/solution.py
+++ b/solution.py
@@ -121,20 +121,20 @@
     fields = jnp.stack([eta, phi])
     n_src = ROUNDS * 4 * width
     payload = jnp.concatenate([
-        sources[0].reshape(-1),
-        fields[:, :2].reshape(-1), fields[:, -2:].reshape(-1),
-        target_geom[:, :1].reshape(-1), target_geom[:, -1:].reshape(-1),
+        jnp.pad(sources[0].reshape(ROUNDS * 4, width), ((0, 0), (0, cols_here - width))),
+        fields[:, :2].reshape(4, cols_here), fields[:, -2:].reshape(4, cols_here),
+        target_geom[:, 0], target_geom[:, -1],
     ])
     got = copy_for_each(payload, "tile")
-    src_rows = got[:, :n_src].reshape(n_tile, ROUNDS, width * 4)
+    src_rows = got[:, :ROUNDS * 4, :width].reshape(n_tile, ROUNDS, 4 * width)
     stacked = src_rows[owner, jnp.arange(ROUNDS)]
-    rim = 2 * cols_here * 2
-    above = from_peer(got[:, n_src:], row, -1, n_tile)
-    below = from_peer(got[:, n_src:], row, 1, n_tile)
-    f_above = above[rim:2 * rim].reshape(2, 2, cols_here)
-    f_below = below[:rim].reshape(2, 2, cols_here)
-    t_above = above[2 * rim + 6 * cols_here:].reshape(6, cols_here)
-    t_below = below[2 * rim:2 * rim + 6 * cols_here].reshape(6, cols_here)
+    above = from_peer(got, row, -1, n_tile)
+    below = from_peer(got, row, 1, n_tile)
+    top = ROUNDS * 4
+    f_above = above[top + 4:top + 8].reshape(2, 2, cols_here)
+    f_below = below[top:top + 4].reshape(2, 2, cols_here)
+    t_above = above[top + 14:top + 20]
+    t_below = below[top + 8:top + 14]
     ext_rows = jnp.concatenate([f_above, fields, f_below], axis=1)
 
     payload = jnp.concatenate([

time: 72 us -> 73.8 us (1.025)
  waiting for transfers between devices: 12.7 us -> 15.1 us
    all_to_all x2, waiting for transfers between devices: 12.7 us -> 15.1 us  [copy_for_each(): lax.all_to_all(jnp.broadcast_to(x[None], (peers, *x.shape)), axis, 0, 0,...]
    another operation x1 -> x0, local copies, waits for them, and re-layouts: 0.78 us -> none  [body(): sources[0].reshape(-1)]
where the time goes in v8:
time: 73.8 us; the launch traced here: 73.2 us
  starting transfers between devices  23.3 us (32%)
  Pallas kernels  19.6 us (27%)
  waiting for transfers between devices  15.1 us (20%)
  local copies, waits for them, and re-layouts  8.08 us (11%)
  other arithmetic  6.19 us (8%)
  between operations  0.92 us (1%)
    all_to_all x2, starting transfers between devices, copy_for_each(): lax.all_to_all(jnp.broadcast_to(x[None], (peers, *x.shape)), axis, 0, 0,...  23.3 us
    pallas_call x1, Pallas kernels, velocity(): pl.pallas_call(velocity_kernel, out_shape=(block, block), in_specs=[pl.Bl...  19.6 us
    all_to_all x2, waiting for transfers between devices, copy_for_each(): lax.all_to_all(jnp.broadcast_to(x[None], (peers, *x.shape)), axis, 0, 0,...  15.1 us
  transfers between devices with their start and end apart: 2, of which 2 were waited for; matrix products, arithmetic and copies ran while one was open for 6% of the time, Pallas kernels for 0%

profile of v8, /device:TPU:1, one launch (start us, length us, event | category | flops | bytes accessed | tf_op | source)
XLA Modules:
  0.0 73.2 jit_solution(6206240863687066383)
XLA Ops:
  0.6 0.8 %fusion.18 = (f32[6,1,128]{2,1,0:T(1,128)S(1)}, f32[6,1,128]{2,1,0:T(1,128)S(1)}) fusion(f32[6,8,128]{2,1,0:T(8,128)} %main_ref.1), kind=kLoop, calls=%fused_computation.85 | loop fusion | bytes 12288 | tf_op jit(solution)/shard_map/slice | solution.py:126
  1.5 0.8 %pad_maximum_fusion.11 = (f32[2,2,128]{2,1,0:T(2,128)S(1)}, f32[2,2,128]{2,1,0:T(2,128)S(1)}) fusion(f32[1,8,128]{2,1,0:T(8,128)} %bitcast.56, f32[1,8,128]{2,1,0:T(8,128)} %bitcast.60), kind=kLoop, calls=%fused_computation.60 | loop fusion | flops 1024 | bytes 12288 | tf_op jit(solution)/shard_map/stack | solution.py:121
  2.2 0.7 pad.13
  2.9 0.1 concatenate.63
  3.0 0.7 %broadcast_in_dim.44 = f32[16,36,128]{2,1,0:T(8,128)} broadcast(f32[36,128]{1,0:T(8,128)S(1)} %concatenate.63), dimensions={1,2} | broadcast | bytes 313344 | tf_op jit(solution)/shard_map/broadcast_in_dim | solution.py:19
  3.8 13.5 %all-to-all-start = ((f32[16,36,128]{2,1,0:T(8,128)}), f32[16,36,128]{2,1,0:T(8,128)S(1)}, u32[]{:S(2)}, u32[]{:S(2)}) async-start(f32[16,36,128]{2,1,0:T(8,128)} %broadcast_in_dim.44), calls=%async_computation | async-start | bytes 655360 | tf_op jit(solution)/shard_map/all_to_all | solution.py:19
  17.4 0.1 slice_reduce_fusion
  17.5 0.1 copy.31
  17.7 0.1 broadcast_in_dim.24
  17.8 0.2 reduce-window.4
  18.0 0.1 reduce
  18.1 0.5 slice.207
  18.6 0.1 reshape_squeeze.10
  18.7 0.1 reshape_squeeze.11
  18.8 1.2 %convert_reduce_fusion = (s32[4096]{0:T(1024)S(1)}, s32[4096]{0:T(1024)S(1)}) fusion(s32[128]{0:T(128)S(1)} %reduce, s32[128]{0:T(128)S(1)} %broadcast_in_dim.24), kind=kLoop, calls=%fused_computation.2 | loop fusion | flops 2613248 | bytes 33792 | tf_op jit(solution)/shard_map/reduce_sum | solution.py:69
  20.0 0.7 add_select_fusion
  20.6 1.3 %pad_add_fusion.idx_ref = s32[4097]{0:T(1024)} fusion(s32[1]{0:T(128)} %bitcast.2, s32[4096]{0:T(1024)S(1)} %add_select_fusion), kind=kLoop, calls=%fused_computation.28 | loop fusion | flops 4097 | bytes 32776 | tf_op jit(solution)/shard_map/concatenate | solution.py:73
  21.9 0.1 and_convert_fusion
  22.0 6.7 %all-to-all-done = f32[16,36,128]{2,1,0:T(8,128)S(1)} async-done(((f32[16,36,128]{2,1,0:T(8,128)}), f32[16,36,128]{2,1,0:T(8,128)S(1)}, u32[]{:S(2)}, u32[]{:S(2)}) %all-to-all-start) | async-done | bytes 294944 | tf_op jit(solution)/shard_map/all_to_all | solution.py:19
  28.9 0.1 reshape.232
  29.0 0.1 reshape.233
  29.1 0.1 reshape.228
  29.2 0.6 gather_fusion
  29.8 0.1 concatenate.66
  29.9 0.7 broadcast_in_dim.46
  30.5 9.8 %all-to-all-start.1 = ((f32[32,1,704]{2,1,0:T(1,128)}), f32[32,1,704]{2,1,0:T(1,128)S(1)}, u32[]{:S(2)}, u32[]{:S(2)}) async-start(f32[32,1,704]{2,1,0:T(1,128)} %broadcast_in_dim.46), calls=%async_computation.1 | async-start | bytes 196608 | tf_op jit(solution)/shard_map/all_to_all | solution.py:19
  40.3 8.3 %all-to-all-done.1 = f32[32,1,704]{2,1,0:T(1,128)S(1)} async-done(((f32[32,1,704]{2,1,0:T(1,128)}), f32[32,1,704]{2,1,0:T(1,128)S(1)}, u32[]{:S(2)}, u32[]{:S(2)}) %all-to-all-start.1) | async-done | bytes 90144 | tf_op jit(solution)/shard_map/all_to_all | solution.py:19
  48.8 0.1 slice_reduce_fusion.4
  48.8 0.1 slice.178
  48.9 0.1 slice.180
  49.0 0.1 select_maximum_fusion.2
  49.1 0.6 concatenate.67.src_ref
  49.7 0.6 select_maximum_fusion.halo_ref
  50.4 19.6 %shard_map.85 = (f32[8,128]{1,0:T(8,128)}, f32[8,128]{1,0:T(8,128)}) custom-call(s32[4097]{0:T(1024)} %pad_add_fusion.idx_ref, f32[16512]{0:T(1024)} %concatenate.67.src_ref, f32[6,8,128]{2,1,0:T(8,128)} %main_ref.1, f32[6,8,128]{2,1,0:T(8,128)} %select_maximum_fusion.halo_ref), custom_call_target="tpu_custom_call" | custom-call | tf_op jit(solution)/shard_map/pallas_call | solution.py:78
  69.9 0.8 %fusion.20 = (f32[1,128]{1,0:T(1,128)S(1)}, f32[1,128]{1,0:T(1,128)S(1)}) fusion(f32[8,128]{1,0:T(8,128)} %get-tuple-element.5), kind=kLoop, calls=%fused_computation.87 | loop fusion | bytes 2048 | tf_op jit(solution)/shard_map/slice | solution.py:162
  70.7 0.8 %slice_bitcast_fusion.4 = (f32[8,1]{0,1:T(1,128)S(1)}, f32[8,1]{0,1:T(1,128)S(1)}) fusion(f32[8,128]{1,0:T(8,128)} %get-tuple-element.5), kind=kLoop, calls=%fused_computation.83 | loop fusion | bytes 128 | tf_op jit(solution)/shard_map/broadcast_in_dim;squeeze | solution.py:164
  71.5 0.1 slice.186
  71.6 0.1 slice.188
  71.7 0.1 pad_maximum_fusion.8
  71.8 0.1 fusion.1
  71.9 0.1 fusion.11
  72.0 0.1 copy.38
  72.1 0.1 fusion.12
  72.2 0.1 copy.39
  72.3 0.1 fusion.2
  72.4 0.1 add_subtract_fusion
  72.5 0.1 fusion.6
  72.6 0.6 fusion.8
  (35 shorter events, 0.4 us)
Async XLA Ops:
  3.8 13.6 %copy-start = (f32[6,8,128]{2,1,0:T(8,128)S(1)}, f32[6,8,128]{2,1,0:T(8,128)}, u32[]{:S(2)}) copy-start(f32[6,8,128]{2,1,0:T(8,128)} %main_ref.1) | copy-start | bytes 73732
  3.8 13.7 %copy-start.4 = (s32[4,32]{1,0:T(4,128)S(1)}, s32[4,32]{1,0:T(4,128)}, u32[]{:S(2)}) copy-start(s32[4,32]{1,0:T(4,128)} %param.10) | copy-start | bytes 1540
  3.8 24.9 %all-to-all-start = ((f32[16,36,128]{2,1,0:T(8,128)}), f32[16,36,128]{2,1,0:T(8,128)S(1)}, u32[]{:S(2)}, u32[]{:S(2)}) async-start(f32[16,36,128]{2,1,0:T(8,128)} %broadcast_in_dim.44), calls=%async_computation | async-start | bytes 655360 | tf_op jit(solution)/shard_map/all_to_all | solution.py:19
  17.3 4.6 %copy-start.5 = (s32[16]{0:T(128)S(1)}, s32[16]{0:T(128)}, u32[]{:S(2)}) copy-start(s32[16]{0:T(128)} %param.11) | copy-start | bytes 196
  17.6 11.2 %copy-start.1 = (f32[8,128]{1,0:T(8,128)S(1)}, f32[8,128]{1,0:T(8,128)}, u32[]{:S(2)}) copy-start(f32[8,128]{1,0:T(8,128)} %param.8) | copy-start | bytes 12292
  17.6 11.2 %copy-start.2 = (f32[8,128]{1,0:T(8,128)S(1)}, f32[8,128]{1,0:T(8,128)}, u32[]{:S(2)}) copy-start(f32[8,128]{1,0:T(8,128)} %param.7) | copy-start | bytes 12292
  30.5 18.1 %all-to-all-start.1 = ((f32[32,1,704]{2,1,0:T(1,128)}), f32[32,1,704]{2,1,0:T(1,128)S(1)}, u32[]{:S(2)}, u32[]{:S(2)}) async-start(f32[32,1,704]{2,1,0:T(1,128)} %broadcast_in_dim.46), calls=%async_computation.1 | async-start | bytes 196608 | tf_op jit(solution)/shard_map/all_to_all | solution.py:19
  69.9 2.4 %copy-start.3 = (f32[8,128]{1,0:T(8,128)S(1)}, f32[8,128]{1,0:T(8,128)}, u32[]{:S(2)}) copy-start(f32[8,128]{1,0:T(8,128)} %get-tuple-element.4) | copy-start | bytes 12292

commit v9 on v7

--- a/solution.py
+++ b/solution.py
@@ -119,39 +119,45 @@
     owner = owner[:ROUNDS]
 
     fields = jnp.stack([eta, phi])
+    mine = (owner == row).astype(jnp.float32)
+    own_block = jnp.sum(mine[:, None, None] * sources[0], axis=0).reshape(-1)
+    top = jnp.concatenate([fields[:, :2].reshape(-1), target_geom[:, 0].reshape(-1)])
+    bottom = jnp.concatenate([fields[:, -2:].reshape(-1), target_geom[:, -1].reshape(-1)])
+    to_above = (jnp.arange(n_tile, dtype=jnp.int32) == row - 1)[:, None]
+    payload = jnp.concatenate([
+        jnp.broadcast_to(own_block[None], (n_tile, own_block.shape[0])),
+        jnp.where(to_above, top[None], bottom[None]),
+    ], axis=1)
+    got = lax.all_to_all(payload, "tile", 0, 0, tiled=True)
+    n_own = own_block.shape[0]
+    stacked = got[owner, :n_own]
+    rim = 2 * cols_here * 2
+    above = from_peer(got[:, n_own:], row, -1, n_tile)
+    below = from_peer(got[:, n_own:], row, 1, n_tile)
+    f_above = above[:rim].reshape(2, 2, cols_here)
+    f_below = below[:rim].reshape(2, 2, cols_here)
+    t_above = above[rim:].reshape(6, cols_here)
+    t_below = below[rim:].reshape(6, cols_here)
+    ext_rows = jnp.concatenate([f_above, fields, f_below], axis=1)
+
     n_src = ROUNDS * 4 * width
+    left_rim = jnp.concatenate([ext_rows[:, :, :2].reshape(-1), target_geom[:, :, 0].reshape(-1)])
+    right_rim = jnp.concatenate([ext_rows[:, :, -2:].reshape(-1), target_geom[:, :, -1].reshape(-1)])
+    to_left = (jnp.arange(n_eval, dtype=jnp.int32) == column - 1)[:, None]
     payload = jnp.concatenate([
-        sources[0].reshape(-1),
-        fields[:, :2].reshape(-1), fields[:, -2:].reshape(-1),
-        target_geom[:, :1].reshape(-1), target_geom[:, -1:].reshape(-1),
-    ])
-    got = copy_for_each(payload, "tile")
-    src_rows = got[:, :n_src].reshape(n_tile, ROUNDS, width * 4)
-    stacked = src_rows[owner, jnp.arange(ROUNDS)]
-    rim = 2 * cols_here * 2
-    above = from_peer(got[:, n_src:], row, -1, n_tile)
-    below = from_peer(got[:, n_src:], row, 1, n_tile)
-    f_above = above[rim:2 * rim].reshape(2, 2, cols_here)
-    f_below = below[:rim].reshape(2, 2, cols_here)
-    t_above = above[2 * rim + 6 * cols_here:].reshape(6, cols_here)
-    t_below = below[2 * rim:2 * rim + 6 * cols_here].reshape(6, cols_here)
-    ext_rows = jnp.concatenate([f_above, fields, f_below], axis=1)
-
-    payload = jnp.concatenate([
-        stacked.reshape(-1),
-        ext_rows[:, :, :2].reshape(-1), ext_rows[:, :, -2:].reshape(-1),
-        target_geom[:, :, 0].reshape(-1), target_geom[:, :, -1].reshape(-1),
-    ])
-    got = copy_for_each(payload, "eval")
+        jnp.broadcast_to(stacked.reshape(-1)[None], (n_eval, n_src)),
+        jnp.where(to_left, left_rim[None], right_rim[None]),
+    ], axis=1)
+    got = lax.all_to_all(payload, "eval", 0, 0, tiled=True)
     all_src = jnp.concatenate([got[:, :n_src].reshape(-1), jnp.zeros((4 * SC,), jnp.float32)])
     idx = live_slots(group_len, n_eval * ROUNDS * width)
     rim = 2 * (rows_here + 4) * 2
     left = from_peer(got[:, n_src:], column, -1, n_eval)
     right = from_peer(got[:, n_src:], column, 1, n_eval)
-    f_left = left[rim:2 * rim].reshape(2, rows_here + 4, 2)
+    f_left = left[:rim].reshape(2, rows_here + 4, 2)
     f_right = right[:rim].reshape(2, rows_here + 4, 2)
-    t_left = left[2 * rim + 6 * rows_here:].reshape(6, rows_here)
-    t_right = right[2 * rim:2 * rim + 6 * rows_here].reshape(6, rows_here)
+    t_left = left[rim:].reshape(6, rows_here)
+    t_right = right[rim:].reshape(6, rows_here)
     ext = jnp.concatenate([f_left, ext_rows, f_right], axis=2)
 
     sides = jnp.concatenate([t_left, t_right], axis=1)

time: 72 us -> 79.3 us (1.10)
  local copies, waits for them, and re-layouts: 8.68 us -> 15.1 us
  other arithmetic: 6.17 us -> 7.96 us
    gather x1 -> x16, local copies, waits for them, and re-layouts: 0.58 us -> 7.98 us  [body(): stacked = src_rows[owner, jnp.arange(ROUNDS)]]
    all_to_all x0 -> x2, local copies, waits for them, and re-layouts: none -> 1.36 us  [the longest x1 0.69 us: body(): got = lax.all_to_all(payload, 'tile', 0, 0, tiled=True)]
    broadcast_in_dim x2 -> x1, local copies, waits for them, and re-layouts: 1.45 us -> 0.09 us  [body(): jnp.broadcast_to(own_block[None], (n_tile, own_block.shape[0]))]
where the time goes in v9:
time: 79.3 us; the launch traced here: 78.6 us
  starting transfers between devices  22.8 us (29%)
  Pallas kernels  19.6 us (25%)
  local copies, waits for them, and re-layouts  15.1 us (19%)
  waiting for transfers between devices  12.1 us (15%)
  other arithmetic  7.96 us (10%)
  between operations  0.98 us (1%)
    pallas_call x1, Pallas kernels, velocity(): pl.pallas_call(velocity_kernel, out_shape=(block, block), in_specs=[pl.Bl...  19.6 us
    all_to_all x1, starting transfers between devices, body(): got = lax.all_to_all(payload, 'tile', 0, 0, tiled=True)  13.5 us
    all_to_all x1, starting transfers between devices, body(): got = lax.all_to_all(payload, 'eval', 0, 0, tiled=True)  9.29 us
    all_to_all x1, waiting for transfers between devices, body(): got = lax.all_to_all(payload, 'eval', 0, 0, tiled=True)  8.21 us
    gather x16, local copies, waits for them, and re-layouts  7.98 us
    all_to_all x1, waiting for transfers between devices, body(): got = lax.all_to_all(payload, 'tile', 0, 0, tiled=True)  3.86 us
  transfers between devices with their start and end apart: 2, of which 2 were waited for; matrix products, arithmetic and copies ran while one was open for 6% of the time, Pallas kernels for 0%

profile of v9, /device:TPU:1, one launch (start us, length us, event | category | flops | bytes accessed | tf_op | source)
XLA Modules:
  0.0 78.6 jit_solution(12852040641983024495)
XLA Ops:
  0.6 0.7 compare_convert_fusion
  1.3 0.8 fusion.7
  2.1 0.1 reshape.305
  2.2 0.8 %fusion.16 = (f32[6,1,128]{2,1,0:T(1,128)S(1)}, f32[6,1,128]{2,1,0:T(1,128)S(1)}) fusion(f32[6,8,128]{2,1,0:T(8,128)} %main_ref.1), kind=kLoop, calls=%fused_computation.96 | loop fusion | bytes 12288 | tf_op jit(solution)/shard_map/slice | solution.py:124
  3.0 0.8 pad_maximum_fusion.16
  3.9 0.7 all_to_all.16
  4.6 13.5 %all-to-all-start = ((f32[16,1,1408]{2,1,0:T(1,128)}), f32[16,1,1408]{2,1,0:T(1,128)S(1)}, u32[]{:S(2)}, u32[]{:S(2)}) async-start(f32[16,1,1408]{2,1,0:T(1,128)} %all_to_all.16), calls=%async_computation | async-start | bytes 180224 | tf_op jit(solution)/shard_map/all_to_all | solution.py:131
  18.2 0.1 slice_reduce_fusion.1
  18.4 0.5 copy-done.4
  18.8 0.1 copy.28
  18.9 0.1 broadcast_in_dim.96
  19.1 0.2 reduce-window.4
  19.3 0.5 slice.232
  19.8 0.1 reduce
  20.1 1.2 %convert_reduce_fusion = (s32[4096]{0:T(1024)S(1)}, s32[4096]{0:T(1024)S(1)}) fusion(s32[128]{0:T(128)S(1)} %reduce, s32[128]{0:T(128)S(1)} %broadcast_in_dim.96), kind=kLoop, calls=%fused_computation.2 | loop fusion | flops 2613248 | bytes 33792 | tf_op jit(solution)/shard_map/reduce_sum | solution.py:69
  21.3 0.7 add_select_fusion
  21.9 1.3 %pad_add_fusion.idx_ref = s32[4097]{0:T(1024)} fusion(s32[1]{0:T(128)} %bitcast.2, s32[4096]{0:T(1024)S(1)} %add_select_fusion), kind=kLoop, calls=%fused_computation.30 | loop fusion | flops 4097 | bytes 32776 | tf_op jit(solution)/shard_map/concatenate | solution.py:73
  23.3 3.9 %all-to-all-done = f32[16,1,1408]{2,1,0:T(1,128)S(1)} async-done(((f32[16,1,1408]{2,1,0:T(1,128)}), f32[16,1,1408]{2,1,0:T(1,128)S(1)}, u32[]{:S(2)}, u32[]{:S(2)}) %all-to-all-start) | async-done | bytes 90144 | tf_op jit(solution)/shard_map/all_to_all | solution.py:131
  27.2 8.0 %while.1 = (s32[]{:T(128)}, f32[16,1408]{1,0:T(8,128)S(1)}, s32[4,2]{0,1:T(2,128)S(1)}, f32[4,128]{1,0:T(4,128)S(1)}, s32[]{:T(128)}, /*index=5*/s32[]{:T(128)}) while((s32[]{:T(128)}, f32[16,1408]{1,0:T(8,128)S(1)}, s32[4,2]{0,1:T(2,128)S(1)}, f32[4,128]{1,0:T(4,128)S(1)}, s32[]{:T(128)}, /*index=5*/s32[]{:T(128)}) %tuple.42), condition=%wide.while_cond, body=%wide.while_body.sunk | while | flops 2 | bytes 2169 | solution.py:133
  27.3 0.5 fusion.20
  27.8 1.4 %dynamic-slice.7 = f32[1,128]{1,0:T(1,128)S(1)} dynamic-slice(f32[16,1408]{1,0:T(8,128)S(1)} %get-tuple-element.97, s32[]{:T(128)} %bitcast.57, s32[]{:T(128)} %bitcast.58), dynamic_slice_sizes={1,128} | dynamic-slice | bytes 1028 | tf_op jit(solution)/shard_map/gather
  29.3 0.5 fusion.20
  29.8 1.4 %dynamic-slice.7 = f32[1,128]{1,0:T(1,128)S(1)} dynamic-slice(f32[16,1408]{1,0:T(8,128)S(1)} %get-tuple-element.97, s32[]{:T(128)} %bitcast.57, s32[]{:T(128)} %bitcast.58), dynamic_slice_sizes={1,128} | dynamic-slice | bytes 1028 | tf_op jit(solution)/shard_map/gather
  31.3 0.5 fusion.20
  31.8 1.4 %dynamic-slice.7 = f32[1,128]{1,0:T(1,128)S(1)} dynamic-slice(f32[16,1408]{1,0:T(8,128)S(1)} %get-tuple-element.97, s32[]{:T(128)} %bitcast.57, s32[]{:T(128)} %bitcast.58), dynamic_slice_sizes={1,128} | dynamic-slice | bytes 1028 | tf_op jit(solution)/shard_map/gather
  33.3 0.5 fusion.20
  33.8 1.4 %dynamic-slice.7 = f32[1,128]{1,0:T(1,128)S(1)} dynamic-slice(f32[16,1408]{1,0:T(8,128)S(1)} %get-tuple-element.97, s32[]{:T(128)} %bitcast.57, s32[]{:T(128)} %bitcast.58), dynamic_slice_sizes={1,128} | dynamic-slice | bytes 1028 | tf_op jit(solution)/shard_map/gather
  35.3 0.1 reshape.258
  35.4 0.1 reshape.259
  35.8 0.7 all_to_all.19
  36.5 9.3 %all-to-all-start.1 = ((f32[32,1,608]{2,1,0:T(1,128)}), f32[32,1,608]{2,1,0:T(1,128)S(1)}, u32[]{:S(2)}, u32[]{:S(2)}) async-start(f32[32,1,608]{2,1,0:T(1,128)} %all_to_all.19), calls=%async_computation.1 | async-start | bytes 163840 | tf_op jit(solution)/shard_map/all_to_all | solution.py:151
  45.8 8.2 %all-to-all-done.1 = f32[32,1,608]{2,1,0:T(1,128)S(1)} async-done(((f32[32,1,608]{2,1,0:T(1,128)}), f32[32,1,608]{2,1,0:T(1,128)S(1)}, u32[]{:S(2)}, u32[]{:S(2)}) %all-to-all-start.1) | async-done | bytes 77856 | tf_op jit(solution)/shard_map/all_to_all | solution.py:151
  54.1 0.1 slice_reduce_fusion.4
  54.4 0.6 concatenate.83.src_ref
  55.0 0.6 select_maximum_fusion.halo_ref
  55.6 19.6 %shard_map.85 = (f32[8,128]{1,0:T(8,128)}, f32[8,128]{1,0:T(8,128)}) custom-call(s32[4097]{0:T(1024)} %pad_add_fusion.idx_ref, f32[16512]{0:T(1024)} %concatenate.83.src_ref, f32[6,8,128]{2,1,0:T(8,128)} %main_ref.1, f32[6,8,128]{2,1,0:T(8,128)} %select_maximum_fusion.halo_ref), custom_call_target="tpu_custom_call" | custom-call | tf_op jit(solution)/shard_map/pallas_call | solution.py:78
  75.2 0.8 fusion.18
  76.0 0.8 %slice_bitcast_fusion.4 = (f32[8,1]{0,1:T(1,128)S(1)}, f32[8,1]{0,1:T(1,128)S(1)}) fusion(f32[8,128]{1,0:T(8,128)} %get-tuple-element.5), kind=kLoop, calls=%fused_computation.90 | loop fusion | bytes 128 | tf_op jit(solution)/shard_map/broadcast_in_dim;squeeze | solution.py:170
  76.8 0.1 slice.205
  76.9 0.1 slice.203
  77.0 0.1 pad_maximum_fusion.10
  77.1 0.1 fusion.1
  77.3 0.1 copy.34
  77.4 0.1 copy.33
  77.5 0.1 fusion.2
  77.6 0.1 copy-done.3
  77.8 0.1 add_subtract_fusion
  78.0 0.6 fusion.9
  (63 shorter events, 1.8 us)
Async XLA Ops:
  4.6 13.6 %copy-start.5 = (s32[16]{0:T(128)S(1)}, s32[16]{0:T(128)}, u32[]{:S(2)}) copy-start(s32[16]{0:T(128)} %param.11) | copy-start | bytes 196
  4.6 13.6 %copy-start = (f32[6,8,128]{2,1,0:T(8,128)S(1)}, f32[6,8,128]{2,1,0:T(8,128)}, u32[]{:S(2)}) copy-start(f32[6,8,128]{2,1,0:T(8,128)} %main_ref.1) | copy-start | bytes 73732
  4.6 22.6 %all-to-all-start = ((f32[16,1,1408]{2,1,0:T(1,128)}), f32[16,1,1408]{2,1,0:T(1,128)S(1)}, u32[]{:S(2)}, u32[]{:S(2)}) async-start(f32[16,1,1408]{2,1,0:T(1,128)} %all_to_all.16), calls=%async_computation | async-start | bytes 180224 | tf_op jit(solution)/shard_map/all_to_all | solution.py:131
  18.1 0.7 copy-start.4
  27.2 8.1 %copy-start.1 = (f32[8,128]{1,0:T(8,128)S(1)}, f32[8,128]{1,0:T(8,128)}, u32[]{:S(2)}) copy-start(f32[8,128]{1,0:T(8,128)} %param.8) | copy-start | bytes 12292
  27.2 8.1 %copy-start.2 = (f32[8,128]{1,0:T(8,128)S(1)}, f32[8,128]{1,0:T(8,128)}, u32[]{:S(2)}) copy-start(f32[8,128]{1,0:T(8,128)} %param.7) | copy-start | bytes 12292
  36.5 17.5 %all-to-all-start.1 = ((f32[32,1,608]{2,1,0:T(1,128)}), f32[32,1,608]{2,1,0:T(1,128)S(1)}, u32[]{:S(2)}, u32[]{:S(2)}) async-start(f32[32,1,608]{2,1,0:T(1,128)} %all_to_all.19), calls=%async_computation.1 | async-start | bytes 163840 | tf_op jit(solution)/shard_map/all_to_all | solution.py:151
  77.1 0.7 copy-start.3

commit v10 on v9

--- a/solution.py
+++ b/solution.py
@@ -130,7 +130,7 @@
     ], axis=1)
     got = lax.all_to_all(payload, "tile", 0, 0, tiled=True)
     n_own = own_block.shape[0]
-    stacked = got[owner, :n_own]
+    stacked = got[:, :n_own][owner]
     rim = 2 * cols_here * 2
     above = from_peer(got[:, n_own:], row, -1, n_tile)
     below = from_peer(got[:, n_own:], row, 1, n_tile)

time: 79.3 us -> 71.9 us (0.907)
  local copies, waits for them, and re-layouts: 15.1 us -> 7.77 us
    gather x16 -> x1, local copies, waits for them, and re-layouts: 7.98 us -> 0.56 us  [body(): stacked = got[:, :n_own][owner]]
where the time goes in v10:
time: 71.9 us; the launch traced here: 71.2 us
  starting transfers between devices  22.8 us (32%)
  Pallas kernels  19.6 us (27%)
  waiting for transfers between devices  12.1 us (17%)
  other arithmetic  7.97 us (11%)
  local copies, waits for them, and re-layouts  7.77 us (11%)
  between operations  0.97 us (1%)
    pallas_call x1, Pallas kernels, velocity(): pl.pallas_call(velocity_kernel, out_shape=(block, block), in_specs=[pl.Bl...  19.6 us
    all_to_all x1, starting transfers between devices, body(): got = lax.all_to_all(payload, 'tile', 0, 0, tiled=True)  13.5 us
    all_to_all x1, starting transfers between devices, body(): got = lax.all_to_all(payload, 'eval', 0, 0, tiled=True)  9.28 us
    all_to_all x1, waiting for transfers between devices, body(): got = lax.all_to_all(payload, 'eval', 0, 0, tiled=True)  8.21 us
    all_to_all x1, waiting for transfers between devices, body(): got = lax.all_to_all(payload, 'tile', 0, 0, tiled=True)  3.86 us
  transfers between devices with their start and end apart: 2, of which 2 were waited for; matrix products, arithmetic and copies ran while one was open for 6% of the time, Pallas kernels for 0%

profile of v10, /device:TPU:1, one launch (start us, length us, event | category | flops | bytes accessed | tf_op | source)
XLA Modules:
  0.0 71.2 jit_solution(14164147357427324255)
XLA Ops:
  0.6 0.7 compare_convert_fusion
  1.3 0.8 %fusion.7 = f32[4,32]{1,0:T(4,128)S(1)} fusion(f32[1,4,4,32]{3,2,1,0:T(4,128)} %param.9, f32[4]{0:T(128)S(1)} %compare_convert_fusion), kind=kLoop, calls=%fused_computation.54 | loop fusion | flops 896 | bytes 2576 | tf_op jit(solution)/shard_map/reduce_sum | solution.py:123
  2.1 0.1 reshape.295
  2.2 0.8 %fusion.14 = (f32[6,1,128]{2,1,0:T(1,128)S(1)}, f32[6,1,128]{2,1,0:T(1,128)S(1)}) fusion(f32[6,8,128]{2,1,0:T(8,128)} %main_ref.1), kind=kLoop, calls=%fused_computation.95 | loop fusion | bytes 12288 | tf_op jit(solution)/shard_map/slice | solution.py:124
  3.0 0.8 %pad_maximum_fusion.16 = (f32[2,2,128]{2,1,0:T(2,128)S(1)}, f32[2,2,128]{2,1,0:T(2,128)S(1)}) fusion(f32[1,8,128]{2,1,0:T(8,128)} %bitcast.56, f32[1,8,128]{2,1,0:T(8,128)} %bitcast.60), kind=kLoop, calls=%fused_computation.71 | loop fusion | flops 1024 | bytes 12288 | tf_op jit(solution)/shard_map/slice | solution.py:124
  3.8 0.1 broadcast_select_fusion
  3.9 0.7 all_to_all.16
  4.6 13.5 %all-to-all-start = ((f32[16,1,1408]{2,1,0:T(1,128)}), f32[16,1,1408]{2,1,0:T(1,128)S(1)}, u32[]{:S(2)}, u32[]{:S(2)}) async-start(f32[16,1,1408]{2,1,0:T(1,128)} %all_to_all.16), calls=%async_computation | async-start | bytes 180224 | tf_op jit(solution)/shard_map/all_to_all | solution.py:131
  18.2 0.1 slice_reduce_fusion.1
  18.4 0.5 copy-done.4
  18.8 0.1 copy.28
  18.9 0.1 broadcast_in_dim.96
  19.1 0.2 reduce-window.4
  19.3 0.5 slice.228
  19.8 0.1 reduce
  20.0 0.1 reshape_squeeze.14
  20.0 0.1 reshape_squeeze.15
  20.1 1.2 %convert_reduce_fusion = (s32[4096]{0:T(1024)S(1)}, s32[4096]{0:T(1024)S(1)}) fusion(s32[128]{0:T(128)S(1)} %reduce, s32[128]{0:T(128)S(1)} %broadcast_in_dim.96), kind=kLoop, calls=%fused_computation.2 | loop fusion | flops 2613248 | bytes 33792 | tf_op jit(solution)/shard_map/reduce_sum | solution.py:69
  21.3 0.7 add_select_fusion
  21.9 1.3 %pad_add_fusion.idx_ref = s32[4097]{0:T(1024)} fusion(s32[1]{0:T(128)} %bitcast.2, s32[4096]{0:T(1024)S(1)} %add_select_fusion), kind=kLoop, calls=%fused_computation.30 | loop fusion | flops 4097 | bytes 32776 | tf_op jit(solution)/shard_map/concatenate | solution.py:73
  23.3 3.9 %all-to-all-done = f32[16,1,1408]{2,1,0:T(1,128)S(1)} async-done(((f32[16,1,1408]{2,1,0:T(1,128)}), f32[16,1,1408]{2,1,0:T(1,128)S(1)}, u32[]{:S(2)}, u32[]{:S(2)}) %all-to-all-start) | async-done | bytes 90144 | tf_op jit(solution)/shard_map/all_to_all | solution.py:131
  27.2 0.6 gather_fusion
  27.9 0.1 reshape.258
  28.0 0.1 reshape.259
  28.1 0.1 pad_maximum_fusion.21
  28.4 0.7 all_to_all.19
  29.1 9.3 %all-to-all-start.1 = ((f32[32,1,608]{2,1,0:T(1,128)}), f32[32,1,608]{2,1,0:T(1,128)S(1)}, u32[]{:S(2)}, u32[]{:S(2)}) async-start(f32[32,1,608]{2,1,0:T(1,128)} %all_to_all.19), calls=%async_computation.1 | async-start | bytes 163840 | tf_op jit(solution)/shard_map/all_to_all | solution.py:151
  38.4 8.2 %all-to-all-done.1 = f32[32,1,608]{2,1,0:T(1,128)S(1)} async-done(((f32[32,1,608]{2,1,0:T(1,128)}), f32[32,1,608]{2,1,0:T(1,128)S(1)}, u32[]{:S(2)}, u32[]{:S(2)}) %all-to-all-start.1) | async-done | bytes 77856 | tf_op jit(solution)/shard_map/all_to_all | solution.py:151
  46.6 0.1 slice_reduce_fusion.4
  46.7 0.1 slice.201
  46.8 0.1 slice.199
  46.9 0.1 select_maximum_fusion.2
  47.0 0.6 concatenate.79.src_ref
  47.6 0.6 select_maximum_fusion.halo_ref
  48.2 19.6 %shard_map.85 = (f32[8,128]{1,0:T(8,128)}, f32[8,128]{1,0:T(8,128)}) custom-call(s32[4097]{0:T(1024)} %pad_add_fusion.idx_ref, f32[16512]{0:T(1024)} %concatenate.79.src_ref, f32[6,8,128]{2,1,0:T(8,128)} %main_ref.1, f32[6,8,128]{2,1,0:T(8,128)} %select_maximum_fusion.halo_ref), custom_call_target="tpu_custom_call" | custom-call | tf_op jit(solution)/shard_map/pallas_call | solution.py:78
  67.8 0.8 %fusion.16 = (f32[1,128]{1,0:T(1,128)S(1)}, f32[1,128]{1,0:T(1,128)S(1)}) fusion(f32[8,128]{1,0:T(8,128)} %get-tuple-element.5), kind=kLoop, calls=%fused_computation.97 | loop fusion | bytes 2048 | tf_op jit(solution)/shard_map/slice | solution.py:168
  68.6 0.8 %slice_bitcast_fusion.4 = (f32[8,1]{0,1:T(1,128)S(1)}, f32[8,1]{0,1:T(1,128)S(1)}) fusion(f32[8,128]{1,0:T(8,128)} %get-tuple-element.5), kind=kLoop, calls=%fused_computation.90 | loop fusion | bytes 128 | tf_op jit(solution)/shard_map/broadcast_in_dim;squeeze | solution.py:170
  69.4 0.1 slice.209
  69.5 0.1 slice.207
  69.6 0.1 pad_maximum_fusion.10
  69.7 0.1 fusion.1
  69.9 0.1 copy.34
  70.0 0.1 copy.33
  70.1 0.1 fusion.2
  70.2 0.1 copy-done.3
  70.4 0.1 add_subtract_fusion
  70.5 0.1 fusion.6
  70.6 0.6 fusion.9
  (47 shorter events, 0.8 us)
Async XLA Ops:
  4.6 13.6 %copy-start.5 = (s32[16]{0:T(128)S(1)}, s32[16]{0:T(128)}, u32[]{:S(2)}) copy-start(s32[16]{0:T(128)} %param.11) | copy-start | bytes 196
  4.6 13.6 %copy-start = (f32[6,8,128]{2,1,0:T(8,128)S(1)}, f32[6,8,128]{2,1,0:T(8,128)}, u32[]{:S(2)}) copy-start(f32[6,8,128]{2,1,0:T(8,128)} %main_ref.1) | copy-start | bytes 73732
  4.6 22.6 %all-to-all-start = ((f32[16,1,1408]{2,1,0:T(1,128)}), f32[16,1,1408]{2,1,0:T(1,128)S(1)}, u32[]{:S(2)}, u32[]{:S(2)}) async-start(f32[16,1,1408]{2,1,0:T(1,128)} %all_to_all.16), calls=%async_computation | async-start | bytes 180224 | tf_op jit(solution)/shard_map/all_to_all | solution.py:131
  18.1 0.7 copy-start.4
  27.1 0.7 copy-start.1
  27.2 0.7 copy-start.2
  29.1 17.5 %all-to-all-start.1 = ((f32[32,1,608]{2,1,0:T(1,128)}), f32[32,1,608]{2,1,0:T(1,128)S(1)}, u32[]{:S(2)}, u32[]{:S(2)}) async-start(f32[32,1,608]{2,1,0:T(1,128)} %all_to_all.19), calls=%async_computation.1 | async-start | bytes 163840 | tf_op jit(solution)/shard_map/all_to_all | solution.py:151
  69.7 0.7 copy-start.3

commit v11 on v10

--- a/solution.py
+++ b/solution.py
@@ -27,20 +27,17 @@
 
 
 def velocity_kernel(idx_ref, src_ref, main_ref, halo_ref, out_main_ref, out_halo_ref):
-    tx = jnp.concatenate([main_ref[0], halo_ref[0]])
-    ty = jnp.concatenate([main_ref[1], halo_ref[1]])
-    tz = jnp.concatenate([main_ref[2], halo_ref[2]])
-    nx = jnp.concatenate([main_ref[3], halo_ref[3]])
-    ny = jnp.concatenate([main_ref[4], halo_ref[4]])
-    nz = jnp.concatenate([main_ref[5], halo_ref[5]])
     total = idx_ref[idx_ref.shape[0] - 1]
-    rows = main_ref.shape[1]
-
-    def term(at, acc):
-        sx = src_ref[at]
-        sy = src_ref[at + SC]
-        sz = src_ref[at + 2 * SC]
-        q = src_ref[at + 3 * SC]
+    main = tuple(main_ref[k] for k in range(6))
+    halo = tuple(halo_ref[k] for k in range(6))
+    upper = lax.broadcasted_iota(jnp.int32, main[0].shape, 0) < main[0].shape[0] // 2
+
+    def load(at):
+        return src_ref[at], src_ref[at + SC], src_ref[at + 2 * SC], src_ref[at + 3 * SC]
+
+    def term(targ, src, acc):
+        tx, ty, tz, nx, ny, nz = targ
+        sx, sy, sz, q = src
         dx = tx - sx
         dy = ty - sy
         dz = tz - sz
@@ -49,16 +46,24 @@
         r = lax.rsqrt(dist2)
         return acc + (q * numer) * (r * r * r)
 
-    def block(b, acc):
+    def block(b, accs):
+        acc_m, acc_h = accs
         first = b * BLOCK
-        for u in range(BLOCK):
-            acc = term(idx_ref[first + u], acc)
-        return acc
+        for u in range(0, BLOCK, 2):
+            one = load(idx_ref[first + u])
+            two = load(idx_ref[first + u + 1])
+            acc_m = term(main, one, acc_m)
+            acc_m = term(main, two, acc_m)
+            both = tuple(jnp.where(upper, x, y) for x, y in zip(one, two))
+            acc_h = term(halo, both, acc_h)
+        return acc_m, acc_h
 
     blocks = (total + (BLOCK - 1)) // BLOCK
-    acc = lax.fori_loop(0, blocks, block, jnp.zeros((2 * rows, main_ref.shape[2]), jnp.float32))
-    out_main_ref[...] = acc[:rows]
-    out_halo_ref[...] = acc[rows:]
+    zero = jnp.zeros(main[0].shape, jnp.float32)
+    acc_m, acc_h = lax.fori_loop(0, blocks, block, (zero, zero))
+    half = acc_h.shape[0] // 2
+    out_main_ref[...] = acc_m
+    out_halo_ref[...] = acc_h[:half] + acc_h[half:]
 
 
 def live_slots(group_len, slots):
@@ -74,10 +79,10 @@
 
 
 def velocity(idx, src, main, halo):
-    block = jax.ShapeDtypeStruct(main.shape[1:], jnp.float32)
+    half = jax.ShapeDtypeStruct((halo.shape[1] // 2, halo.shape[2]), jnp.float32)
     return pl.pallas_call(
         velocity_kernel,
-        out_shape=(block, block),
+        out_shape=(jax.ShapeDtypeStruct(main.shape[1:], jnp.float32), half),
         in_specs=[
             pl.BlockSpec(memory_space=pltpu.SMEM),
             pl.BlockSpec(memory_space=pltpu.SMEM),
@@ -162,8 +167,8 @@
 
     sides = jnp.concatenate([t_left, t_right], axis=1)
     sides = jnp.pad(sides, ((0, 0), (0, cols_here - 2 * rows_here)))
-    halo = jnp.stack([t_above, t_below, sides], axis=1)
-    halo = jnp.pad(halo, ((0, 0), (0, rows_here - 3), (0, 0)))
+    halo = jnp.stack([t_above, t_below, sides, jnp.zeros_like(sides)], axis=1)
+    halo = jnp.concatenate([halo, halo], axis=1)
     vel_main, vel_halo = velocity(idx, all_src, target_geom, halo)
     vel_up = vel_halo[0:1]
     vel_down = vel_halo[1:2]

time: 71.9 us -> 69.3 us (0.964)
  Pallas kernels: 19.6 us -> 16.9 us
    pallas_call x1, Pallas kernels: 19.6 us -> 16.9 us  [velocity(): pl.pallas_call(velocity_kernel, out_shape=(jax.ShapeDtypeStruct(main.shap...]
  transfers between devices with their start and end apart: 2 -> 2, of which waited for: 2 -> 2; matrix products, arithmetic and copies ran while one was open for 6% -> 7% of each run, Pallas kernels for 0% -> 0%
where the time goes in v11:
time: 69.3 us; the launch traced here: 68.6 us
  starting transfers between devices  22.8 us (33%)
  Pallas kernels  16.9 us (24%)
  waiting for transfers between devices  12.1 us (17%)
  local copies, waits for them, and re-layouts  8.41 us (12%)
  other arithmetic  7.35 us (11%)
  between operations  0.97 us (1%)
    pallas_call x1, Pallas kernels, velocity(): pl.pallas_call(velocity_kernel, out_shape=(jax.ShapeDtypeStruct(main.shap...  16.9 us
    all_to_all x1, starting transfers between devices, body(): got = lax.all_to_all(payload, 'tile', 0, 0, tiled=True)  13.5 us
    all_to_all x1, starting transfers between devices, body(): got = lax.all_to_all(payload, 'eval', 0, 0, tiled=True)  9.28 us
    all_to_all x1, waiting for transfers between devices, body(): got = lax.all_to_all(payload, 'eval', 0, 0, tiled=True)  8.21 us
    all_to_all x1, waiting for transfers between devices, body(): got = lax.all_to_all(payload, 'tile', 0, 0, tiled=True)  3.86 us
  transfers between devices with their start and end apart: 2, of which 2 were waited for; matrix products, arithmetic and copies ran while one was open for 7% of the time, Pallas kernels for 0%

profile of v11, /device:TPU:1, one launch (start us, length us, event | category | flops | bytes accessed | tf_op | source)
XLA Modules:
  0.0 68.6 jit_solution(1568321625557158934)
XLA Ops:
  0.6 0.7 compare_convert_fusion
  1.3 0.8 %fusion.7 = f32[4,32]{1,0:T(4,128)S(1)} fusion(f32[1,4,4,32]{3,2,1,0:T(4,128)} %param.9, f32[4]{0:T(128)S(1)} %compare_convert_fusion), kind=kLoop, calls=%fused_computation.51 | loop fusion | flops 896 | bytes 2576 | tf_op jit(solution)/shard_map/reduce_sum | solution.py:128
  2.1 0.1 reshape.295
  2.2 0.8 %fusion.14 = (f32[6,1,128]{2,1,0:T(1,128)S(1)}, f32[6,1,128]{2,1,0:T(1,128)S(1)}) fusion(f32[6,8,128]{2,1,0:T(8,128)} %main_ref.1), kind=kLoop, calls=%fused_computation.92 | loop fusion | bytes 12288 | tf_op jit(solution)/shard_map/slice | solution.py:129
  3.0 0.8 %pad_maximum_fusion.16 = (f32[2,2,128]{2,1,0:T(2,128)S(1)}, f32[2,2,128]{2,1,0:T(2,128)S(1)}) fusion(f32[1,8,128]{2,1,0:T(8,128)} %bitcast.56, f32[1,8,128]{2,1,0:T(8,128)} %bitcast.60), kind=kLoop, calls=%fused_computation.68 | loop fusion | flops 1024 | bytes 12288 | tf_op jit(solution)/shard_map/slice | solution.py:129
  3.8 0.1 broadcast_select_fusion
  3.9 0.7 all_to_all.16
  4.6 13.5 %all-to-all-start = ((f32[16,1,1408]{2,1,0:T(1,128)}), f32[16,1,1408]{2,1,0:T(1,128)S(1)}, u32[]{:S(2)}, u32[]{:S(2)}) async-start(f32[16,1,1408]{2,1,0:T(1,128)} %all_to_all.16), calls=%async_computation | async-start | bytes 180224 | tf_op jit(solution)/shard_map/all_to_all | solution.py:136
  18.2 0.1 slice_reduce_fusion.1
  18.4 0.5 copy-done.4
  18.8 0.1 copy.28
  18.9 0.1 broadcast_in_dim.96
  19.1 0.2 reduce-window.4
  19.3 0.5 slice.228
  19.8 0.1 reduce
  20.0 0.1 reshape_squeeze.14
  20.0 0.1 reshape_squeeze.15
  20.1 1.2 %convert_reduce_fusion = (s32[4096]{0:T(1024)S(1)}, s32[4096]{0:T(1024)S(1)}) fusion(s32[128]{0:T(128)S(1)} %reduce, s32[128]{0:T(128)S(1)} %broadcast_in_dim.96), kind=kLoop, calls=%fused_computation.2 | loop fusion | flops 2613248 | bytes 33792 | tf_op jit(solution)/shard_map/reduce_sum | solution.py:74
  21.3 0.7 add_select_fusion
  21.9 1.3 %pad_add_fusion.idx_ref = s32[4097]{0:T(1024)} fusion(s32[1]{0:T(128)} %bitcast.2, s32[4096]{0:T(1024)S(1)} %add_select_fusion), kind=kLoop, calls=%fused_computation.27 | loop fusion | flops 4097 | bytes 32776 | tf_op jit(solution)/shard_map/concatenate | solution.py:78
  23.3 3.9 %all-to-all-done = f32[16,1,1408]{2,1,0:T(1,128)S(1)} async-done(((f32[16,1,1408]{2,1,0:T(1,128)}), f32[16,1,1408]{2,1,0:T(1,128)S(1)}, u32[]{:S(2)}, u32[]{:S(2)}) %all-to-all-start) | async-done | bytes 90144 | tf_op jit(solution)/shard_map/all_to_all | solution.py:136
  27.2 0.6 gather_fusion
  27.9 0.1 reshape.258
  28.0 0.1 reshape.259
  28.1 0.1 pad_maximum_fusion.21
  28.4 0.7 all_to_all.19
  29.1 9.3 %all-to-all-start.1 = ((f32[32,1,608]{2,1,0:T(1,128)}), f32[32,1,608]{2,1,0:T(1,128)S(1)}, u32[]{:S(2)}, u32[]{:S(2)}) async-start(f32[32,1,608]{2,1,0:T(1,128)} %all_to_all.19), calls=%async_computation.1 | async-start | bytes 163840 | tf_op jit(solution)/shard_map/all_to_all | solution.py:156
  38.4 8.2 %all-to-all-done.1 = f32[32,1,608]{2,1,0:T(1,128)S(1)} async-done(((f32[32,1,608]{2,1,0:T(1,128)}), f32[32,1,608]{2,1,0:T(1,128)S(1)}, u32[]{:S(2)}, u32[]{:S(2)}) %all-to-all-start.1) | async-done | bytes 77856 | tf_op jit(solution)/shard_map/all_to_all | solution.py:156
  46.6 0.1 slice_reduce_fusion.4
  46.7 0.1 slice.201
  46.8 0.1 slice.199
  46.9 0.1 select_maximum_fusion
  47.0 0.6 concatenate.83.src_ref
  47.6 0.6 concatenate.85.halo_ref
  48.3 16.9 %shard_map.85 = (f32[8,128]{1,0:T(8,128)}, f32[4,128]{1,0:T(4,128)}) custom-call(s32[4097]{0:T(1024)} %pad_add_fusion.idx_ref, f32[16512]{0:T(1024)} %concatenate.83.src_ref, f32[6,8,128]{2,1,0:T(8,128)} %main_ref.1, f32[6,8,128]{2,1,0:T(8,128)} %concatenate.85.halo_ref), custom_call_target="tpu_custom_call" | custom-call | tf_op jit(solution)/shard_map/pallas_call | solution.py:83
  65.2 0.8 %fusion.16 = (f32[1,128]{1,0:T(1,128)S(1)}, f32[1,128]{1,0:T(1,128)S(1)}) fusion(f32[4,128]{1,0:T(4,128)} %get-tuple-element.5), kind=kLoop, calls=%fused_computation.94 | loop fusion | bytes 2048 | tf_op jit(solution)/shard_map/slice | solution.py:173
  66.0 0.8 %slice_bitcast_fusion.4 = (f32[8,1]{0,1:T(1,128)S(1)}, f32[8,1]{0,1:T(1,128)S(1)}) fusion(f32[4,128]{1,0:T(4,128)} %get-tuple-element.5), kind=kLoop, calls=%fused_computation.87 | loop fusion | bytes 128 | tf_op jit(solution)/shard_map/broadcast_in_dim;squeeze | solution.py:175
  66.8 0.1 slice.209
  66.9 0.1 slice.207
  67.0 0.1 pad_maximum_fusion.10
  67.1 0.1 fusion.1
  67.3 0.1 copy.34
  67.4 0.1 copy.33
  67.5 0.1 fusion.2
  67.6 0.1 copy-done.3
  67.8 0.1 add_subtract_fusion
  67.9 0.1 fusion.6
  68.0 0.6 fusion.9
  (48 shorter events, 0.8 us)
Async XLA Ops:
  4.6 13.6 %copy-start.5 = (s32[16]{0:T(128)S(1)}, s32[16]{0:T(128)}, u32[]{:S(2)}) copy-start(s32[16]{0:T(128)} %param.11) | copy-start | bytes 196
  4.6 13.6 %copy-start = (f32[6,8,128]{2,1,0:T(8,128)S(1)}, f32[6,8,128]{2,1,0:T(8,128)}, u32[]{:S(2)}) copy-start(f32[6,8,128]{2,1,0:T(8,128)} %main_ref.1) | copy-start | bytes 73732
  4.6 22.6 %all-to-all-start = ((f32[16,1,1408]{2,1,0:T(1,128)}), f32[16,1,1408]{2,1,0:T(1,128)S(1)}, u32[]{:S(2)}, u32[]{:S(2)}) async-start(f32[16,1,1408]{2,1,0:T(1,128)} %all_to_all.16), calls=%async_computation | async-start | bytes 180224 | tf_op jit(solution)/shard_map/all_to_all | solution.py:136
  18.1 0.7 copy-start.4
  27.1 0.7 %copy-start.1 = (f32[8,128]{1,0:T(8,128)S(1)}, f32[8,128]{1,0:T(8,128)}, u32[]{:S(2)}) copy-start(f32[8,128]{1,0:T(8,128)} %param.8) | copy-start | bytes 12292
  27.2 0.7 %copy-start.2 = (f32[8,128]{1,0:T(8,128)S(1)}, f32[8,128]{1,0:T(8,128)}, u32[]{:S(2)}) copy-start(f32[8,128]{1,0:T(8,128)} %param.7) | copy-start | bytes 12292
  29.1 17.5 %all-to-all-start.1 = ((f32[32,1,608]{2,1,0:T(1,128)}), f32[32,1,608]{2,1,0:T(1,128)S(1)}, u32[]{:S(2)}, u32[]{:S(2)}) async-start(f32[32,1,608]{2,1,0:T(1,128)} %all_to_all.19), calls=%async_computation.1 | async-start | bytes 163840 | tf_op jit(solution)/shard_map/all_to_all | solution.py:156
  67.1 0.7 %copy-start.3 = (f32[8,128]{1,0:T(8,128)S(1)}, f32[8,128]{1,0:T(8,128)}, u32[]{:S(2)}) copy-start(f32[8,128]{1,0:T(8,128)} %get-tuple-element.4) | copy-start | bytes 12292

commit v12 on v11

--- a/solution.py
+++ b/solution.py
@@ -9,7 +9,7 @@
 
 ROUNDS = 4
 SC = 32
-BLOCK = 16
+BLOCK = 32
 
 EPS2 = 0.05
 

time: 69.3 us -> 68.2 us (0.984)
  Pallas kernels: 16.9 us -> 15.9 us
    pallas_call x1, Pallas kernels: 16.9 us -> 15.9 us  [velocity(): pl.pallas_call(velocity_kernel, out_shape=(jax.ShapeDtypeStruct(main.shap...]
where the time goes in v12:
time: 68.2 us; the launch traced here: 67.5 us
  starting transfers between devices  22.8 us (33%)
  Pallas kernels  15.9 us (23%)
  waiting for transfers between devices  12.1 us (18%)
  local copies, waits for them, and re-layouts  8.41 us (12%)
  other arithmetic  7.35 us (11%)
  between operations  0.97 us (1%)
    pallas_call x1, Pallas kernels, velocity(): pl.pallas_call(velocity_kernel, out_shape=(jax.ShapeDtypeStruct(main.shap...  15.9 us
    all_to_all x1, starting transfers between devices, body(): got = lax.all_to_all(payload, 'tile', 0, 0, tiled=True)  13.5 us
    all_to_all x1, starting transfers between devices, body(): got = lax.all_to_all(payload, 'eval', 0, 0, tiled=True)  9.28 us
    all_to_all x1, waiting for transfers between devices, body(): got = lax.all_to_all(payload, 'eval', 0, 0, tiled=True)  8.21 us
    all_to_all x1, waiting for transfers between devices, body(): got = lax.all_to_all(payload, 'tile', 0, 0, tiled=True)  3.86 us
  transfers between devices with their start and end apart: 2, of which 2 were waited for; matrix products, arithmetic and copies ran while one was open for 7% of the time, Pallas kernels for 0%

profile of v12, /device:TPU:1, one launch (start us, length us, event | category | flops | bytes accessed | tf_op | source)
XLA Modules:
  0.0 67.5 jit_solution(11684531053097289370)
XLA Ops:
  0.6 0.7 compare_convert_fusion
  1.3 0.8 %fusion.7 = f32[4,32]{1,0:T(4,128)S(1)} fusion(f32[1,4,4,32]{3,2,1,0:T(4,128)} %param.9, f32[4]{0:T(128)S(1)} %compare_convert_fusion), kind=kLoop, calls=%fused_computation.51 | loop fusion | flops 896 | bytes 2576 | tf_op jit(solution)/shard_map/reduce_sum | solution.py:128
  2.1 0.1 reshape.295
  2.2 0.8 %fusion.14 = (f32[6,1,128]{2,1,0:T(1,128)S(1)}, f32[6,1,128]{2,1,0:T(1,128)S(1)}) fusion(f32[6,8,128]{2,1,0:T(8,128)} %main_ref.1), kind=kLoop, calls=%fused_computation.92 | loop fusion | bytes 12288 | tf_op jit(solution)/shard_map/slice | solution.py:129
  3.0 0.8 %pad_maximum_fusion.16 = (f32[2,2,128]{2,1,0:T(2,128)S(1)}, f32[2,2,128]{2,1,0:T(2,128)S(1)}) fusion(f32[1,8,128]{2,1,0:T(8,128)} %bitcast.56, f32[1,8,128]{2,1,0:T(8,128)} %bitcast.60), kind=kLoop, calls=%fused_computation.68 | loop fusion | flops 1024 | bytes 12288 | tf_op jit(solution)/shard_map/slice | solution.py:129
  3.8 0.1 broadcast_select_fusion
  3.9 0.7 %all_to_all.16 = f32[16,1,1408]{2,1,0:T(1,128)} reshape(f32[16,1408]{1,0:T(8,128)S(1)} %pad_maximum_fusion) | data formatting | bytes 180224 | tf_op jit(solution)/shard_map/all_to_all | solution.py:136
  4.6 13.5 %all-to-all-start = ((f32[16,1,1408]{2,1,0:T(1,128)}), f32[16,1,1408]{2,1,0:T(1,128)S(1)}, u32[]{:S(2)}, u32[]{:S(2)}) async-start(f32[16,1,1408]{2,1,0:T(1,128)} %all_to_all.16), calls=%async_computation | async-start | bytes 180224 | tf_op jit(solution)/shard_map/all_to_all | solution.py:136
  18.2 0.1 slice_reduce_fusion.1
  18.4 0.5 copy-done.4
  18.8 0.1 copy.28
  18.9 0.1 broadcast_in_dim.96
  19.1 0.2 reduce-window.4
  19.3 0.5 slice.228
  19.8 0.1 reduce
  20.0 0.1 reshape_squeeze.14
  20.0 0.1 reshape_squeeze.15
  20.1 1.2 %convert_reduce_fusion = (s32[4096]{0:T(1024)S(1)}, s32[4096]{0:T(1024)S(1)}) fusion(s32[128]{0:T(128)S(1)} %reduce, s32[128]{0:T(128)S(1)} %broadcast_in_dim.96), kind=kLoop, calls=%fused_computation.2 | loop fusion | flops 2613248 | bytes 33792 | tf_op jit(solution)/shard_map/reduce_sum | solution.py:74
  21.3 0.7 add_select_fusion
  21.9 1.3 %pad_add_fusion.idx_ref = s32[4097]{0:T(1024)} fusion(s32[1]{0:T(128)} %bitcast.2, s32[4096]{0:T(1024)S(1)} %add_select_fusion), kind=kLoop, calls=%fused_computation.27 | loop fusion | flops 4097 | bytes 32776 | tf_op jit(solution)/shard_map/concatenate | solution.py:78
  23.3 3.9 %all-to-all-done = f32[16,1,1408]{2,1,0:T(1,128)S(1)} async-done(((f32[16,1,1408]{2,1,0:T(1,128)}), f32[16,1,1408]{2,1,0:T(1,128)S(1)}, u32[]{:S(2)}, u32[]{:S(2)}) %all-to-all-start) | async-done | bytes 90144 | tf_op jit(solution)/shard_map/all_to_all | solution.py:136
  27.2 0.6 gather_fusion
  27.9 0.1 reshape.258
  28.0 0.1 reshape.259
  28.1 0.1 pad_maximum_fusion.21
  28.4 0.7 %all_to_all.19 = f32[32,1,608]{2,1,0:T(1,128)} reshape(f32[32,608]{1,0:T(8,128)S(1)} %pad_maximum_fusion.1) | data formatting | bytes 155648 | tf_op jit(solution)/shard_map/all_to_all | solution.py:156
  29.1 9.3 %all-to-all-start.1 = ((f32[32,1,608]{2,1,0:T(1,128)}), f32[32,1,608]{2,1,0:T(1,128)S(1)}, u32[]{:S(2)}, u32[]{:S(2)}) async-start(f32[32,1,608]{2,1,0:T(1,128)} %all_to_all.19), calls=%async_computation.1 | async-start | bytes 163840 | tf_op jit(solution)/shard_map/all_to_all | solution.py:156
  38.4 8.2 %all-to-all-done.1 = f32[32,1,608]{2,1,0:T(1,128)S(1)} async-done(((f32[32,1,608]{2,1,0:T(1,128)}), f32[32,1,608]{2,1,0:T(1,128)S(1)}, u32[]{:S(2)}, u32[]{:S(2)}) %all-to-all-start.1) | async-done | bytes 77856 | tf_op jit(solution)/shard_map/all_to_all | solution.py:156
  46.6 0.1 slice_reduce_fusion.4
  46.7 0.1 slice.201
  46.8 0.1 slice.199
  46.9 0.1 select_maximum_fusion
  47.0 0.6 concatenate.83.src_ref
  47.6 0.6 concatenate.85.halo_ref
  48.3 15.9 %shard_map.85 = (f32[8,128]{1,0:T(8,128)}, f32[4,128]{1,0:T(4,128)}) custom-call(s32[4097]{0:T(1024)} %pad_add_fusion.idx_ref, f32[16512]{0:T(1024)} %concatenate.83.src_ref, f32[6,8,128]{2,1,0:T(8,128)} %main_ref.1, f32[6,8,128]{2,1,0:T(8,128)} %concatenate.85.halo_ref), custom_call_target="tpu_custom_call" | custom-call | tf_op jit(solution)/shard_map/pallas_call | solution.py:83
  64.1 0.8 %fusion.16 = (f32[1,128]{1,0:T(1,128)S(1)}, f32[1,128]{1,0:T(1,128)S(1)}) fusion(f32[4,128]{1,0:T(4,128)} %get-tuple-element.5), kind=kLoop, calls=%fused_computation.94 | loop fusion | bytes 2048 | tf_op jit(solution)/shard_map/slice | solution.py:173
  64.9 0.8 %slice_bitcast_fusion.4 = (f32[8,1]{0,1:T(1,128)S(1)}, f32[8,1]{0,1:T(1,128)S(1)}) fusion(f32[4,128]{1,0:T(4,128)} %get-tuple-element.5), kind=kLoop, calls=%fused_computation.87 | loop fusion | bytes 128 | tf_op jit(solution)/shard_map/broadcast_in_dim;squeeze | solution.py:175
  65.7 0.1 slice.209
  65.8 0.1 slice.207
  65.9 0.1 pad_maximum_fusion.10
  66.0 0.1 fusion.1
  66.3 0.1 copy.34
  66.4 0.1 copy.33
  66.4 0.1 fusion.2
  66.5 0.1 copy-done.3
  66.7 0.1 add_subtract_fusion
  66.8 0.1 fusion.6
  66.9 0.6 fusion.9
  (48 shorter events, 0.8 us)
Async XLA Ops:
  4.6 13.6 %copy-start.5 = (s32[16]{0:T(128)S(1)}, s32[16]{0:T(128)}, u32[]{:S(2)}) copy-start(s32[16]{0:T(128)} %param.11) | copy-start | bytes 196
  4.6 13.6 %copy-start = (f32[6,8,128]{2,1,0:T(8,128)S(1)}, f32[6,8,128]{2,1,0:T(8,128)}, u32[]{:S(2)}) copy-start(f32[6,8,128]{2,1,0:T(8,128)} %main_ref.1) | copy-start | bytes 73732
  4.6 22.6 %all-to-all-start = ((f32[16,1,1408]{2,1,0:T(1,128)}), f32[16,1,1408]{2,1,0:T(1,128)S(1)}, u32[]{:S(2)}, u32[]{:S(2)}) async-start(f32[16,1,1408]{2,1,0:T(1,128)} %all_to_all.16), calls=%async_computation | async-start | bytes 180224 | tf_op jit(solution)/shard_map/all_to_all | solution.py:136
  18.1 0.7 %copy-start.4 = (s32[4,32]{1,0:T(4,128)S(1)}, s32[4,32]{1,0:T(4,128)}, u32[]{:S(2)}) copy-start(s32[4,32]{1,0:T(4,128)} %param.10) | copy-start | bytes 1540
  27.1 0.7 %copy-start.1 = (f32[8,128]{1,0:T(8,128)S(1)}, f32[8,128]{1,0:T(8,128)}, u32[]{:S(2)}) copy-start(f32[8,128]{1,0:T(8,128)} %param.8) | copy-start | bytes 12292
  27.2 0.7 %copy-start.2 = (f32[8,128]{1,0:T(8,128)S(1)}, f32[8,128]{1,0:T(8,128)}, u32[]{:S(2)}) copy-start(f32[8,128]{1,0:T(8,128)} %param.7) | copy-start | bytes 12292
  29.1 17.5 %all-to-all-start.1 = ((f32[32,1,608]{2,1,0:T(1,128)}), f32[32,1,608]{2,1,0:T(1,128)S(1)}, u32[]{:S(2)}, u32[]{:S(2)}) async-start(f32[32,1,608]{2,1,0:T(1,128)} %all_to_all.19), calls=%async_computation.1 | async-start | bytes 163840 | tf_op jit(solution)/shard_map/all_to_all | solution.py:156
  66.0 0.7 %copy-start.3 = (f32[8,128]{1,0:T(8,128)S(1)}, f32[8,128]{1,0:T(8,128)}, u32[]{:S(2)}) copy-start(f32[8,128]{1,0:T(8,128)} %get-tuple-element.4) | copy-start | bytes 12292

commit v13 on v12

--- a/solution.py
+++ b/solution.py
@@ -9,7 +9,7 @@
 
 ROUNDS = 4
 SC = 32
-BLOCK = 32
+BLOCK = 64
 
 EPS2 = 0.05
 

time: 68.2 us -> 67.6 us (level)
  no operation moved by 1% of the time
where the time goes in v13:
time: 67.6 us; the launch traced here: 66.9 us
  starting transfers between devices  22.8 us (34%)
  Pallas kernels  15.3 us (23%)
  waiting for transfers between devices  12.1 us (18%)
  local copies, waits for them, and re-layouts  8.41 us (12%)
  other arithmetic  7.35 us (11%)
  between operations  0.97 us (1%)
    pallas_call x1, Pallas kernels, velocity(): pl.pallas_call(velocity_kernel, out_shape=(jax.ShapeDtypeStruct(main.shap...  15.3 us
    all_to_all x1, starting transfers between devices, body(): got = lax.all_to_all(payload, 'tile', 0, 0, tiled=True)  13.5 us
    all_to_all x1, starting transfers between devices, body(): got = lax.all_to_all(payload, 'eval', 0, 0, tiled=True)  9.28 us
    all_to_all x1, waiting for transfers between devices, body(): got = lax.all_to_all(payload, 'eval', 0, 0, tiled=True)  8.21 us
    all_to_all x1, waiting for transfers between devices, body(): got = lax.all_to_all(payload, 'tile', 0, 0, tiled=True)  3.86 us
  transfers between devices with their start and end apart: 2, of which 2 were waited for; matrix products, arithmetic and copies ran while one was open for 7% of the time, Pallas kernels for 0%

profile of v13, /device:TPU:1, one launch (start us, length us, event | category | flops | bytes accessed | tf_op | source)
XLA Modules:
  0.0 66.9 jit_solution(7068006639642317319)
XLA Ops:
  0.6 0.7 compare_convert_fusion
  1.3 0.8 %fusion.7 = f32[4,32]{1,0:T(4,128)S(1)} fusion(f32[1,4,4,32]{3,2,1,0:T(4,128)} %param.9, f32[4]{0:T(128)S(1)} %compare_convert_fusion), kind=kLoop, calls=%fused_computation.51 | loop fusion | flops 896 | bytes 2576 | tf_op jit(solution)/shard_map/reduce_sum | solution.py:128
  2.1 0.1 reshape.295
  2.2 0.8 %fusion.14 = (f32[6,1,128]{2,1,0:T(1,128)S(1)}, f32[6,1,128]{2,1,0:T(1,128)S(1)}) fusion(f32[6,8,128]{2,1,0:T(8,128)} %main_ref.1), kind=kLoop, calls=%fused_computation.92 | loop fusion | bytes 12288 | tf_op jit(solution)/shard_map/slice | solution.py:129
  3.0 0.8 %pad_maximum_fusion.16 = (f32[2,2,128]{2,1,0:T(2,128)S(1)}, f32[2,2,128]{2,1,0:T(2,128)S(1)}) fusion(f32[1,8,128]{2,1,0:T(8,128)} %bitcast.56, f32[1,8,128]{2,1,0:T(8,128)} %bitcast.60), kind=kLoop, calls=%fused_computation.68 | loop fusion | flops 1024 | bytes 12288 | tf_op jit(solution)/shard_map/slice | solution.py:129
  3.8 0.1 broadcast_select_fusion
  3.9 0.7 %all_to_all.16 = f32[16,1,1408]{2,1,0:T(1,128)} reshape(f32[16,1408]{1,0:T(8,128)S(1)} %pad_maximum_fusion) | data formatting | bytes 180224 | tf_op jit(solution)/shard_map/all_to_all | solution.py:136
  4.6 13.5 %all-to-all-start = ((f32[16,1,1408]{2,1,0:T(1,128)}), f32[16,1,1408]{2,1,0:T(1,128)S(1)}, u32[]{:S(2)}, u32[]{:S(2)}) async-start(f32[16,1,1408]{2,1,0:T(1,128)} %all_to_all.16), calls=%async_computation | async-start | bytes 180224 | tf_op jit(solution)/shard_map/all_to_all | solution.py:136
  18.2 0.1 slice_reduce_fusion.1
  18.4 0.5 copy-done.4
  18.8 0.1 copy.28
  18.9 0.1 broadcast_in_dim.96
  19.1 0.2 reduce-window.4
  19.3 0.5 slice.228
  19.8 0.1 reduce
  20.0 0.1 reshape_squeeze.14
  20.0 0.1 reshape_squeeze.15
  20.1 1.2 %convert_reduce_fusion = (s32[4096]{0:T(1024)S(1)}, s32[4096]{0:T(1024)S(1)}) fusion(s32[128]{0:T(128)S(1)} %reduce, s32[128]{0:T(128)S(1)} %broadcast_in_dim.96), kind=kLoop, calls=%fused_computation.2 | loop fusion | flops 2613248 | bytes 33792 | tf_op jit(solution)/shard_map/reduce_sum | solution.py:74
  21.3 0.7 add_select_fusion
  21.9 1.3 %pad_add_fusion.idx_ref = s32[4097]{0:T(1024)} fusion(s32[1]{0:T(128)} %bitcast.2, s32[4096]{0:T(1024)S(1)} %add_select_fusion), kind=kLoop, calls=%fused_computation.27 | loop fusion | flops 4097 | bytes 32776 | tf_op jit(solution)/shard_map/concatenate | solution.py:78
  23.3 3.9 %all-to-all-done = f32[16,1,1408]{2,1,0:T(1,128)S(1)} async-done(((f32[16,1,1408]{2,1,0:T(1,128)}), f32[16,1,1408]{2,1,0:T(1,128)S(1)}, u32[]{:S(2)}, u32[]{:S(2)}) %all-to-all-start) | async-done | bytes 90144 | tf_op jit(solution)/shard_map/all_to_all | solution.py:136
  27.2 0.6 gather_fusion
  27.9 0.1 reshape.258
  28.0 0.1 reshape.259
  28.1 0.1 pad_maximum_fusion.21
  28.4 0.7 %all_to_all.19 = f32[32,1,608]{2,1,0:T(1,128)} reshape(f32[32,608]{1,0:T(8,128)S(1)} %pad_maximum_fusion.1) | data formatting | bytes 155648 | tf_op jit(solution)/shard_map/all_to_all | solution.py:156
  29.1 9.3 %all-to-all-start.1 = ((f32[32,1,608]{2,1,0:T(1,128)}), f32[32,1,608]{2,1,0:T(1,128)S(1)}, u32[]{:S(2)}, u32[]{:S(2)}) async-start(f32[32,1,608]{2,1,0:T(1,128)} %all_to_all.19), calls=%async_computation.1 | async-start | bytes 163840 | tf_op jit(solution)/shard_map/all_to_all | solution.py:156
  38.4 8.2 %all-to-all-done.1 = f32[32,1,608]{2,1,0:T(1,128)S(1)} async-done(((f32[32,1,608]{2,1,0:T(1,128)}), f32[32,1,608]{2,1,0:T(1,128)S(1)}, u32[]{:S(2)}, u32[]{:S(2)}) %all-to-all-start.1) | async-done | bytes 77856 | tf_op jit(solution)/shard_map/all_to_all | solution.py:156
  46.6 0.1 slice_reduce_fusion.4
  46.7 0.1 slice.201
  46.8 0.1 slice.199
  46.9 0.1 select_maximum_fusion
  47.0 0.6 concatenate.83.src_ref
  47.6 0.6 concatenate.85.halo_ref
  48.3 15.3 %shard_map.85 = (f32[8,128]{1,0:T(8,128)}, f32[4,128]{1,0:T(4,128)}) custom-call(s32[4097]{0:T(1024)} %pad_add_fusion.idx_ref, f32[16512]{0:T(1024)} %concatenate.83.src_ref, f32[6,8,128]{2,1,0:T(8,128)} %main_ref.1, f32[6,8,128]{2,1,0:T(8,128)} %concatenate.85.halo_ref), custom_call_target="tpu_custom_call" | custom-call | tf_op jit(solution)/shard_map/pallas_call | solution.py:83
  63.6 0.8 %fusion.16 = (f32[1,128]{1,0:T(1,128)S(1)}, f32[1,128]{1,0:T(1,128)S(1)}) fusion(f32[4,128]{1,0:T(4,128)} %get-tuple-element.5), kind=kLoop, calls=%fused_computation.94 | loop fusion | bytes 2048 | tf_op jit(solution)/shard_map/slice | solution.py:173
  64.3 0.8 %slice_bitcast_fusion.4 = (f32[8,1]{0,1:T(1,128)S(1)}, f32[8,1]{0,1:T(1,128)S(1)}) fusion(f32[4,128]{1,0:T(4,128)} %get-tuple-element.5), kind=kLoop, calls=%fused_computation.87 | loop fusion | bytes 128 | tf_op jit(solution)/shard_map/broadcast_in_dim;squeeze | solution.py:175
  65.2 0.1 slice.209
  65.2 0.1 slice.207
  65.3 0.1 pad_maximum_fusion.10
  65.5 0.1 fusion.1
  65.7 0.1 copy.34
  65.8 0.1 copy.33
  65.9 0.1 fusion.2
  66.0 0.1 copy-done.3
  66.1 0.1 add_subtract_fusion
  66.2 0.1 fusion.6
  66.3 0.6 fusion.9
  (48 shorter events, 0.8 us)
Async XLA Ops:
  4.6 13.6 %copy-start.5 = (s32[16]{0:T(128)S(1)}, s32[16]{0:T(128)}, u32[]{:S(2)}) copy-start(s32[16]{0:T(128)} %param.11) | copy-start | bytes 196
  4.6 13.6 %copy-start = (f32[6,8,128]{2,1,0:T(8,128)S(1)}, f32[6,8,128]{2,1,0:T(8,128)}, u32[]{:S(2)}) copy-start(f32[6,8,128]{2,1,0:T(8,128)} %main_ref.1) | copy-start | bytes 73732
  4.6 22.6 %all-to-all-start = ((f32[16,1,1408]{2,1,0:T(1,128)}), f32[16,1,1408]{2,1,0:T(1,128)S(1)}, u32[]{:S(2)}, u32[]{:S(2)}) async-start(f32[16,1,1408]{2,1,0:T(1,128)} %all_to_all.16), calls=%async_computation | async-start | bytes 180224 | tf_op jit(solution)/shard_map/all_to_all | solution.py:136
  18.1 0.7 %copy-start.4 = (s32[4,32]{1,0:T(4,128)S(1)}, s32[4,32]{1,0:T(4,128)}, u32[]{:S(2)}) copy-start(s32[4,32]{1,0:T(4,128)} %param.10) | copy-start | bytes 1540
  27.1 0.7 %copy-start.1 = (f32[8,128]{1,0:T(8,128)S(1)}, f32[8,128]{1,0:T(8,128)}, u32[]{:S(2)}) copy-start(f32[8,128]{1,0:T(8,128)} %param.8) | copy-start | bytes 12292
  27.2 0.7 %copy-start.2 = (f32[8,128]{1,0:T(8,128)S(1)}, f32[8,128]{1,0:T(8,128)}, u32[]{:S(2)}) copy-start(f32[8,128]{1,0:T(8,128)} %param.7) | copy-start | bytes 12292
  29.1 17.5 %all-to-all-start.1 = ((f32[32,1,608]{2,1,0:T(1,128)}), f32[32,1,608]{2,1,0:T(1,128)S(1)}, u32[]{:S(2)}, u32[]{:S(2)}) async-start(f32[32,1,608]{2,1,0:T(1,128)} %all_to_all.19), calls=%async_computation.1 | async-start | bytes 163840 | tf_op jit(solution)/shard_map/all_to_all | solution.py:156
  65.4 0.7 %copy-start.3 = (f32[8,128]{1,0:T(8,128)S(1)}, f32[8,128]{1,0:T(8,128)}, u32[]{:S(2)}) copy-start(f32[8,128]{1,0:T(8,128)} %get-tuple-element.4) | copy-start | bytes 12292

commit v14 on v13

--- a/solution.py
+++ b/solution.py
@@ -124,8 +124,7 @@
     owner = owner[:ROUNDS]
 
     fields = jnp.stack([eta, phi])
-    mine = (owner == row).astype(jnp.float32)
-    own_block = jnp.sum(mine[:, None, None] * sources[0], axis=0).reshape(-1)
+    own_block = sources[0].reshape(-1)
     top = jnp.concatenate([fields[:, :2].reshape(-1), target_geom[:, 0].reshape(-1)])
     bottom = jnp.concatenate([fields[:, -2:].reshape(-1), target_geom[:, -1].reshape(-1)])
     to_above = (jnp.arange(n_tile, dtype=jnp.int32) == row - 1)[:, None]
@@ -135,7 +134,8 @@
     ], axis=1)
     got = lax.all_to_all(payload, "tile", 0, 0, tiled=True)
     n_own = own_block.shape[0]
-    stacked = got[:, :n_own][owner]
+    src_rows = got[:, :n_own].reshape(n_tile, ROUNDS, n_own // ROUNDS)
+    stacked = src_rows[owner, jnp.arange(ROUNDS)]
     rim = 2 * cols_here * 2
     above = from_peer(got[:, n_own:], row, -1, n_tile)
     below = from_peer(got[:, n_own:], row, 1, n_tile)

time: 67.6 us -> 67.5 us (level)
  other arithmetic: 7.35 us -> 5.9 us
  local copies, waits for them, and re-layouts: 8.41 us -> 9.28 us
    reduce_sum x1 -> x0, other arithmetic: 0.78 us -> none  [body(): own_block = jnp.sum(mine[:, None, None] * sources[0], axis=0).reshape(-1)]
    broadcast_in_dim x1, local copies, waits for them, and re-layouts: 0.09 us -> 0.78 us  [body(): jnp.broadcast_to(own_block[None], (n_tile, own_block.shape[0]))]
where the time goes in v14:
time: 67.5 us; the launch traced here: 66.9 us
  starting transfers between devices  22.8 us (34%)
  Pallas kernels  15.3 us (23%)
  waiting for transfers between devices  12.6 us (19%)
  local copies, waits for them, and re-layouts  9.28 us (14%)
  other arithmetic  5.9 us (9%)
  between operations  0.97 us (1%)
    pallas_call x1, Pallas kernels, velocity(): pl.pallas_call(velocity_kernel, out_shape=(jax.ShapeDtypeStruct(main.shap...  15.3 us
    all_to_all x1, starting transfers between devices, body(): got = lax.all_to_all(payload, 'tile', 0, 0, tiled=True)  13.5 us
    all_to_all x1, starting transfers between devices, body(): got = lax.all_to_all(payload, 'eval', 0, 0, tiled=True)  9.3 us
    all_to_all x1, waiting for transfers between devices, body(): got = lax.all_to_all(payload, 'eval', 0, 0, tiled=True)  8.21 us
    all_to_all x1, waiting for transfers between devices, body(): got = lax.all_to_all(payload, 'tile', 0, 0, tiled=True)  4.35 us
  transfers between devices with their start and end apart: 2, of which 2 were waited for; matrix products, arithmetic and copies ran while one was open for 7% of the time, Pallas kernels for 0%

profile of v14, /device:TPU:1, one launch (start us, length us, event | category | flops | bytes accessed | tf_op | source)
XLA Modules:
  0.0 66.9 jit_solution(13082909924896238772)
XLA Ops:
  0.6 0.8 %fusion.18 = (f32[6,1,128]{2,1,0:T(1,128)S(1)}, f32[6,1,128]{2,1,0:T(1,128)S(1)}) fusion(f32[6,8,128]{2,1,0:T(8,128)} %main_ref.1), kind=kLoop, calls=%fused_computation.93 | loop fusion | bytes 12288 | tf_op jit(solution)/shard_map/slice | solution.py:128
  1.5 0.8 %reshape.300 = f32[512]{0:T(512)S(1)} reshape(f32[1,4,4,32]{3,2,1,0:T(4,128)} %param.9) | data formatting | bytes 4096 | tf_op jit(solution)/shard_map/broadcast_in_dim | solution.py:132
  2.3 0.8 %pad_maximum_fusion.16 = (f32[2,2,128]{2,1,0:T(2,128)S(1)}, f32[2,2,128]{2,1,0:T(2,128)S(1)}) fusion(f32[1,8,128]{2,1,0:T(8,128)} %bitcast.60, f32[1,8,128]{2,1,0:T(8,128)} %bitcast.64), kind=kLoop, calls=%fused_computation.65 | loop fusion | flops 1024 | bytes 12288 | tf_op jit(solution)/shard_map/slice | solution.py:128
  3.1 0.1 broadcast_select_fusion
  3.2 0.7 %all_to_all.16 = f32[16,1,1792]{2,1,0:T(1,128)} reshape(f32[16,1792]{1,0:T(8,128)S(1)} %pad_maximum_fusion) | data formatting | bytes 229376 | tf_op jit(solution)/shard_map/all_to_all | solution.py:135
  3.9 13.5 %all-to-all-start = ((f32[16,1,1792]{2,1,0:T(1,128)}), f32[16,1,1792]{2,1,0:T(1,128)S(1)}, u32[]{:S(2)}, u32[]{:S(2)}) async-start(f32[16,1,1792]{2,1,0:T(1,128)} %all_to_all.16), calls=%async_computation | async-start | bytes 229376 | tf_op jit(solution)/shard_map/all_to_all | solution.py:135
  17.5 0.1 slice_reduce_fusion.1
  17.6 0.1 copy.28
  17.7 0.1 reshape.275
  17.8 0.1 broadcast_in_dim.96
  17.9 0.2 reduce-window.4
  18.1 0.1 reduce
  18.2 0.5 slice.228
  18.7 0.1 reshape_squeeze.14
  18.8 0.1 reshape_squeeze.15
  18.9 1.2 %convert_reduce_fusion = (s32[4096]{0:T(1024)S(1)}, s32[4096]{0:T(1024)S(1)}) fusion(s32[128]{0:T(128)S(1)} %reduce, s32[128]{0:T(128)S(1)} %broadcast_in_dim.96), kind=kLoop, calls=%fused_computation.2 | loop fusion | flops 2613248 | bytes 33792 | tf_op jit(solution)/shard_map/reduce_sum | solution.py:74
  20.1 0.7 add_select_fusion
  20.8 1.3 %pad_add_fusion.idx_ref = s32[4097]{0:T(1024)} fusion(s32[1]{0:T(128)} %bitcast.2, s32[4096]{0:T(1024)S(1)} %add_select_fusion), kind=kLoop, calls=%fused_computation.27 | loop fusion | flops 4097 | bytes 32776 | tf_op jit(solution)/shard_map/concatenate | solution.py:78
  22.1 4.4 %all-to-all-done = f32[16,1,1792]{2,1,0:T(1,128)S(1)} async-done(((f32[16,1,1792]{2,1,0:T(1,128)}), f32[16,1,1792]{2,1,0:T(1,128)S(1)}, u32[]{:S(2)}, u32[]{:S(2)}) %all-to-all-start) | async-done | bytes 114720 | tf_op jit(solution)/shard_map/all_to_all | solution.py:135
  26.6 0.6 copy-done.1
  27.3 0.1 reshape.261
  27.3 0.1 reshape.262
  27.5 0.6 gather_fusion
  28.1 0.1 pad_maximum_fusion.21
  28.3 0.7 %all_to_all.19 = f32[32,1,608]{2,1,0:T(1,128)} reshape(f32[32,608]{1,0:T(8,128)S(1)} %pad_maximum_fusion.1) | data formatting | bytes 155648 | tf_op jit(solution)/shard_map/all_to_all | solution.py:156
  29.0 9.3 %all-to-all-start.1 = ((f32[32,1,608]{2,1,0:T(1,128)}), f32[32,1,608]{2,1,0:T(1,128)S(1)}, u32[]{:S(2)}, u32[]{:S(2)}) async-start(f32[32,1,608]{2,1,0:T(1,128)} %all_to_all.19), calls=%async_computation.1 | async-start | bytes 163840 | tf_op jit(solution)/shard_map/all_to_all | solution.py:156
  38.3 8.2 %all-to-all-done.1 = f32[32,1,608]{2,1,0:T(1,128)S(1)} async-done(((f32[32,1,608]{2,1,0:T(1,128)}), f32[32,1,608]{2,1,0:T(1,128)S(1)}, u32[]{:S(2)}, u32[]{:S(2)}) %all-to-all-start.1) | async-done | bytes 77856 | tf_op jit(solution)/shard_map/all_to_all | solution.py:156
  46.5 0.1 slice_reduce_fusion.4
  46.6 0.1 slice.199
  46.7 0.1 slice.201
  46.8 0.1 select_maximum_fusion
  46.9 0.6 concatenate.87.src_ref
  47.5 0.6 concatenate.89.halo_ref
  48.2 15.3 %shard_map.85 = (f32[8,128]{1,0:T(8,128)}, f32[4,128]{1,0:T(4,128)}) custom-call(s32[4097]{0:T(1024)} %pad_add_fusion.idx_ref, f32[16512]{0:T(1024)} %concatenate.87.src_ref, f32[6,8,128]{2,1,0:T(8,128)} %main_ref.1, f32[6,8,128]{2,1,0:T(8,128)} %concatenate.89.halo_ref), custom_call_target="tpu_custom_call" | custom-call | tf_op jit(solution)/shard_map/pallas_call | solution.py:83
  63.5 0.8 %fusion.20 = (f32[1,128]{1,0:T(1,128)S(1)}, f32[1,128]{1,0:T(1,128)S(1)}) fusion(f32[4,128]{1,0:T(4,128)} %get-tuple-element.5), kind=kLoop, calls=%fused_computation.95 | loop fusion | bytes 2048 | tf_op jit(solution)/shard_map/slice | solution.py:173
  64.3 0.8 %slice_bitcast_fusion.4 = (f32[8,1]{0,1:T(1,128)S(1)}, f32[8,1]{0,1:T(1,128)S(1)}) fusion(f32[4,128]{1,0:T(4,128)} %get-tuple-element.5), kind=kLoop, calls=%fused_computation.87 | loop fusion | bytes 128 | tf_op jit(solution)/shard_map/broadcast_in_dim;squeeze | solution.py:175
  65.1 0.1 slice.207
  65.2 0.1 slice.209
  65.3 0.1 pad_maximum_fusion.10
  65.4 0.1 fusion.1
  65.5 0.1 fusion.11
  65.6 0.1 copy.33
  65.7 0.1 copy.34
  65.8 0.1 fusion.2
  65.9 0.1 copy-done.3
  66.1 0.1 add_subtract_fusion
  66.2 0.1 fusion.6
  66.3 0.6 fusion.8
  (46 shorter events, 0.7 us)
Async XLA Ops:
  3.9 13.6 %copy-start = (f32[6,8,128]{2,1,0:T(8,128)S(1)}, f32[6,8,128]{2,1,0:T(8,128)}, u32[]{:S(2)}) copy-start(f32[6,8,128]{2,1,0:T(8,128)} %main_ref.1) | copy-start | bytes 73732
  3.9 13.8 %copy-start.4 = (s32[4,32]{1,0:T(4,128)S(1)}, s32[4,32]{1,0:T(4,128)}, u32[]{:S(2)}) copy-start(s32[4,32]{1,0:T(4,128)} %param.10) | copy-start | bytes 1540
  3.9 22.6 %all-to-all-start = ((f32[16,1,1792]{2,1,0:T(1,128)}), f32[16,1,1792]{2,1,0:T(1,128)S(1)}, u32[]{:S(2)}, u32[]{:S(2)}) async-start(f32[16,1,1792]{2,1,0:T(1,128)} %all_to_all.16), calls=%async_computation | async-start | bytes 229376 | tf_op jit(solution)/shard_map/all_to_all | solution.py:135
  18.1 4.0 %copy-start.5 = (s32[16]{0:T(128)S(1)}, s32[16]{0:T(128)}, u32[]{:S(2)}) copy-start(s32[16]{0:T(128)} %param.11) | copy-start | bytes 196
  26.5 0.7 %copy-start.1 = (f32[8,128]{1,0:T(8,128)S(1)}, f32[8,128]{1,0:T(8,128)}, u32[]{:S(2)}) copy-start(f32[8,128]{1,0:T(8,128)} %param.8) | copy-start | bytes 12292
  26.5 0.7 %copy-start.2 = (f32[8,128]{1,0:T(8,128)S(1)}, f32[8,128]{1,0:T(8,128)}, u32[]{:S(2)}) copy-start(f32[8,128]{1,0:T(8,128)} %param.7) | copy-start | bytes 12292
  29.0 17.5 %all-to-all-start.1 = ((f32[32,1,608]{2,1,0:T(1,128)}), f32[32,1,608]{2,1,0:T(1,128)S(1)}, u32[]{:S(2)}, u32[]{:S(2)}) async-start(f32[32,1,608]{2,1,0:T(1,128)} %all_to_all.19), calls=%async_computation.1 | async-start | bytes 163840 | tf_op jit(solution)/shard_map/all_to_all | solution.py:156
  65.4 0.7 %copy-start.3 = (f32[8,128]{1,0:T(8,128)S(1)}, f32[8,128]{1,0:T(8,128)}, u32[]{:S(2)}) copy-start(f32[8,128]{1,0:T(8,128)} %get-tuple-element.4) | copy-start | bytes 12292

commit v15 on v13

--- a/solution.py
+++ b/solution.py
@@ -26,7 +26,7 @@
     return jnp.where(ok, chunk, jnp.zeros_like(chunk))
 
 
-def velocity_kernel(idx_ref, src_ref, main_ref, halo_ref, out_main_ref, out_halo_ref):
+def velocity_kernel(idx_ref, src_ref, main_ref, halo_ref, out_main_ref, out_up_ref, out_down_ref, out_side_ref):
     total = idx_ref[idx_ref.shape[0] - 1]
     main = tuple(main_ref[k] for k in range(6))
     halo = tuple(halo_ref[k] for k in range(6))
@@ -63,7 +63,10 @@
     acc_m, acc_h = lax.fori_loop(0, blocks, block, (zero, zero))
     half = acc_h.shape[0] // 2
     out_main_ref[...] = acc_m
-    out_halo_ref[...] = acc_h[:half] + acc_h[half:]
+    acc_h = acc_h[:half] + acc_h[half:]
+    out_up_ref[...] = acc_h[0:1]
+    out_down_ref[...] = acc_h[1:2]
+    out_side_ref[...] = acc_h[2:3]
 
 
 def live_slots(group_len, slots):
@@ -79,17 +82,17 @@
 
 
 def velocity(idx, src, main, halo):
-    half = jax.ShapeDtypeStruct((halo.shape[1] // 2, halo.shape[2]), jnp.float32)
+    row = jax.ShapeDtypeStruct((1, halo.shape[2]), jnp.float32)
     return pl.pallas_call(
         velocity_kernel,
-        out_shape=(jax.ShapeDtypeStruct(main.shape[1:], jnp.float32), half),
+        out_shape=(jax.ShapeDtypeStruct(main.shape[1:], jnp.float32), row, row, row),
         in_specs=[
             pl.BlockSpec(memory_space=pltpu.SMEM),
             pl.BlockSpec(memory_space=pltpu.SMEM),
             pl.BlockSpec(memory_space=pltpu.VMEM),
             pl.BlockSpec(memory_space=pltpu.VMEM),
         ],
-        out_specs=(pl.BlockSpec(memory_space=pltpu.VMEM), pl.BlockSpec(memory_space=pltpu.VMEM)),
+        out_specs=tuple(pl.BlockSpec(memory_space=pltpu.VMEM) for _ in range(4)),
     )(idx, src, main, halo)
 
 
@@ -169,11 +172,9 @@
     sides = jnp.pad(sides, ((0, 0), (0, cols_here - 2 * rows_here)))
     halo = jnp.stack([t_above, t_below, sides, jnp.zeros_like(sides)], axis=1)
     halo = jnp.concatenate([halo, halo], axis=1)
-    vel_main, vel_halo = velocity(idx, all_src, target_geom, halo)
-    vel_up = vel_halo[0:1]
-    vel_down = vel_halo[1:2]
-    vel_left = vel_halo[2, :rows_here][:, None]
-    vel_right = vel_halo[2, rows_here:2 * rows_here][:, None]
+    vel_main, vel_up, vel_down, vel_side = velocity(idx, all_src, target_geom, halo)
+    vel_left = vel_side[0, :rows_here][:, None]
+    vel_right = vel_side[0, rows_here:2 * rows_here][:, None]
 
     vel_rows = jnp.concatenate([vel_up, vel_main, vel_down], axis=0)
     corner = jnp.zeros((1, 1), jnp.float32)

time: 67.6 us -> 66.7 us (0.987)
  local copies, waits for them, and re-layouts: 8.41 us -> 7.46 us
    slice x1 -> x0, local copies, waits for them, and re-layouts: 0.76 us -> none  [body(): vel_up = vel_halo[0:1]]
where the time goes in v15:
time: 66.7 us; the launch traced here: 66 us
  starting transfers between devices  22.8 us (34%)
  Pallas kernels  15.3 us (23%)
  waiting for transfers between devices  12.1 us (18%)
  local copies, waits for them, and re-layouts  7.46 us (11%)
  other arithmetic  7.34 us (11%)
  between operations  1 us (1%)
    pallas_call x1, Pallas kernels, velocity(): pl.pallas_call(velocity_kernel, out_shape=(jax.ShapeDtypeStruct(main.shap...  15.3 us
    all_to_all x1, starting transfers between devices, body(): got = lax.all_to_all(payload, 'tile', 0, 0, tiled=True)  13.5 us
    all_to_all x1, starting transfers between devices, body(): got = lax.all_to_all(payload, 'eval', 0, 0, tiled=True)  9.28 us
    all_to_all x1, waiting for transfers between devices, body(): got = lax.all_to_all(payload, 'eval', 0, 0, tiled=True)  8.21 us
    all_to_all x1, waiting for transfers between devices, body(): got = lax.all_to_all(payload, 'tile', 0, 0, tiled=True)  3.86 us
  transfers between devices with their start and end apart: 2, of which 2 were waited for; matrix products, arithmetic and copies ran while one was open for 7% of the time, Pallas kernels for 0%

profile of v15, /device:TPU:1, one launch (start us, length us, event | category | flops | bytes accessed | tf_op | source)
XLA Modules:
  0.0 66.0 jit_solution(10750028327421280589)
XLA Ops:
  0.6 0.7 compare_convert_fusion
  1.3 0.8 %fusion.7 = f32[4,32]{1,0:T(4,128)S(1)} fusion(f32[1,4,4,32]{3,2,1,0:T(4,128)} %param.9, f32[4]{0:T(128)S(1)} %compare_convert_fusion), kind=kLoop, calls=%fused_computation.51 | loop fusion | flops 896 | bytes 2576 | tf_op jit(solution)/shard_map/reduce_sum | solution.py:131
  2.1 0.1 reshape.295
  2.2 0.8 %fusion.14 = (f32[6,1,128]{2,1,0:T(1,128)S(1)}, f32[6,1,128]{2,1,0:T(1,128)S(1)}) fusion(f32[6,8,128]{2,1,0:T(8,128)} %main_ref.1), kind=kLoop, calls=%fused_computation.92 | loop fusion | bytes 12288 | tf_op jit(solution)/shard_map/slice | solution.py:132
  3.0 0.8 %pad_maximum_fusion.16 = (f32[2,2,128]{2,1,0:T(2,128)S(1)}, f32[2,2,128]{2,1,0:T(2,128)S(1)}) fusion(f32[1,8,128]{2,1,0:T(8,128)} %bitcast.56, f32[1,8,128]{2,1,0:T(8,128)} %bitcast.60), kind=kLoop, calls=%fused_computation.68 | loop fusion | flops 1024 | bytes 12288 | tf_op jit(solution)/shard_map/slice | solution.py:132
  3.8 0.1 broadcast_select_fusion
  3.9 0.7 %all_to_all.16 = f32[16,1,1408]{2,1,0:T(1,128)} reshape(f32[16,1408]{1,0:T(8,128)S(1)} %pad_maximum_fusion) | data formatting | bytes 180224 | tf_op jit(solution)/shard_map/all_to_all | solution.py:139
  4.6 13.5 %all-to-all-start = ((f32[16,1,1408]{2,1,0:T(1,128)}), f32[16,1,1408]{2,1,0:T(1,128)S(1)}, u32[]{:S(2)}, u32[]{:S(2)}) async-start(f32[16,1,1408]{2,1,0:T(1,128)} %all_to_all.16), calls=%async_computation | async-start | bytes 180224 | tf_op jit(solution)/shard_map/all_to_all | solution.py:139
  18.2 0.1 slice_reduce_fusion.1
  18.4 0.5 copy-done.4
  18.8 0.1 copy.28
  18.9 0.1 broadcast_in_dim.96
  19.1 0.2 reduce-window.4
  19.3 0.5 slice.220
  19.8 0.1 reduce
  20.0 0.1 reshape_squeeze.14
  20.0 0.1 reshape_squeeze.15
  20.1 1.2 %convert_reduce_fusion = (s32[4096]{0:T(1024)S(1)}, s32[4096]{0:T(1024)S(1)}) fusion(s32[128]{0:T(128)S(1)} %reduce, s32[128]{0:T(128)S(1)} %broadcast_in_dim.96), kind=kLoop, calls=%fused_computation.2 | loop fusion | flops 2613248 | bytes 33792 | tf_op jit(solution)/shard_map/reduce_sum | solution.py:77
  21.3 0.7 add_select_fusion
  21.9 1.3 %pad_add_fusion.idx_ref = s32[4097]{0:T(1024)} fusion(s32[1]{0:T(128)} %bitcast.2, s32[4096]{0:T(1024)S(1)} %add_select_fusion), kind=kLoop, calls=%fused_computation.27 | loop fusion | flops 4097 | bytes 32776 | tf_op jit(solution)/shard_map/concatenate | solution.py:81
  23.3 3.9 %all-to-all-done = f32[16,1,1408]{2,1,0:T(1,128)S(1)} async-done(((f32[16,1,1408]{2,1,0:T(1,128)}), f32[16,1,1408]{2,1,0:T(1,128)S(1)}, u32[]{:S(2)}, u32[]{:S(2)}) %all-to-all-start) | async-done | bytes 90144 | tf_op jit(solution)/shard_map/all_to_all | solution.py:139
  27.2 0.6 gather_fusion
  27.9 0.1 fusion.15
  27.9 0.1 reshape.258
  28.0 0.1 reshape.259
  28.1 0.1 pad_maximum_fusion.21
  28.2 0.1 pad_maximum_fusion.22
  28.4 0.7 %all_to_all.19 = f32[32,1,608]{2,1,0:T(1,128)} reshape(f32[32,608]{1,0:T(8,128)S(1)} %pad_maximum_fusion.1) | data formatting | bytes 155648 | tf_op jit(solution)/shard_map/all_to_all | solution.py:159
  29.1 9.3 %all-to-all-start.1 = ((f32[32,1,608]{2,1,0:T(1,128)}), f32[32,1,608]{2,1,0:T(1,128)S(1)}, u32[]{:S(2)}, u32[]{:S(2)}) async-start(f32[32,1,608]{2,1,0:T(1,128)} %all_to_all.19), calls=%async_computation.1 | async-start | bytes 163840 | tf_op jit(solution)/shard_map/all_to_all | solution.py:159
  38.4 8.2 %all-to-all-done.1 = f32[32,1,608]{2,1,0:T(1,128)S(1)} async-done(((f32[32,1,608]{2,1,0:T(1,128)}), f32[32,1,608]{2,1,0:T(1,128)S(1)}, u32[]{:S(2)}, u32[]{:S(2)}) %all-to-all-start.1) | async-done | bytes 77856 | tf_op jit(solution)/shard_map/all_to_all | solution.py:159
  46.6 0.1 slice_reduce_fusion.4
  46.7 0.1 slice.201
  46.8 0.1 slice.199
  46.9 0.1 pad_maximum_fusion.10
  47.0 0.1 fusion.1
  47.1 0.1 slice.195
  47.2 0.1 slice.193
  47.3 0.1 select_maximum_fusion
  47.4 0.6 concatenate.83.src_ref
  48.0 0.6 concatenate.85.halo_ref
  48.6 15.3 %shard_map.85 = (f32[8,128]{1,0:T(8,128)}, f32[1,128]{1,0:T(1,128)}, f32[1,128]{1,0:T(1,128)}, f32[1,128]{1,0:T(1,128)}) custom-call(s32[4097]{0:T(1024)} %pad_add_fusion.idx_ref, f32[16512]{0:T(1024)} %concatenate.83.src_ref, f32[6,8,128]{2,1,0:T(8,128)} %main_ref.1, f32[6,8,128]{2,1,0:T(8,128)} %concatenate.85.halo_ref), custom_call_target="tpu_custom_call" | custom-call | tf_op jit(solution)/shard_map/pallas_call | solution.py:86
  64.0 0.8 %slice_bitcast_fusion.4 = (f32[8,1]{0,1:T(1,128)S(1)}, f32[8,1]{0,1:T(1,128)S(1)}) fusion(f32[1,128]{1,0:T(1,128)} %get-tuple-element.7), kind=kLoop, calls=%fused_computation.87 | loop fusion | bytes 128 | tf_op jit(solution)/shard_map/broadcast_in_dim;squeeze | solution.py:176
  64.9 0.1 copy.34
  65.0 0.1 copy.33
  65.1 0.1 fusion.2
  65.2 0.1 add_subtract_fusion
  65.3 0.1 fusion.6
  65.4 0.6 fusion.9
  (51 shorter events, 0.7 us)
Async XLA Ops:
  4.6 13.6 %copy-start.7 = (s32[16]{0:T(128)S(1)}, s32[16]{0:T(128)}, u32[]{:S(2)}) copy-start(s32[16]{0:T(128)} %param.11) | copy-start | bytes 196
  4.6 13.6 %copy-start = (f32[6,8,128]{2,1,0:T(8,128)S(1)}, f32[6,8,128]{2,1,0:T(8,128)}, u32[]{:S(2)}) copy-start(f32[6,8,128]{2,1,0:T(8,128)} %main_ref.1) | copy-start | bytes 73732
  4.6 22.6 %all-to-all-start = ((f32[16,1,1408]{2,1,0:T(1,128)}), f32[16,1,1408]{2,1,0:T(1,128)S(1)}, u32[]{:S(2)}, u32[]{:S(2)}) async-start(f32[16,1,1408]{2,1,0:T(1,128)} %all_to_all.16), calls=%async_computation | async-start | bytes 180224 | tf_op jit(solution)/shard_map/all_to_all | solution.py:139
  18.1 0.7 %copy-start.4 = (s32[4,32]{1,0:T(4,128)S(1)}, s32[4,32]{1,0:T(4,128)}, u32[]{:S(2)}) copy-start(s32[4,32]{1,0:T(4,128)} %param.10) | copy-start | bytes 1540
  27.1 0.7 %copy-start.1 = (f32[8,128]{1,0:T(8,128)S(1)}, f32[8,128]{1,0:T(8,128)}, u32[]{:S(2)}) copy-start(f32[8,128]{1,0:T(8,128)} %param.8) | copy-start | bytes 12292
  27.2 0.7 %copy-start.2 = (f32[8,128]{1,0:T(8,128)S(1)}, f32[8,128]{1,0:T(8,128)}, u32[]{:S(2)}) copy-start(f32[8,128]{1,0:T(8,128)} %param.7) | copy-start | bytes 12292
  29.1 17.5 %all-to-all-start.1 = ((f32[32,1,608]{2,1,0:T(1,128)}), f32[32,1,608]{2,1,0:T(1,128)S(1)}, u32[]{:S(2)}, u32[]{:S(2)}) async-start(f32[32,1,608]{2,1,0:T(1,128)} %all_to_all.19), calls=%async_computation.1 | async-start | bytes 163840 | tf_op jit(solution)/shard_map/all_to_all | solution.py:159
  64.0 1.2 %copy-start.3 = (f32[8,128]{1,0:T(8,128)S(1)}, f32[8,128]{1,0:T(8,128)}, u32[]{:S(2)}) copy-start(f32[8,128]{1,0:T(8,128)} %get-tuple-element.6) | copy-start | bytes 12292
  64.0 1.2 %copy-start.5 = (f32[1,128]{1,0:T(1,128)S(1)}, f32[1,128]{1,0:T(1,128)}, u32[]{:S(2)}) copy-start(f32[1,128]{1,0:T(1,128)} %get-tuple-element.8) | copy-start | bytes 1540
  64.0 1.2 %copy-start.6 = (f32[1,128]{1,0:T(1,128)S(1)}, f32[1,128]{1,0:T(1,128)}, u32[]{:S(2)}) copy-start(f32[1,128]{1,0:T(1,128)} %get-tuple-element.10) | copy-start | bytes 1540

commit v16 on v15

--- a/solution.py
+++ b/solution.py
@@ -26,7 +26,7 @@
     return jnp.where(ok, chunk, jnp.zeros_like(chunk))
 
 
-def velocity_kernel(idx_ref, src_ref, main_ref, halo_ref, out_main_ref, out_up_ref, out_down_ref, out_side_ref):
+def velocity_kernel(idx_ref, src_ref, main_ref, halo_ref, out_main_ref, out_up_ref, out_down_ref, out_left_ref, out_right_ref):
     total = idx_ref[idx_ref.shape[0] - 1]
     main = tuple(main_ref[k] for k in range(6))
     halo = tuple(halo_ref[k] for k in range(6))
@@ -66,7 +66,10 @@
     acc_h = acc_h[:half] + acc_h[half:]
     out_up_ref[...] = acc_h[0:1]
     out_down_ref[...] = acc_h[1:2]
-    out_side_ref[...] = acc_h[2:3]
+    rows = out_left_ref.shape[0]
+    columns = jnp.transpose(jnp.concatenate([acc_h, acc_h]))
+    out_left_ref[...] = columns[0:rows, 2:3]
+    out_right_ref[...] = columns[rows:2 * rows, 2:3]
 
 
 def live_slots(group_len, slots):
@@ -83,16 +86,17 @@
 
 def velocity(idx, src, main, halo):
     row = jax.ShapeDtypeStruct((1, halo.shape[2]), jnp.float32)
+    column = jax.ShapeDtypeStruct((main.shape[1], 1), jnp.float32)
     return pl.pallas_call(
         velocity_kernel,
-        out_shape=(jax.ShapeDtypeStruct(main.shape[1:], jnp.float32), row, row, row),
+        out_shape=(jax.ShapeDtypeStruct(main.shape[1:], jnp.float32), row, row, column, column),
         in_specs=[
             pl.BlockSpec(memory_space=pltpu.SMEM),
             pl.BlockSpec(memory_space=pltpu.SMEM),
             pl.BlockSpec(memory_space=pltpu.VMEM),
             pl.BlockSpec(memory_space=pltpu.VMEM),
         ],
-        out_specs=tuple(pl.BlockSpec(memory_space=pltpu.VMEM) for _ in range(4)),
+        out_specs=tuple(pl.BlockSpec(memory_space=pltpu.VMEM) for _ in range(5)),
     )(idx, src, main, halo)
 
 
@@ -172,9 +176,7 @@
     sides = jnp.pad(sides, ((0, 0), (0, cols_here - 2 * rows_here)))
     halo = jnp.stack([t_above, t_below, sides, jnp.zeros_like(sides)], axis=1)
     halo = jnp.concatenate([halo, halo], axis=1)
-    vel_main, vel_up, vel_down, vel_side = velocity(idx, all_src, target_geom, halo)
-    vel_left = vel_side[0, :rows_here][:, None]
-    vel_right = vel_side[0, rows_here:2 * rows_here][:, None]
+    vel_main, vel_up, vel_down, vel_left, vel_right = velocity(idx, all_src, target_geom, halo)
 
     vel_rows = jnp.concatenate([vel_up, vel_main, vel_down], axis=0)
     corner = jnp.zeros((1, 1), jnp.float32)

time: 66.7 us -> 67.6 us (1.013)
  local copies, waits for them, and re-layouts: 7.46 us -> 8.23 us
    pallas_call x0 -> x2, local copies, waits for them, and re-layouts: none -> 1.55 us  [velocity(): pl.pallas_call(velocity_kernel, out_shape=(jax.ShapeDtypeStruct(main.shap...]
    another operation x1 -> x0, local copies, waits for them, and re-layouts: 0.78 us -> none  [body(): vel_left = vel_side[0, :rows_here][:, None]]
where the time goes in v16:
time: 67.6 us; the launch traced here: 66.9 us
  starting transfers between devices  22.8 us (34%)
  Pallas kernels  15.4 us (23%)
  waiting for transfers between devices  12.1 us (18%)
  local copies, waits for them, and re-layouts  8.23 us (12%)
  other arithmetic  7.34 us (11%)
  between operations  0.99 us (1%)
    pallas_call x1, Pallas kernels, velocity(): pl.pallas_call(velocity_kernel, out_shape=(jax.ShapeDtypeStruct(main.shap...  15.4 us
    all_to_all x1, starting transfers between devices, body(): got = lax.all_to_all(payload, 'tile', 0, 0, tiled=True)  13.5 us
    all_to_all x1, starting transfers between devices, body(): got = lax.all_to_all(payload, 'eval', 0, 0, tiled=True)  9.28 us
    all_to_all x1, waiting for transfers between devices, body(): got = lax.all_to_all(payload, 'eval', 0, 0, tiled=True)  8.21 us
    all_to_all x1, waiting for transfers between devices, body(): got = lax.all_to_all(payload, 'tile', 0, 0, tiled=True)  3.86 us
    pallas_call x2, local copies, waits for them, and re-layouts, velocity(): pl.pallas_call(velocity_kernel, out_shape=(jax.ShapeDtypeStruct(main.shap...  1.55 us
  transfers between devices with their start and end apart: 2, of which 2 were waited for; matrix products, arithmetic and copies ran while one was open for 7% of the time, Pallas kernels for 0%

profile of v16, /device:TPU:1, one launch (start us, length us, event | category | flops | bytes accessed | tf_op | source)
XLA Modules:
  0.0 66.9 jit_solution(16206870100533665589)
XLA Ops:
  0.6 0.7 compare_convert_fusion
  1.3 0.8 %fusion.7 = f32[4,32]{1,0:T(4,128)S(1)} fusion(f32[1,4,4,32]{3,2,1,0:T(4,128)} %param.9, f32[4]{0:T(128)S(1)} %compare_convert_fusion), kind=kLoop, calls=%fused_computation.51 | loop fusion | flops 896 | bytes 2576 | tf_op jit(solution)/shard_map/reduce_sum | solution.py:135
  2.1 0.1 reshape.295
  2.2 0.8 %fusion.14 = (f32[6,1,128]{2,1,0:T(1,128)S(1)}, f32[6,1,128]{2,1,0:T(1,128)S(1)}) fusion(f32[6,8,128]{2,1,0:T(8,128)} %main_ref.1), kind=kLoop, calls=%fused_computation.90 | loop fusion | bytes 12288 | tf_op jit(solution)/shard_map/slice | solution.py:136
  3.0 0.8 %pad_maximum_fusion.16 = (f32[2,2,128]{2,1,0:T(2,128)S(1)}, f32[2,2,128]{2,1,0:T(2,128)S(1)}) fusion(f32[1,8,128]{2,1,0:T(8,128)} %bitcast.52, f32[1,8,128]{2,1,0:T(8,128)} %bitcast.56), kind=kLoop, calls=%fused_computation.68 | loop fusion | flops 1024 | bytes 12288 | tf_op jit(solution)/shard_map/slice | solution.py:136
  3.8 0.1 broadcast_select_fusion
  3.9 0.7 %all_to_all.16 = f32[16,1,1408]{2,1,0:T(1,128)} reshape(f32[16,1408]{1,0:T(8,128)S(1)} %pad_maximum_fusion) | data formatting | bytes 180224 | tf_op jit(solution)/shard_map/all_to_all | solution.py:143
  4.6 13.5 %all-to-all-start = ((f32[16,1,1408]{2,1,0:T(1,128)}), f32[16,1,1408]{2,1,0:T(1,128)S(1)}, u32[]{:S(2)}, u32[]{:S(2)}) async-start(f32[16,1,1408]{2,1,0:T(1,128)} %all_to_all.16), calls=%async_computation | async-start | bytes 180224 | tf_op jit(solution)/shard_map/all_to_all | solution.py:143
  18.2 0.1 slice_reduce_fusion.1
  18.4 0.5 copy-done.4
  18.8 0.1 copy.30
  18.9 0.1 broadcast_in_dim.96
  19.1 0.2 reduce-window.4
  19.3 0.5 slice.212
  19.8 0.1 reduce
  20.0 0.1 reshape_squeeze.14
  20.0 0.1 reshape_squeeze.15
  20.1 1.2 %convert_reduce_fusion = (s32[4096]{0:T(1024)S(1)}, s32[4096]{0:T(1024)S(1)}) fusion(s32[128]{0:T(128)S(1)} %reduce, s32[128]{0:T(128)S(1)} %broadcast_in_dim.96), kind=kLoop, calls=%fused_computation.2 | loop fusion | flops 2613248 | bytes 33792 | tf_op jit(solution)/shard_map/reduce_sum | solution.py:80
  21.3 0.7 add_select_fusion
  21.9 1.3 %pad_add_fusion.idx_ref = s32[4097]{0:T(1024)} fusion(s32[1]{0:T(128)} %bitcast.2, s32[4096]{0:T(1024)S(1)} %add_select_fusion), kind=kLoop, calls=%fused_computation.27 | loop fusion | flops 4097 | bytes 32776 | tf_op jit(solution)/shard_map/concatenate | solution.py:84
  23.3 3.9 %all-to-all-done = f32[16,1,1408]{2,1,0:T(1,128)S(1)} async-done(((f32[16,1,1408]{2,1,0:T(1,128)}), f32[16,1,1408]{2,1,0:T(1,128)S(1)}, u32[]{:S(2)}, u32[]{:S(2)}) %all-to-all-start) | async-done | bytes 90144 | tf_op jit(solution)/shard_map/all_to_all | solution.py:143
  27.2 0.6 gather_fusion
  27.9 0.1 fusion.15
  27.9 0.1 reshape.258
  28.0 0.1 reshape.259
  28.1 0.1 pad_maximum_fusion.21
  28.4 0.7 %all_to_all.19 = f32[32,1,608]{2,1,0:T(1,128)} reshape(f32[32,608]{1,0:T(8,128)S(1)} %pad_maximum_fusion.1) | data formatting | bytes 155648 | tf_op jit(solution)/shard_map/all_to_all | solution.py:163
  29.1 9.3 %all-to-all-start.1 = ((f32[32,1,608]{2,1,0:T(1,128)}), f32[32,1,608]{2,1,0:T(1,128)S(1)}, u32[]{:S(2)}, u32[]{:S(2)}) async-start(f32[32,1,608]{2,1,0:T(1,128)} %all_to_all.19), calls=%async_computation.1 | async-start | bytes 163840 | tf_op jit(solution)/shard_map/all_to_all | solution.py:163
  38.4 8.2 %all-to-all-done.1 = f32[32,1,608]{2,1,0:T(1,128)S(1)} async-done(((f32[32,1,608]{2,1,0:T(1,128)}), f32[32,1,608]{2,1,0:T(1,128)S(1)}, u32[]{:S(2)}, u32[]{:S(2)}) %all-to-all-start.1) | async-done | bytes 77856 | tf_op jit(solution)/shard_map/all_to_all | solution.py:163
  46.6 0.1 slice_reduce_fusion.4
  46.7 0.1 slice.193
  46.8 0.1 slice.191
  46.9 0.1 pad_maximum_fusion.10
  47.0 0.1 fusion.1
  47.1 0.1 slice.189
  47.2 0.1 slice.187
  47.3 0.1 select_maximum_fusion
  47.4 0.6 concatenate.83.src_ref
  48.0 0.6 concatenate.85.halo_ref
  48.6 15.4 %shard_map.85 = (f32[8,128]{1,0:T(8,128)}, f32[1,128]{1,0:T(1,128)}, f32[1,128]{1,0:T(1,128)}, f32[8,1]{1,0:T(8,128)}, f32[8,1]{1,0:T(8,128)}) custom-call(s32[4097]{0:T(1024)} %pad_add_fusion.idx_ref, f32[16512]{0:T(1024)} %concatenate.83.src_ref, f32[6,8,128]{2,1,0:T(8,128)} %main_ref.1, f32[6,8,128]{2,1,0:T(8,128)} %concatenate.85.halo_ref), custom_call_target="tpu_custom_call" | custom-call | tf_op jit(solution)/shard_map/pallas_call | solution.py:90
  64.1 0.8 %copy.35 = f32[8,1]{0,1:T(1,128)S(1)} copy(f32[8,1]{1,0:T(8,128)} %get-tuple-element.8) | data formatting | bytes 64 | tf_op jit(solution)/shard_map/pallas_call | solution.py:90
  64.9 0.8 %copy.36 = f32[8,1]{0,1:T(1,128)S(1)} copy(f32[8,1]{1,0:T(8,128)} %get-tuple-element.12) | data formatting | bytes 64 | tf_op jit(solution)/shard_map/pallas_call | solution.py:90
  65.8 0.1 copy.38
  65.9 0.1 copy.37
  66.0 0.1 fusion.2
  66.1 0.1 add_subtract_fusion
  66.2 0.1 fusion.6
  66.3 0.6 fusion.9
  (52 shorter events, 0.7 us)
Async XLA Ops:
  4.6 13.6 %copy-start.7 = (s32[16]{0:T(128)S(1)}, s32[16]{0:T(128)}, u32[]{:S(2)}) copy-start(s32[16]{0:T(128)} %param.11) | copy-start | bytes 196
  4.6 13.6 %copy-start = (f32[6,8,128]{2,1,0:T(8,128)S(1)}, f32[6,8,128]{2,1,0:T(8,128)}, u32[]{:S(2)}) copy-start(f32[6,8,128]{2,1,0:T(8,128)} %main_ref.1) | copy-start | bytes 73732
  4.6 22.6 %all-to-all-start = ((f32[16,1,1408]{2,1,0:T(1,128)}), f32[16,1,1408]{2,1,0:T(1,128)S(1)}, u32[]{:S(2)}, u32[]{:S(2)}) async-start(f32[16,1,1408]{2,1,0:T(1,128)} %all_to_all.16), calls=%async_computation | async-start | bytes 180224 | tf_op jit(solution)/shard_map/all_to_all | solution.py:143
  18.1 0.7 %copy-start.4 = (s32[4,32]{1,0:T(4,128)S(1)}, s32[4,32]{1,0:T(4,128)}, u32[]{:S(2)}) copy-start(s32[4,32]{1,0:T(4,128)} %param.10) | copy-start | bytes 1540
  27.1 0.7 %copy-start.1 = (f32[8,128]{1,0:T(8,128)S(1)}, f32[8,128]{1,0:T(8,128)}, u32[]{:S(2)}) copy-start(f32[8,128]{1,0:T(8,128)} %param.8) | copy-start | bytes 12292
  27.2 0.7 %copy-start.2 = (f32[8,128]{1,0:T(8,128)S(1)}, f32[8,128]{1,0:T(8,128)}, u32[]{:S(2)}) copy-start(f32[8,128]{1,0:T(8,128)} %param.7) | copy-start | bytes 12292
  29.1 17.5 %all-to-all-start.1 = ((f32[32,1,608]{2,1,0:T(1,128)}), f32[32,1,608]{2,1,0:T(1,128)S(1)}, u32[]{:S(2)}, u32[]{:S(2)}) async-start(f32[32,1,608]{2,1,0:T(1,128)} %all_to_all.19), calls=%async_computation.1 | async-start | bytes 163840 | tf_op jit(solution)/shard_map/all_to_all | solution.py:163
  64.1 2.0 %copy-start.3 = (f32[8,128]{1,0:T(8,128)S(1)}, f32[8,128]{1,0:T(8,128)}, u32[]{:S(2)}) copy-start(f32[8,128]{1,0:T(8,128)} %get-tuple-element.7) | copy-start | bytes 12292
  64.1 2.0 %copy-start.5 = (f32[1,128]{1,0:T(1,128)S(1)}, f32[1,128]{1,0:T(1,128)}, u32[]{:S(2)}) copy-start(f32[1,128]{1,0:T(1,128)} %get-tuple-element.9) | copy-start | bytes 1540
  64.1 2.0 %copy-start.6 = (f32[1,128]{1,0:T(1,128)S(1)}, f32[1,128]{1,0:T(1,128)}, u32[]{:S(2)}) copy-start(f32[1,128]{1,0:T(1,128)} %get-tuple-element.11) | copy-start | bytes 1540

commit v17 on v15

--- a/solution.py
+++ b/solution.py
@@ -127,8 +127,7 @@
     owner = owner[:ROUNDS]
 
     fields = jnp.stack([eta, phi])
-    mine = (owner == row).astype(jnp.float32)
-    own_block = jnp.sum(mine[:, None, None] * sources[0], axis=0).reshape(-1)
+    own_block = sources[0].reshape(-1)
     top = jnp.concatenate([fields[:, :2].reshape(-1), target_geom[:, 0].reshape(-1)])
     bottom = jnp.concatenate([fields[:, -2:].reshape(-1), target_geom[:, -1].reshape(-1)])
     to_above = (jnp.arange(n_tile, dtype=jnp.int32) == row - 1)[:, None]
@@ -138,7 +137,8 @@
     ], axis=1)
     got = lax.all_to_all(payload, "tile", 0, 0, tiled=True)
     n_own = own_block.shape[0]
-    stacked = got[:, :n_own][owner]
+    src_rows = got[:, :n_own].reshape(n_tile, ROUNDS, n_own // ROUNDS)
+    stacked = src_rows[owner, jnp.arange(ROUNDS)]
     rim = 2 * cols_here * 2
     above = from_peer(got[:, n_own:], row, -1, n_tile)
     below = from_peer(got[:, n_own:], row, 1, n_tile)

time: 66.7 us -> 66.6 us (level)
  other arithmetic: 7.34 us -> 5.9 us
  local copies, waits for them, and re-layouts: 7.46 us -> 8.33 us
    reduce_sum x1 -> x0, other arithmetic: 0.78 us -> none  [body(): own_block = jnp.sum(mine[:, None, None] * sources[0], axis=0).reshape(-1)]
    broadcast_in_dim x1, local copies, waits for them, and re-layouts: 0.09 us -> 0.78 us  [body(): jnp.broadcast_to(own_block[None], (n_tile, own_block.shape[0]))]
where the time goes in v17:
time: 66.6 us; the launch traced here: 66 us
  starting transfers between devices  22.8 us (34%)
  Pallas kernels  15.3 us (23%)
  waiting for transfers between devices  12.6 us (19%)
  local copies, waits for them, and re-layouts  8.33 us (13%)
  other arithmetic  5.9 us (9%)
  between operations  1.01 us (2%)
    pallas_call x1, Pallas kernels, velocity(): pl.pallas_call(velocity_kernel, out_shape=(jax.ShapeDtypeStruct(main.shap...  15.3 us
    all_to_all x1, starting transfers between devices, body(): got = lax.all_to_all(payload, 'tile', 0, 0, tiled=True)  13.5 us
    all_to_all x1, starting transfers between devices, body(): got = lax.all_to_all(payload, 'eval', 0, 0, tiled=True)  9.3 us
    all_to_all x1, waiting for transfers between devices, body(): got = lax.all_to_all(payload, 'eval', 0, 0, tiled=True)  8.21 us
    all_to_all x1, waiting for transfers between devices, body(): got = lax.all_to_all(payload, 'tile', 0, 0, tiled=True)  4.35 us
  transfers between devices with their start and end apart: 2, of which 2 were waited for; matrix products, arithmetic and copies ran while one was open for 7% of the time, Pallas kernels for 0%

profile of v17, /device:TPU:1, one launch (start us, length us, event | category | flops | bytes accessed | tf_op | source)
XLA Modules:
  0.0 66.0 jit_solution(5565688100110547127)
XLA Ops:
  0.6 0.8 %fusion.18 = (f32[6,1,128]{2,1,0:T(1,128)S(1)}, f32[6,1,128]{2,1,0:T(1,128)S(1)}) fusion(f32[6,8,128]{2,1,0:T(8,128)} %main_ref.1), kind=kLoop, calls=%fused_computation.93 | loop fusion | bytes 12288 | tf_op jit(solution)/shard_map/slice | solution.py:131
  1.5 0.8 %reshape.300 = f32[512]{0:T(512)S(1)} reshape(f32[1,4,4,32]{3,2,1,0:T(4,128)} %param.9) | data formatting | bytes 4096 | tf_op jit(solution)/shard_map/broadcast_in_dim | solution.py:135
  2.3 0.8 %pad_maximum_fusion.16 = (f32[2,2,128]{2,1,0:T(2,128)S(1)}, f32[2,2,128]{2,1,0:T(2,128)S(1)}) fusion(f32[1,8,128]{2,1,0:T(8,128)} %bitcast.60, f32[1,8,128]{2,1,0:T(8,128)} %bitcast.64), kind=kLoop, calls=%fused_computation.65 | loop fusion | flops 1024 | bytes 12288 | tf_op jit(solution)/shard_map/slice | solution.py:131
  3.1 0.1 broadcast_select_fusion
  3.2 0.7 %all_to_all.16 = f32[16,1,1792]{2,1,0:T(1,128)} reshape(f32[16,1792]{1,0:T(8,128)S(1)} %pad_maximum_fusion) | data formatting | bytes 229376 | tf_op jit(solution)/shard_map/all_to_all | solution.py:138
  3.9 13.5 %all-to-all-start = ((f32[16,1,1792]{2,1,0:T(1,128)}), f32[16,1,1792]{2,1,0:T(1,128)S(1)}, u32[]{:S(2)}, u32[]{:S(2)}) async-start(f32[16,1,1792]{2,1,0:T(1,128)} %all_to_all.16), calls=%async_computation | async-start | bytes 229376 | tf_op jit(solution)/shard_map/all_to_all | solution.py:138
  17.5 0.1 slice_reduce_fusion.1
  17.6 0.1 copy.28
  17.7 0.1 reshape.275
  17.8 0.1 broadcast_in_dim.96
  17.9 0.2 reduce-window.4
  18.1 0.1 reduce
  18.2 0.5 slice.220
  18.7 0.1 reshape_squeeze.14
  18.8 0.1 reshape_squeeze.15
  18.9 1.2 %convert_reduce_fusion = (s32[4096]{0:T(1024)S(1)}, s32[4096]{0:T(1024)S(1)}) fusion(s32[128]{0:T(128)S(1)} %reduce, s32[128]{0:T(128)S(1)} %broadcast_in_dim.96), kind=kLoop, calls=%fused_computation.2 | loop fusion | flops 2613248 | bytes 33792 | tf_op jit(solution)/shard_map/reduce_sum | solution.py:77
  20.1 0.7 add_select_fusion
  20.8 1.3 %pad_add_fusion.idx_ref = s32[4097]{0:T(1024)} fusion(s32[1]{0:T(128)} %bitcast.2, s32[4096]{0:T(1024)S(1)} %add_select_fusion), kind=kLoop, calls=%fused_computation.27 | loop fusion | flops 4097 | bytes 32776 | tf_op jit(solution)/shard_map/concatenate | solution.py:81
  22.1 4.4 %all-to-all-done = f32[16,1,1792]{2,1,0:T(1,128)S(1)} async-done(((f32[16,1,1792]{2,1,0:T(1,128)}), f32[16,1,1792]{2,1,0:T(1,128)S(1)}, u32[]{:S(2)}, u32[]{:S(2)}) %all-to-all-start) | async-done | bytes 114720 | tf_op jit(solution)/shard_map/all_to_all | solution.py:138
  26.6 0.6 copy-done.1
  27.2 0.1 fusion.19
  27.3 0.1 reshape.261
  27.3 0.1 reshape.262
  27.5 0.6 gather_fusion
  28.1 0.1 pad_maximum_fusion.21
  28.1 0.1 pad_maximum_fusion.22
  28.3 0.7 %all_to_all.19 = f32[32,1,608]{2,1,0:T(1,128)} reshape(f32[32,608]{1,0:T(8,128)S(1)} %pad_maximum_fusion.1) | data formatting | bytes 155648 | tf_op jit(solution)/shard_map/all_to_all | solution.py:159
  29.0 9.3 %all-to-all-start.1 = ((f32[32,1,608]{2,1,0:T(1,128)}), f32[32,1,608]{2,1,0:T(1,128)S(1)}, u32[]{:S(2)}, u32[]{:S(2)}) async-start(f32[32,1,608]{2,1,0:T(1,128)} %all_to_all.19), calls=%async_computation.1 | async-start | bytes 163840 | tf_op jit(solution)/shard_map/all_to_all | solution.py:159
  38.3 8.2 %all-to-all-done.1 = f32[32,1,608]{2,1,0:T(1,128)S(1)} async-done(((f32[32,1,608]{2,1,0:T(1,128)}), f32[32,1,608]{2,1,0:T(1,128)S(1)}, u32[]{:S(2)}, u32[]{:S(2)}) %all-to-all-start.1) | async-done | bytes 77856 | tf_op jit(solution)/shard_map/all_to_all | solution.py:159
  46.5 0.1 slice_reduce_fusion.4
  46.6 0.1 slice.199
  46.7 0.1 slice.201
  46.8 0.1 pad_maximum_fusion.10
  46.9 0.1 fusion.1
  47.0 0.1 slice.193
  47.1 0.1 slice.195
  47.2 0.1 select_maximum_fusion
  47.3 0.6 concatenate.87.src_ref
  47.9 0.6 concatenate.89.halo_ref
  48.6 15.3 %shard_map.85 = (f32[8,128]{1,0:T(8,128)}, f32[1,128]{1,0:T(1,128)}, f32[1,128]{1,0:T(1,128)}, f32[1,128]{1,0:T(1,128)}) custom-call(s32[4097]{0:T(1024)} %pad_add_fusion.idx_ref, f32[16512]{0:T(1024)} %concatenate.87.src_ref, f32[6,8,128]{2,1,0:T(8,128)} %main_ref.1, f32[6,8,128]{2,1,0:T(8,128)} %concatenate.89.halo_ref), custom_call_target="tpu_custom_call" | custom-call | tf_op jit(solution)/shard_map/pallas_call | solution.py:86
  63.9 0.8 %slice_bitcast_fusion.4 = (f32[8,1]{0,1:T(1,128)S(1)}, f32[8,1]{0,1:T(1,128)S(1)}) fusion(f32[1,128]{1,0:T(1,128)} %get-tuple-element.7), kind=kLoop, calls=%fused_computation.87 | loop fusion | bytes 128 | tf_op jit(solution)/shard_map/broadcast_in_dim;squeeze | solution.py:176
  64.7 0.1 fusion.11
  64.8 0.1 copy.33
  64.9 0.1 copy.34
  65.0 0.1 fusion.2
  65.2 0.1 add_subtract_fusion
  65.3 0.1 fusion.6
  65.3 0.6 fusion.8
  (49 shorter events, 0.5 us)
Async XLA Ops:
  3.9 13.6 %copy-start = (f32[6,8,128]{2,1,0:T(8,128)S(1)}, f32[6,8,128]{2,1,0:T(8,128)}, u32[]{:S(2)}) copy-start(f32[6,8,128]{2,1,0:T(8,128)} %main_ref.1) | copy-start | bytes 73732
  3.9 13.8 %copy-start.4 = (s32[4,32]{1,0:T(4,128)S(1)}, s32[4,32]{1,0:T(4,128)}, u32[]{:S(2)}) copy-start(s32[4,32]{1,0:T(4,128)} %param.10) | copy-start | bytes 1540
  3.9 22.6 %all-to-all-start = ((f32[16,1,1792]{2,1,0:T(1,128)}), f32[16,1,1792]{2,1,0:T(1,128)S(1)}, u32[]{:S(2)}, u32[]{:S(2)}) async-start(f32[16,1,1792]{2,1,0:T(1,128)} %all_to_all.16), calls=%async_computation | async-start | bytes 229376 | tf_op jit(solution)/shard_map/all_to_all | solution.py:138
  18.1 4.0 %copy-start.7 = (s32[16]{0:T(128)S(1)}, s32[16]{0:T(128)}, u32[]{:S(2)}) copy-start(s32[16]{0:T(128)} %param.11) | copy-start | bytes 196
  26.5 0.7 %copy-start.1 = (f32[8,128]{1,0:T(8,128)S(1)}, f32[8,128]{1,0:T(8,128)}, u32[]{:S(2)}) copy-start(f32[8,128]{1,0:T(8,128)} %param.8) | copy-start | bytes 12292
  26.5 0.7 %copy-start.2 = (f32[8,128]{1,0:T(8,128)S(1)}, f32[8,128]{1,0:T(8,128)}, u32[]{:S(2)}) copy-start(f32[8,128]{1,0:T(8,128)} %param.7) | copy-start | bytes 12292
  29.0 17.5 %all-to-all-start.1 = ((f32[32,1,608]{2,1,0:T(1,128)}), f32[32,1,608]{2,1,0:T(1,128)S(1)}, u32[]{:S(2)}, u32[]{:S(2)}) async-start(f32[32,1,608]{2,1,0:T(1,128)} %all_to_all.19), calls=%async_computation.1 | async-start | bytes 163840 | tf_op jit(solution)/shard_map/all_to_all | solution.py:159
  63.9 1.2 %copy-start.3 = (f32[8,128]{1,0:T(8,128)S(1)}, f32[8,128]{1,0:T(8,128)}, u32[]{:S(2)}) copy-start(f32[8,128]{1,0:T(8,128)} %get-tuple-element.6) | copy-start | bytes 12292
  63.9 1.2 %copy-start.5 = (f32[1,128]{1,0:T(1,128)S(1)}, f32[1,128]{1,0:T(1,128)}, u32[]{:S(2)}) copy-start(f32[1,128]{1,0:T(1,128)} %get-tuple-element.8) | copy-start | bytes 1540
  63.9 1.2 %copy-start.6 = (f32[1,128]{1,0:T(1,128)S(1)}, f32[1,128]{1,0:T(1,128)}, u32[]{:S(2)}) copy-start(f32[1,128]{1,0:T(1,128)} %get-tuple-element.10) | copy-start | bytes 1540

commit v18 on v15

--- a/solution.py
+++ b/solution.py
@@ -9,7 +9,7 @@
 
 ROUNDS = 4
 SC = 32
-BLOCK = 64
+BLOCK = 128
 
 EPS2 = 0.05
 

time: 66.7 us -> 66.4 us (level)
  no operation moved by 1% of the time
where the time goes in v18:
time: 66.4 us; the launch traced here: 65.7 us
  starting transfers between devices  22.8 us (34%)
  Pallas kernels  15 us (23%)
  waiting for transfers between devices  12.1 us (18%)
  local copies, waits for them, and re-layouts  7.46 us (11%)
  other arithmetic  7.34 us (11%)
  between operations  1 us (2%)
    pallas_call x1, Pallas kernels, velocity(): pl.pallas_call(velocity_kernel, out_shape=(jax.ShapeDtypeStruct(main.shap...  15 us
    all_to_all x1, starting transfers between devices, body(): got = lax.all_to_all(payload, 'tile', 0, 0, tiled=True)  13.5 us
    all_to_all x1, starting transfers between devices, body(): got = lax.all_to_all(payload, 'eval', 0, 0, tiled=True)  9.28 us
    all_to_all x1, waiting for transfers between devices, body(): got = lax.all_to_all(payload, 'eval', 0, 0, tiled=True)  8.21 us
    all_to_all x1, waiting for transfers between devices, body(): got = lax.all_to_all(payload, 'tile', 0, 0, tiled=True)  3.86 us
  transfers between devices with their start and end apart: 2, of which 2 were waited for; matrix products, arithmetic and copies ran while one was open for 7% of the time, Pallas kernels for 0%

profile of v18, /device:TPU:1, one launch (start us, length us, event | category | flops | bytes accessed | tf_op | source)
XLA Modules:
  0.0 65.7 jit_solution(14150499944033640799)
XLA Ops:
  0.6 0.7 %compare_convert_fusion = f32[4]{0:T(128)S(1)} fusion(s32[16]{0:T(128)} %param.11, s32[]{:T(128)S(6)} %axis_index.23), kind=kLoop, calls=%fused_computation.71 | loop fusion | flops 8 | bytes 36 | tf_op jit(solution)/shard_map/convert_element_type | solution.py:130
  1.3 0.8 %fusion.7 = f32[4,32]{1,0:T(4,128)S(1)} fusion(f32[1,4,4,32]{3,2,1,0:T(4,128)} %param.9, f32[4]{0:T(128)S(1)} %compare_convert_fusion), kind=kLoop, calls=%fused_computation.51 | loop fusion | flops 896 | bytes 2576 | tf_op jit(solution)/shard_map/reduce_sum | solution.py:131
  2.1 0.1 reshape.295
  2.2 0.8 %fusion.14 = (f32[6,1,128]{2,1,0:T(1,128)S(1)}, f32[6,1,128]{2,1,0:T(1,128)S(1)}) fusion(f32[6,8,128]{2,1,0:T(8,128)} %main_ref.1), kind=kLoop, calls=%fused_computation.92 | loop fusion | bytes 12288 | tf_op jit(solution)/shard_map/slice | solution.py:132
  3.0 0.8 %pad_maximum_fusion.16 = (f32[2,2,128]{2,1,0:T(2,128)S(1)}, f32[2,2,128]{2,1,0:T(2,128)S(1)}) fusion(f32[1,8,128]{2,1,0:T(8,128)} %bitcast.56, f32[1,8,128]{2,1,0:T(8,128)} %bitcast.60), kind=kLoop, calls=%fused_computation.68 | loop fusion | flops 1024 | bytes 12288 | tf_op jit(solution)/shard_map/slice | solution.py:132
  3.8 0.1 broadcast_select_fusion
  3.9 0.7 %all_to_all.16 = f32[16,1,1408]{2,1,0:T(1,128)} reshape(f32[16,1408]{1,0:T(8,128)S(1)} %pad_maximum_fusion) | data formatting | bytes 180224 | tf_op jit(solution)/shard_map/all_to_all | solution.py:139
  4.6 13.5 %all-to-all-start = ((f32[16,1,1408]{2,1,0:T(1,128)}), f32[16,1,1408]{2,1,0:T(1,128)S(1)}, u32[]{:S(2)}, u32[]{:S(2)}) async-start(f32[16,1,1408]{2,1,0:T(1,128)} %all_to_all.16), calls=%async_computation | async-start | bytes 180224 | tf_op jit(solution)/shard_map/all_to_all | solution.py:139
  18.2 0.1 slice_reduce_fusion.1
  18.4 0.5 copy-done.4
  18.8 0.1 copy.28
  18.9 0.1 broadcast_in_dim.96
  19.1 0.2 reduce-window.4
  19.3 0.5 slice.220
  19.8 0.1 reduce
  20.0 0.1 reshape_squeeze.14
  20.0 0.1 reshape_squeeze.15
  20.1 1.2 %convert_reduce_fusion = (s32[4096]{0:T(1024)S(1)}, s32[4096]{0:T(1024)S(1)}) fusion(s32[128]{0:T(128)S(1)} %reduce, s32[128]{0:T(128)S(1)} %broadcast_in_dim.96), kind=kLoop, calls=%fused_computation.2 | loop fusion | flops 2613248 | bytes 33792 | tf_op jit(solution)/shard_map/reduce_sum | solution.py:77
  21.3 0.7 add_select_fusion
  21.9 1.3 %pad_add_fusion.idx_ref = s32[4097]{0:T(1024)} fusion(s32[1]{0:T(128)} %bitcast.2, s32[4096]{0:T(1024)S(1)} %add_select_fusion), kind=kLoop, calls=%fused_computation.27 | loop fusion | flops 4097 | bytes 32776 | tf_op jit(solution)/shard_map/concatenate | solution.py:81
  23.3 3.9 %all-to-all-done = f32[16,1,1408]{2,1,0:T(1,128)S(1)} async-done(((f32[16,1,1408]{2,1,0:T(1,128)}), f32[16,1,1408]{2,1,0:T(1,128)S(1)}, u32[]{:S(2)}, u32[]{:S(2)}) %all-to-all-start) | async-done | bytes 90144 | tf_op jit(solution)/shard_map/all_to_all | solution.py:139
  27.2 0.6 gather_fusion
  27.9 0.1 fusion.15
  27.9 0.1 reshape.258
  28.0 0.1 reshape.259
  28.1 0.1 pad_maximum_fusion.21
  28.2 0.1 pad_maximum_fusion.22
  28.4 0.7 %all_to_all.19 = f32[32,1,608]{2,1,0:T(1,128)} reshape(f32[32,608]{1,0:T(8,128)S(1)} %pad_maximum_fusion.1) | data formatting | bytes 155648 | tf_op jit(solution)/shard_map/all_to_all | solution.py:159
  29.1 9.3 %all-to-all-start.1 = ((f32[32,1,608]{2,1,0:T(1,128)}), f32[32,1,608]{2,1,0:T(1,128)S(1)}, u32[]{:S(2)}, u32[]{:S(2)}) async-start(f32[32,1,608]{2,1,0:T(1,128)} %all_to_all.19), calls=%async_computation.1 | async-start | bytes 163840 | tf_op jit(solution)/shard_map/all_to_all | solution.py:159
  38.4 8.2 %all-to-all-done.1 = f32[32,1,608]{2,1,0:T(1,128)S(1)} async-done(((f32[32,1,608]{2,1,0:T(1,128)}), f32[32,1,608]{2,1,0:T(1,128)S(1)}, u32[]{:S(2)}, u32[]{:S(2)}) %all-to-all-start.1) | async-done | bytes 77856 | tf_op jit(solution)/shard_map/all_to_all | solution.py:159
  46.6 0.1 slice_reduce_fusion.4
  46.7 0.1 slice.201
  46.8 0.1 slice.199
  46.9 0.1 pad_maximum_fusion.10
  47.0 0.1 fusion.1
  47.1 0.1 slice.195
  47.2 0.1 slice.193
  47.3 0.1 select_maximum_fusion
  47.4 0.6 concatenate.83.src_ref
  48.0 0.6 concatenate.85.halo_ref
  48.6 15.0 %shard_map.85 = (f32[8,128]{1,0:T(8,128)}, f32[1,128]{1,0:T(1,128)}, f32[1,128]{1,0:T(1,128)}, f32[1,128]{1,0:T(1,128)}) custom-call(s32[4097]{0:T(1024)} %pad_add_fusion.idx_ref, f32[16512]{0:T(1024)} %concatenate.83.src_ref, f32[6,8,128]{2,1,0:T(8,128)} %main_ref.1, f32[6,8,128]{2,1,0:T(8,128)} %concatenate.85.halo_ref), custom_call_target="tpu_custom_call" | custom-call | tf_op jit(solution)/shard_map/pallas_call | solution.py:86
  63.7 0.8 %slice_bitcast_fusion.4 = (f32[8,1]{0,1:T(1,128)S(1)}, f32[8,1]{0,1:T(1,128)S(1)}) fusion(f32[1,128]{1,0:T(1,128)} %get-tuple-element.7), kind=kLoop, calls=%fused_computation.87 | loop fusion | bytes 128 | tf_op jit(solution)/shard_map/broadcast_in_dim;squeeze | solution.py:176
  64.6 0.1 copy.34
  64.7 0.1 copy.33
  64.8 0.1 fusion.2
  65.0 0.1 add_subtract_fusion
  65.0 0.1 fusion.6
  65.1 0.6 fusion.9
  (51 shorter events, 0.7 us)
Async XLA Ops:
  4.6 13.6 %copy-start.7 = (s32[16]{0:T(128)S(1)}, s32[16]{0:T(128)}, u32[]{:S(2)}) copy-start(s32[16]{0:T(128)} %param.11) | copy-start | bytes 196
  4.6 13.6 %copy-start = (f32[6,8,128]{2,1,0:T(8,128)S(1)}, f32[6,8,128]{2,1,0:T(8,128)}, u32[]{:S(2)}) copy-start(f32[6,8,128]{2,1,0:T(8,128)} %main_ref.1) | copy-start | bytes 73732
  4.6 22.6 %all-to-all-start = ((f32[16,1,1408]{2,1,0:T(1,128)}), f32[16,1,1408]{2,1,0:T(1,128)S(1)}, u32[]{:S(2)}, u32[]{:S(2)}) async-start(f32[16,1,1408]{2,1,0:T(1,128)} %all_to_all.16), calls=%async_computation | async-start | bytes 180224 | tf_op jit(solution)/shard_map/all_to_all | solution.py:139
  18.1 0.7 %copy-start.4 = (s32[4,32]{1,0:T(4,128)S(1)}, s32[4,32]{1,0:T(4,128)}, u32[]{:S(2)}) copy-start(s32[4,32]{1,0:T(4,128)} %param.10) | copy-start | bytes 1540
  27.1 0.7 %copy-start.1 = (f32[8,128]{1,0:T(8,128)S(1)}, f32[8,128]{1,0:T(8,128)}, u32[]{:S(2)}) copy-start(f32[8,128]{1,0:T(8,128)} %param.8) | copy-start | bytes 12292
  27.2 0.7 %copy-start.2 = (f32[8,128]{1,0:T(8,128)S(1)}, f32[8,128]{1,0:T(8,128)}, u32[]{:S(2)}) copy-start(f32[8,128]{1,0:T(8,128)} %param.7) | copy-start | bytes 12292
  29.1 17.5 %all-to-all-start.1 = ((f32[32,1,608]{2,1,0:T(1,128)}), f32[32,1,608]{2,1,0:T(1,128)S(1)}, u32[]{:S(2)}, u32[]{:S(2)}) async-start(f32[32,1,608]{2,1,0:T(1,128)} %all_to_all.19), calls=%async_computation.1 | async-start | bytes 163840 | tf_op jit(solution)/shard_map/all_to_all | solution.py:159
  63.7 1.2 %copy-start.3 = (f32[8,128]{1,0:T(8,128)S(1)}, f32[8,128]{1,0:T(8,128)}, u32[]{:S(2)}) copy-start(f32[8,128]{1,0:T(8,128)} %get-tuple-element.6) | copy-start | bytes 12292
  63.7 1.2 %copy-start.5 = (f32[1,128]{1,0:T(1,128)S(1)}, f32[1,128]{1,0:T(1,128)}, u32[]{:S(2)}) copy-start(f32[1,128]{1,0:T(1,128)} %get-tuple-element.8) | copy-start | bytes 1540
  63.7 1.2 %copy-start.6 = (f32[1,128]{1,0:T(1,128)S(1)}, f32[1,128]{1,0:T(1,128)}, u32[]{:S(2)}) copy-start(f32[1,128]{1,0:T(1,128)} %get-tuple-element.10) | copy-start | bytes 1540

commit v19 on v17

--- a/solution.py
+++ b/solution.py
@@ -9,7 +9,7 @@
 
 ROUNDS = 4
 SC = 32
-BLOCK = 64
+BLOCK = 128
 
 EPS2 = 0.05
 

time: 66.6 us -> 66.3 us (level)
  no operation moved by 1% of the time
where the time goes in v19:
time: 66.3 us; the launch traced here: 65.7 us
  starting transfers between devices  22.8 us (34%)
  Pallas kernels  15 us (23%)
  waiting for transfers between devices  12.6 us (19%)
  local copies, waits for them, and re-layouts  8.33 us (13%)
  other arithmetic  5.9 us (9%)
  between operations  1.01 us (2%)
    pallas_call x1, Pallas kernels, velocity(): pl.pallas_call(velocity_kernel, out_shape=(jax.ShapeDtypeStruct(main.shap...  15 us
    all_to_all x1, starting transfers between devices, body(): got = lax.all_to_all(payload, 'tile', 0, 0, tiled=True)  13.5 us
    all_to_all x1, starting transfers between devices, body(): got = lax.all_to_all(payload, 'eval', 0, 0, tiled=True)  9.3 us
    all_to_all x1, waiting for transfers between devices, body(): got = lax.all_to_all(payload, 'eval', 0, 0, tiled=True)  8.21 us
    all_to_all x1, waiting for transfers between devices, body(): got = lax.all_to_all(payload, 'tile', 0, 0, tiled=True)  4.35 us
  transfers between devices with their start and end apart: 2, of which 2 were waited for; matrix products, arithmetic and copies ran while one was open for 7% of the time, Pallas kernels for 0%

profile of v19, /device:TPU:1, one launch (start us, length us, event | category | flops | bytes accessed | tf_op | source)
XLA Modules:
  0.0 65.7 jit_solution(15291654585685849427)
XLA Ops:
  0.6 0.8 %fusion.18 = (f32[6,1,128]{2,1,0:T(1,128)S(1)}, f32[6,1,128]{2,1,0:T(1,128)S(1)}) fusion(f32[6,8,128]{2,1,0:T(8,128)} %main_ref.1), kind=kLoop, calls=%fused_computation.93 | loop fusion | bytes 12288 | tf_op jit(solution)/shard_map/slice | solution.py:131
  1.5 0.8 %reshape.300 = f32[512]{0:T(512)S(1)} reshape(f32[1,4,4,32]{3,2,1,0:T(4,128)} %param.9) | data formatting | bytes 4096 | tf_op jit(solution)/shard_map/broadcast_in_dim | solution.py:135
  2.3 0.8 %pad_maximum_fusion.16 = (f32[2,2,128]{2,1,0:T(2,128)S(1)}, f32[2,2,128]{2,1,0:T(2,128)S(1)}) fusion(f32[1,8,128]{2,1,0:T(8,128)} %bitcast.60, f32[1,8,128]{2,1,0:T(8,128)} %bitcast.64), kind=kLoop, calls=%fused_computation.65 | loop fusion | flops 1024 | bytes 12288 | tf_op jit(solution)/shard_map/slice | solution.py:131
  3.1 0.1 broadcast_select_fusion
  3.2 0.7 %all_to_all.16 = f32[16,1,1792]{2,1,0:T(1,128)} reshape(f32[16,1792]{1,0:T(8,128)S(1)} %pad_maximum_fusion) | data formatting | bytes 229376 | tf_op jit(solution)/shard_map/all_to_all | solution.py:138
  3.9 13.5 %all-to-all-start = ((f32[16,1,1792]{2,1,0:T(1,128)}), f32[16,1,1792]{2,1,0:T(1,128)S(1)}, u32[]{:S(2)}, u32[]{:S(2)}) async-start(f32[16,1,1792]{2,1,0:T(1,128)} %all_to_all.16), calls=%async_computation | async-start | bytes 229376 | tf_op jit(solution)/shard_map/all_to_all | solution.py:138
  17.5 0.1 slice_reduce_fusion.1
  17.6 0.1 copy.28
  17.7 0.1 reshape.275
  17.8 0.1 broadcast_in_dim.96
  17.9 0.2 reduce-window.4
  18.1 0.1 reduce
  18.2 0.5 slice.220
  18.7 0.1 reshape_squeeze.14
  18.8 0.1 reshape_squeeze.15
  18.9 1.2 %convert_reduce_fusion = (s32[4096]{0:T(1024)S(1)}, s32[4096]{0:T(1024)S(1)}) fusion(s32[128]{0:T(128)S(1)} %reduce, s32[128]{0:T(128)S(1)} %broadcast_in_dim.96), kind=kLoop, calls=%fused_computation.2 | loop fusion | flops 2613248 | bytes 33792 | tf_op jit(solution)/shard_map/reduce_sum | solution.py:77
  20.1 0.7 add_select_fusion
  20.8 1.3 %pad_add_fusion.idx_ref = s32[4097]{0:T(1024)} fusion(s32[1]{0:T(128)} %bitcast.2, s32[4096]{0:T(1024)S(1)} %add_select_fusion), kind=kLoop, calls=%fused_computation.27 | loop fusion | flops 4097 | bytes 32776 | tf_op jit(solution)/shard_map/concatenate | solution.py:81
  22.1 4.4 %all-to-all-done = f32[16,1,1792]{2,1,0:T(1,128)S(1)} async-done(((f32[16,1,1792]{2,1,0:T(1,128)}), f32[16,1,1792]{2,1,0:T(1,128)S(1)}, u32[]{:S(2)}, u32[]{:S(2)}) %all-to-all-start) | async-done | bytes 114720 | tf_op jit(solution)/shard_map/all_to_all | solution.py:138
  26.6 0.6 copy-done.1
  27.2 0.1 fusion.19
  27.3 0.1 reshape.261
  27.3 0.1 reshape.262
  27.5 0.6 gather_fusion
  28.1 0.1 pad_maximum_fusion.21
  28.1 0.1 pad_maximum_fusion.22
  28.3 0.7 %all_to_all.19 = f32[32,1,608]{2,1,0:T(1,128)} reshape(f32[32,608]{1,0:T(8,128)S(1)} %pad_maximum_fusion.1) | data formatting | bytes 155648 | tf_op jit(solution)/shard_map/all_to_all | solution.py:159
  29.0 9.3 %all-to-all-start.1 = ((f32[32,1,608]{2,1,0:T(1,128)}), f32[32,1,608]{2,1,0:T(1,128)S(1)}, u32[]{:S(2)}, u32[]{:S(2)}) async-start(f32[32,1,608]{2,1,0:T(1,128)} %all_to_all.19), calls=%async_computation.1 | async-start | bytes 163840 | tf_op jit(solution)/shard_map/all_to_all | solution.py:159
  38.3 8.2 %all-to-all-done.1 = f32[32,1,608]{2,1,0:T(1,128)S(1)} async-done(((f32[32,1,608]{2,1,0:T(1,128)}), f32[32,1,608]{2,1,0:T(1,128)S(1)}, u32[]{:S(2)}, u32[]{:S(2)}) %all-to-all-start.1) | async-done | bytes 77856 | tf_op jit(solution)/shard_map/all_to_all | solution.py:159
  46.5 0.1 slice_reduce_fusion.4
  46.6 0.1 slice.199
  46.7 0.1 slice.201
  46.8 0.1 pad_maximum_fusion.10
  46.9 0.1 fusion.1
  47.0 0.1 slice.193
  47.1 0.1 slice.195
  47.2 0.1 select_maximum_fusion
  47.3 0.6 concatenate.87.src_ref
  47.9 0.6 concatenate.89.halo_ref
  48.6 15.0 %shard_map.85 = (f32[8,128]{1,0:T(8,128)}, f32[1,128]{1,0:T(1,128)}, f32[1,128]{1,0:T(1,128)}, f32[1,128]{1,0:T(1,128)}) custom-call(s32[4097]{0:T(1024)} %pad_add_fusion.idx_ref, f32[16512]{0:T(1024)} %concatenate.87.src_ref, f32[6,8,128]{2,1,0:T(8,128)} %main_ref.1, f32[6,8,128]{2,1,0:T(8,128)} %concatenate.89.halo_ref), custom_call_target="tpu_custom_call" | custom-call | tf_op jit(solution)/shard_map/pallas_call | solution.py:86
  63.6 0.8 %slice_bitcast_fusion.4 = (f32[8,1]{0,1:T(1,128)S(1)}, f32[8,1]{0,1:T(1,128)S(1)}) fusion(f32[1,128]{1,0:T(1,128)} %get-tuple-element.7), kind=kLoop, calls=%fused_computation.87 | loop fusion | bytes 128 | tf_op jit(solution)/shard_map/broadcast_in_dim;squeeze | solution.py:176
  64.4 0.1 fusion.11
  64.5 0.1 copy.33
  64.6 0.1 copy.34
  64.7 0.1 fusion.2
  64.9 0.1 add_subtract_fusion
  65.0 0.1 fusion.6
  65.1 0.6 fusion.8
  (49 shorter events, 0.5 us)
Async XLA Ops:
  3.9 13.6 %copy-start = (f32[6,8,128]{2,1,0:T(8,128)S(1)}, f32[6,8,128]{2,1,0:T(8,128)}, u32[]{:S(2)}) copy-start(f32[6,8,128]{2,1,0:T(8,128)} %main_ref.1) | copy-start | bytes 73732
  3.9 13.8 %copy-start.4 = (s32[4,32]{1,0:T(4,128)S(1)}, s32[4,32]{1,0:T(4,128)}, u32[]{:S(2)}) copy-start(s32[4,32]{1,0:T(4,128)} %param.10) | copy-start | bytes 1540
  3.9 22.6 %all-to-all-start = ((f32[16,1,1792]{2,1,0:T(1,128)}), f32[16,1,1792]{2,1,0:T(1,128)S(1)}, u32[]{:S(2)}, u32[]{:S(2)}) async-start(f32[16,1,1792]{2,1,0:T(1,128)} %all_to_all.16), calls=%async_computation | async-start | bytes 229376 | tf_op jit(solution)/shard_map/all_to_all | solution.py:138
  18.1 4.0 %copy-start.7 = (s32[16]{0:T(128)S(1)}, s32[16]{0:T(128)}, u32[]{:S(2)}) copy-start(s32[16]{0:T(128)} %param.11) | copy-start | bytes 196
  26.5 0.7 %copy-start.1 = (f32[8,128]{1,0:T(8,128)S(1)}, f32[8,128]{1,0:T(8,128)}, u32[]{:S(2)}) copy-start(f32[8,128]{1,0:T(8,128)} %param.8) | copy-start | bytes 12292
  26.5 0.7 %copy-start.2 = (f32[8,128]{1,0:T(8,128)S(1)}, f32[8,128]{1,0:T(8,128)}, u32[]{:S(2)}) copy-start(f32[8,128]{1,0:T(8,128)} %param.7) | copy-start | bytes 12292
  29.0 17.5 %all-to-all-start.1 = ((f32[32,1,608]{2,1,0:T(1,128)}), f32[32,1,608]{2,1,0:T(1,128)S(1)}, u32[]{:S(2)}, u32[]{:S(2)}) async-start(f32[32,1,608]{2,1,0:T(1,128)} %all_to_all.19), calls=%async_computation.1 | async-start | bytes 163840 | tf_op jit(solution)/shard_map/all_to_all | solution.py:159
  63.6 1.2 %copy-start.3 = (f32[8,128]{1,0:T(8,128)S(1)}, f32[8,128]{1,0:T(8,128)}, u32[]{:S(2)}) copy-start(f32[8,128]{1,0:T(8,128)} %get-tuple-element.6) | copy-start | bytes 12292
  63.6 1.2 %copy-start.5 = (f32[1,128]{1,0:T(1,128)S(1)}, f32[1,128]{1,0:T(1,128)}, u32[]{:S(2)}) copy-start(f32[1,128]{1,0:T(1,128)} %get-tuple-element.8) | copy-start | bytes 1540
  63.6 1.2 %copy-start.6 = (f32[1,128]{1,0:T(1,128)S(1)}, f32[1,128]{1,0:T(1,128)}, u32[]{:S(2)}) copy-start(f32[1,128]{1,0:T(1,128)} %get-tuple-element.10) | copy-start | bytes 1540

commit v20 on v19

--- a/solution.py
+++ b/solution.py
@@ -9,7 +9,7 @@
 
 ROUNDS = 4
 SC = 32
-BLOCK = 128
+BLOCK = 256
 
 EPS2 = 0.05
 

time: 66.3 us -> 66.1 us (level)
  no operation moved by 1% of the time
where the time goes in v20:
time: 66.1 us; the launch traced here: 65.5 us
  starting transfers between devices  22.8 us (34%)
  Pallas kernels  14.9 us (23%)
  waiting for transfers between devices  12.6 us (19%)
  local copies, waits for them, and re-layouts  8.33 us (13%)
  other arithmetic  5.9 us (9%)
  between operations  1.01 us (2%)
    pallas_call x1, Pallas kernels, velocity(): pl.pallas_call(velocity_kernel, out_shape=(jax.ShapeDtypeStruct(main.shap...  14.9 us
    all_to_all x1, starting transfers between devices, body(): got = lax.all_to_all(payload, 'tile', 0, 0, tiled=True)  13.5 us
    all_to_all x1, starting transfers between devices, body(): got = lax.all_to_all(payload, 'eval', 0, 0, tiled=True)  9.3 us
    all_to_all x1, waiting for transfers between devices, body(): got = lax.all_to_all(payload, 'eval', 0, 0, tiled=True)  8.21 us
    all_to_all x1, waiting for transfers between devices, body(): got = lax.all_to_all(payload, 'tile', 0, 0, tiled=True)  4.35 us
  transfers between devices with their start and end apart: 2, of which 2 were waited for; matrix products, arithmetic and copies ran while one was open for 7% of the time, Pallas kernels for 0%

profile of v20, /device:TPU:1, one launch (start us, length us, event | category | flops | bytes accessed | tf_op | source)
XLA Modules:
  0.0 65.5 jit_solution(1529801665147878528)
XLA Ops:
  0.6 0.8 %fusion.18 = (f32[6,1,128]{2,1,0:T(1,128)S(1)}, f32[6,1,128]{2,1,0:T(1,128)S(1)}) fusion(f32[6,8,128]{2,1,0:T(8,128)} %main_ref.1), kind=kLoop, calls=%fused_computation.93 | loop fusion | bytes 12288 | tf_op jit(solution)/shard_map/slice | solution.py:131
  1.5 0.8 %reshape.300 = f32[512]{0:T(512)S(1)} reshape(f32[1,4,4,32]{3,2,1,0:T(4,128)} %param.9) | data formatting | bytes 4096 | tf_op jit(solution)/shard_map/broadcast_in_dim | solution.py:135
  2.3 0.8 %pad_maximum_fusion.16 = (f32[2,2,128]{2,1,0:T(2,128)S(1)}, f32[2,2,128]{2,1,0:T(2,128)S(1)}) fusion(f32[1,8,128]{2,1,0:T(8,128)} %bitcast.60, f32[1,8,128]{2,1,0:T(8,128)} %bitcast.64), kind=kLoop, calls=%fused_computation.65 | loop fusion | flops 1024 | bytes 12288 | tf_op jit(solution)/shard_map/slice | solution.py:131
  3.1 0.1 broadcast_select_fusion
  3.2 0.7 %all_to_all.16 = f32[16,1,1792]{2,1,0:T(1,128)} reshape(f32[16,1792]{1,0:T(8,128)S(1)} %pad_maximum_fusion) | data formatting | bytes 229376 | tf_op jit(solution)/shard_map/all_to_all | solution.py:138
  3.9 13.5 %all-to-all-start = ((f32[16,1,1792]{2,1,0:T(1,128)}), f32[16,1,1792]{2,1,0:T(1,128)S(1)}, u32[]{:S(2)}, u32[]{:S(2)}) async-start(f32[16,1,1792]{2,1,0:T(1,128)} %all_to_all.16), calls=%async_computation | async-start | bytes 229376 | tf_op jit(solution)/shard_map/all_to_all | solution.py:138
  17.5 0.1 slice_reduce_fusion.1
  17.6 0.1 copy.28
  17.7 0.1 reshape.275
  17.8 0.1 broadcast_in_dim.96
  17.9 0.2 reduce-window.4
  18.1 0.1 reduce
  18.2 0.5 slice.220
  18.7 0.1 reshape_squeeze.14
  18.8 0.1 reshape_squeeze.15
  18.9 1.2 %convert_reduce_fusion = (s32[4096]{0:T(1024)S(1)}, s32[4096]{0:T(1024)S(1)}) fusion(s32[128]{0:T(128)S(1)} %reduce, s32[128]{0:T(128)S(1)} %broadcast_in_dim.96), kind=kLoop, calls=%fused_computation.2 | loop fusion | flops 2613248 | bytes 33792 | tf_op jit(solution)/shard_map/reduce_sum | solution.py:77
  20.1 0.7 add_select_fusion
  20.8 1.3 %pad_add_fusion.idx_ref = s32[4097]{0:T(1024)} fusion(s32[1]{0:T(128)} %bitcast.2, s32[4096]{0:T(1024)S(1)} %add_select_fusion), kind=kLoop, calls=%fused_computation.27 | loop fusion | flops 4097 | bytes 32776 | tf_op jit(solution)/shard_map/concatenate | solution.py:81
  22.1 4.4 %all-to-all-done = f32[16,1,1792]{2,1,0:T(1,128)S(1)} async-done(((f32[16,1,1792]{2,1,0:T(1,128)}), f32[16,1,1792]{2,1,0:T(1,128)S(1)}, u32[]{:S(2)}, u32[]{:S(2)}) %all-to-all-start) | async-done | bytes 114720 | tf_op jit(solution)/shard_map/all_to_all | solution.py:138
  26.6 0.6 copy-done.1
  27.2 0.1 fusion.19
  27.3 0.1 reshape.261
  27.3 0.1 reshape.262
  27.5 0.6 gather_fusion
  28.1 0.1 pad_maximum_fusion.21
  28.1 0.1 pad_maximum_fusion.22
  28.3 0.7 %all_to_all.19 = f32[32,1,608]{2,1,0:T(1,128)} reshape(f32[32,608]{1,0:T(8,128)S(1)} %pad_maximum_fusion.1) | data formatting | bytes 155648 | tf_op jit(solution)/shard_map/all_to_all | solution.py:159
  29.0 9.3 %all-to-all-start.1 = ((f32[32,1,608]{2,1,0:T(1,128)}), f32[32,1,608]{2,1,0:T(1,128)S(1)}, u32[]{:S(2)}, u32[]{:S(2)}) async-start(f32[32,1,608]{2,1,0:T(1,128)} %all_to_all.19), calls=%async_computation.1 | async-start | bytes 163840 | tf_op jit(solution)/shard_map/all_to_all | solution.py:159
  38.3 8.2 %all-to-all-done.1 = f32[32,1,608]{2,1,0:T(1,128)S(1)} async-done(((f32[32,1,608]{2,1,0:T(1,128)}), f32[32,1,608]{2,1,0:T(1,128)S(1)}, u32[]{:S(2)}, u32[]{:S(2)}) %all-to-all-start.1) | async-done | bytes 77856 | tf_op jit(solution)/shard_map/all_to_all | solution.py:159
  46.5 0.1 slice_reduce_fusion.4
  46.6 0.1 slice.199
  46.7 0.1 slice.201
  46.8 0.1 pad_maximum_fusion.10
  46.9 0.1 fusion.1
  47.0 0.1 slice.193
  47.1 0.1 slice.195
  47.2 0.1 select_maximum_fusion
  47.3 0.6 concatenate.87.src_ref
  47.9 0.6 concatenate.89.halo_ref
  48.6 14.9 %shard_map.85 = (f32[8,128]{1,0:T(8,128)}, f32[1,128]{1,0:T(1,128)}, f32[1,128]{1,0:T(1,128)}, f32[1,128]{1,0:T(1,128)}) custom-call(s32[4097]{0:T(1024)} %pad_add_fusion.idx_ref, f32[16512]{0:T(1024)} %concatenate.87.src_ref, f32[6,8,128]{2,1,0:T(8,128)} %main_ref.1, f32[6,8,128]{2,1,0:T(8,128)} %concatenate.89.halo_ref), custom_call_target="tpu_custom_call" | custom-call | tf_op jit(solution)/shard_map/pallas_call | solution.py:86
  63.5 0.8 %slice_bitcast_fusion.4 = (f32[8,1]{0,1:T(1,128)S(1)}, f32[8,1]{0,1:T(1,128)S(1)}) fusion(f32[1,128]{1,0:T(1,128)} %get-tuple-element.7), kind=kLoop, calls=%fused_computation.87 | loop fusion | bytes 128 | tf_op jit(solution)/shard_map/broadcast_in_dim;squeeze | solution.py:176
  64.3 0.1 fusion.11
  64.3 0.1 copy.33
  64.5 0.1 copy.34
  64.6 0.1 fusion.2
  64.7 0.1 add_subtract_fusion
  64.8 0.1 fusion.6
  64.9 0.6 fusion.8
  (49 shorter events, 0.5 us)
Async XLA Ops:
  3.9 13.6 %copy-start = (f32[6,8,128]{2,1,0:T(8,128)S(1)}, f32[6,8,128]{2,1,0:T(8,128)}, u32[]{:S(2)}) copy-start(f32[6,8,128]{2,1,0:T(8,128)} %main_ref.1) | copy-start | bytes 73732
  3.9 13.8 %copy-start.4 = (s32[4,32]{1,0:T(4,128)S(1)}, s32[4,32]{1,0:T(4,128)}, u32[]{:S(2)}) copy-start(s32[4,32]{1,0:T(4,128)} %param.10) | copy-start | bytes 1540
  3.9 22.6 %all-to-all-start = ((f32[16,1,1792]{2,1,0:T(1,128)}), f32[16,1,1792]{2,1,0:T(1,128)S(1)}, u32[]{:S(2)}, u32[]{:S(2)}) async-start(f32[16,1,1792]{2,1,0:T(1,128)} %all_to_all.16), calls=%async_computation | async-start | bytes 229376 | tf_op jit(solution)/shard_map/all_to_all | solution.py:138
  18.1 4.0 %copy-start.7 = (s32[16]{0:T(128)S(1)}, s32[16]{0:T(128)}, u32[]{:S(2)}) copy-start(s32[16]{0:T(128)} %param.11) | copy-start | bytes 196
  26.5 0.7 %copy-start.1 = (f32[8,128]{1,0:T(8,128)S(1)}, f32[8,128]{1,0:T(8,128)}, u32[]{:S(2)}) copy-start(f32[8,128]{1,0:T(8,128)} %param.8) | copy-start | bytes 12292
  26.5 0.7 %copy-start.2 = (f32[8,128]{1,0:T(8,128)S(1)}, f32[8,128]{1,0:T(8,128)}, u32[]{:S(2)}) copy-start(f32[8,128]{1,0:T(8,128)} %param.7) | copy-start | bytes 12292
  29.0 17.5 %all-to-all-start.1 = ((f32[32,1,608]{2,1,0:T(1,128)}), f32[32,1,608]{2,1,0:T(1,128)S(1)}, u32[]{:S(2)}, u32[]{:S(2)}) async-start(f32[32,1,608]{2,1,0:T(1,128)} %all_to_all.19), calls=%async_computation.1 | async-start | bytes 163840 | tf_op jit(solution)/shard_map/all_to_all | solution.py:159
  63.5 1.2 %copy-start.3 = (f32[8,128]{1,0:T(8,128)S(1)}, f32[8,128]{1,0:T(8,128)}, u32[]{:S(2)}) copy-start(f32[8,128]{1,0:T(8,128)} %get-tuple-element.6) | copy-start | bytes 12292
  63.5 1.2 %copy-start.5 = (f32[1,128]{1,0:T(1,128)S(1)}, f32[1,128]{1,0:T(1,128)}, u32[]{:S(2)}) copy-start(f32[1,128]{1,0:T(1,128)} %get-tuple-element.8) | copy-start | bytes 1540
  63.5 1.2 %copy-start.6 = (f32[1,128]{1,0:T(1,128)S(1)}, f32[1,128]{1,0:T(1,128)}, u32[]{:S(2)}) copy-start(f32[1,128]{1,0:T(1,128)} %get-tuple-element.10) | copy-start | bytes 1540
